TPU v7x, 32 devices: a whole 2x2x4 slice. The times are simulated.
32 devices in a mesh: region: 2 (over y), mod: 4 (over z), obs: 4 (over x, core).
Axes of the slice: x: 2, y: 2, z: 4, core: 2. Of those that a mesh axis runs over, the one named last changes fastest.
Arguments:
- model_days: float32 [16384, 128], P(('region', 'mod')), parts along dimension 0, may hold values from -48 to 48
- obs_days: float32 [16384, 128], P(('region', 'obs', 'mod')), parts along dimension 0, may hold values from -48 to 48
Outputs:
- mapped: float32 [16384, 128], P(('region', 'mod', 'obs')), parts along dimension 0
- row_potential: float32 [16384], P(('region', 'mod')), parts along dimension 0
- col_potential: float32 [16384], P(('region', 'obs')), parts along dimension 0
There are 2 independent parts, one for each index of `region`. A program takes and returns all parts, laid end to end along the dimension named above; each array names one. Nothing has to cross between parts.
All inputs are finite; a program needn't handle non-finite values.
Results may differ from a plain program's by a relative error of at most 0.0003.
Values sent between devices are 32-bit elements; how exact they have to be, the bound alone decides.
No kernel may reach another device: no remote copies, remote signals or barrier semaphores. Data moves between devices by JAX's collectives and lax.ppermute only.
A program may use at most 64 MiB of HBM per device.

v0:
```python
import math

import jax
import jax.numpy as jnp
from jax import lax
from jax.experimental import pallas as pl
from jax.experimental.pallas import tpu as pltpu
from jax.sharding import PartitionSpec as P

ITERS = 2

RB = 8


def _lane_tiles(s):
    return [s[:, j * 128:(j + 1) * 128] for j in range(s.shape[1] // 128)]


def _final_kernel(*refs):
    h_ref = refs[0]
    nb = len(refs) - 8
    c_refs = refs[1:1 + nb]
    y_ref, m_ref, l_ref, p_ref, w_ref, m_scr, t_scr = refs[1 + nb:]
    tr = c_refs[0].shape[0]
    width = c_refs[0].shape[1]

    def scores(r):
        return [h_ref[:, k * width:(k + 1) * width] + c[pl.ds(r, RB), :] for k, c in enumerate(c_refs)]

    def p1(i, carry):
        r = pl.multiple_of(i * RB, RB)
        tiles = [t for sc in scores(r) for t in _lane_tiles(sc)]
        m = tiles[0]
        for t in tiles[1:]:
            m = jnp.maximum(m, t)
        m_scr[pl.ds(r, RB), :] = m
        return carry
    lax.fori_loop(0, tr // RB, p1, 0, unroll=4)
    m_ref[...] = jnp.max(m_scr[...], axis=1, keepdims=True)

    def p2(i, carry):
        r = pl.multiple_of(i * RB, RB)
        mr = m_ref[pl.ds(r, RB), :]
        t = None
        for k, sc in enumerate(scores(r)):
            w = jnp.exp(sc - mr)
            w_ref[pl.ds(r, RB), k * width:(k + 1) * width] = w
            for u in _lane_tiles(w):
                t = u if t is None else t + u
        t_scr[pl.ds(r, RB), :] = t
        return carry
    lax.fori_loop(0, tr // RB, p2, 0, unroll=4)
    l_ref[...] = m_ref[...] + jnp.log(jnp.sum(t_scr[...], axis=1, keepdims=True))
    w = w_ref[...]
    wh = w.astype(jnp.bfloat16)
    wl = (w - wh.astype(jnp.float32)).astype(jnp.bfloat16)
    y = y_ref[...]
    yh = y.astype(jnp.bfloat16)
    yl = (y - yh.astype(jnp.float32)).astype(jnp.bfloat16)
    acc = jnp.dot(wh, yh, preferred_element_type=jnp.float32)
    acc = acc + jnp.dot(wh, yl, preferred_element_type=jnp.float32)
    acc = acc + jnp.dot(wl, yh, preferred_element_type=jnp.float32)
    p_ref[...] = acc


def final_local(h, blocks, y, tr=256):
    R, width = blocks[0].shape
    C = width * len(blocks)
    F = y.shape[1]
    m, l, p = pl.pallas_call(
        _final_kernel,
        grid=(R // tr,),
        in_specs=[pl.BlockSpec((1, C), lambda i: (0, 0))]
        + [pl.BlockSpec((tr, width), lambda i: (i, 0)) for _ in blocks]
        + [pl.BlockSpec((C, F), lambda i: (0, 0))],
        out_specs=[pl.BlockSpec((tr, 1), lambda i: (i, 0)), pl.BlockSpec((tr, 1), lambda i: (i, 0)),
                   pl.BlockSpec((tr, F), lambda i: (i, 0))],
        out_shape=[jax.ShapeDtypeStruct((R, 1), jnp.float32), jax.ShapeDtypeStruct((R, 1), jnp.float32),
                   jax.ShapeDtypeStruct((R, F), jnp.float32)],
        scratch_shapes=[pltpu.VMEM((tr, C), jnp.float32), pltpu.VMEM((tr, 128), jnp.float32),
                        pltpu.VMEM((tr, 128), jnp.float32)],
    )(h.reshape(1, C), *blocks, y)
    return m.reshape(R), l.reshape(R), p


entropy_scale = 0.02


def shift_pairs(n, s):
    return [(i, (i + s) % n) for i in range(n)]


def pair_scores(block_rows, block_square, columns):
    column_square = jnp.sum(columns * columns, axis=1)
    cross = lax.dot_general(
        block_rows,
        columns,
        (((1,), (1,)), ((), ())),
        precision=lax.Precision.HIGH,
        preferred_element_type=jnp.float32,
    )
    cost = (block_square[:, None] + column_square[None, :] - 2.0 * cross) / block_rows.shape[1]
    return -cost / entropy_scale


def lse_across(local_lse, axis):
    n = lax.axis_size(axis)
    vals = [local_lse] + [lax.ppermute(local_lse, axis, shift_pairs(n, s)) for s in range(1, n)]
    stacked = jnp.stack(vals)
    top = jnp.max(stacked, axis=0)
    return top + jnp.log(jnp.sum(jnp.exp(stacked - top[None]), axis=0))


def reorder(vec, order):
    n = order.shape[0]
    return jnp.take(vec.reshape(n, -1), order, axis=0).reshape(-1)


def scatter_obs(partial, peaks, final_lse):
    n = lax.axis_size("obs")
    half = n // 2
    o = lax.axis_index("obs")
    x = o // 2
    c = o % 2
    share = partial.shape[0] // n
    p4 = partial.reshape(half, 2, share, partial.shape[1])
    m4 = peaks.reshape(half, 2, share)
    keep = lax.dynamic_index_in_dim(p4, c, axis=1, keepdims=False)
    give = lax.dynamic_index_in_dim(p4, 1 - c, axis=1, keepdims=False)
    m_keep = lax.dynamic_index_in_dim(m4, c, axis=1, keepdims=False)
    m_give = lax.dynamic_index_in_dim(m4, 1 - c, axis=1, keepdims=False)
    partner = [(i, i ^ 1) for i in range(n)]
    got = lax.ppermute(give, "obs", partner)
    m_got = lax.ppermute(m_give, "obs", partner)
    top = jnp.maximum(m_keep, m_got)
    acc = keep * jnp.exp(m_keep - top)[..., None] + got * jnp.exp(m_got - top)[..., None]
    pieces = [(lax.dynamic_index_in_dim(acc, x, axis=0, keepdims=False),
               lax.dynamic_index_in_dim(top, x, axis=0, keepdims=False))]
    for k in range(1, half):
        pairs = [(i, ((i // 2 + k) % half) * 2 + i % 2) for i in range(n)]
        j = (x + k) % half
        pieces.append((
            lax.ppermute(lax.dynamic_index_in_dim(acc, j, axis=0, keepdims=False), "obs", pairs),
            lax.ppermute(lax.dynamic_index_in_dim(top, j, axis=0, keepdims=False), "obs", pairs),
        ))
    own_lse = lax.dynamic_slice_in_dim(final_lse, o * share, share)
    total = pieces[0][0] * jnp.exp(pieces[0][1] - own_lse)[:, None]
    for piece, piece_top in pieces[1:]:
        total = total + piece * jnp.exp(piece_top - own_lse)[:, None]
    return total


def on_device(model_days, obs_days):
    row_square = jnp.sum(model_days * model_days, axis=1)
    row_count = model_days.shape[0]
    n_mod = lax.axis_size("mod")
    m = lax.axis_index("mod")
    col_count = obs_days.shape[0] * n_mod
    log_obs = math.log(col_count * lax.axis_size("obs"))
    log_model = math.log(row_count * n_mod)
    blocks = [obs_days] + [
        lax.ppermute(obs_days, "mod", shift_pairs(n_mod, s)) for s in range(1, n_mod)
    ]
    order = (m - jnp.arange(n_mod)) % n_mod
    gathered = jnp.concatenate(blocks, axis=0)
    base_blocks = [pair_scores(model_days, row_square, b) for b in blocks]

    def split(vec):
        return jnp.split(vec, n_mod)

    def row_lse(col_potential):
        parts = []
        for hb, sb in zip(split(col_potential / entropy_scale), base_blocks):
            scores = hb[None, :] + sb
            peaks = jnp.max(scores, axis=1)
            parts.append(peaks + jnp.log(jnp.sum(jnp.exp(scores - peaks[:, None]), axis=1)))
        stacked = jnp.stack(parts)
        top = jnp.max(stacked, axis=0)
        local = top + jnp.log(jnp.sum(jnp.exp(stacked - top[None]), axis=0))
        return lse_across(local, "obs")

    def col_lse(row_potential):
        g = (row_potential / entropy_scale)[:, None]
        parts = []
        for sb in base_blocks:
            col_scores = g + sb
            col_peaks = jnp.max(col_scores, axis=0)
            parts.append(col_peaks + jnp.log(jnp.sum(jnp.exp(col_scores - col_peaks[None, :]), axis=0)))
        return jnp.concatenate(parts)

    col_shift = jnp.zeros((col_count,), jnp.float32)
    for iteration in range(ITERS):
        row_potential = -entropy_scale * (row_lse(col_shift) - log_obs)
        local = col_lse(row_potential)
        col_global = lse_across(reorder(local, order), "mod")
        col_potential = -entropy_scale * (col_global - log_model)
        col_shift = reorder(col_potential, order)
    peaks, local, partial_map = final_local(col_shift / entropy_scale, base_blocks, gathered)
    final_lse = lse_across(local, "obs")
    row_potential = -entropy_scale * (final_lse - log_obs)
    mapped = scatter_obs(partial_map, peaks, final_lse)
    return (mapped, row_potential, col_potential)


def solution(mesh):
    in_specs = (P(("region", "mod"), None), P(("region", "obs", "mod"), None))
    out_specs = (P(("region", "mod", "obs"), None), P(("region", "mod")), P(("region", "obs")))
    return jax.shard_map(
        on_device, mesh=mesh, in_specs=in_specs, out_specs=out_specs, check_vma=False
    )
```

profile of v0, /device:TPU:0, one launch (start us, length us, event | category | flops | bytes accessed | tf_op | source)
XLA Modules:
  0.0 125.1 jit_solution(14726680588081896160)
XLA Ops:
  0.6 5.1 %collective-permute-start.2 = (f32[512,128]{1,0:T(8,128)}, f32[512,128]{1,0:T(8,128)S(1)}, u32[]{:S(2)}, u32[]{:S(2)}) collective-permute-start(f32[512,128]{1,0:T(8,128)} %param.5), channel_id=1, source_target_pairs={{0,12},{4,0},{8,4},{12,8},{1,13},{5,1},{9,5},{13,9},{2,14},{6,2},{... | collective-permute-start | bytes 786440 | tf_op jit(solution)/shard_map/ppermute | solution.py:162
  7.9 1.6 %multiply_reduce_fusion = f32[2048]{0:T(1024)S(1)} fusion(f32[2048,128]{1,0:T(8,128)} %param.4), kind=kLoop, calls=%fused_computation.37 | loop fusion | flops 522240 | bytes 1056768 | tf_op jit(solution)/shard_map/reduce_sum | solution.py:154
  9.5 3.9 %fusion.23 = (f32[2048]{0:T(1024)S(1)}, f32[2048,512]{1,0:T(8,128)S(1)}) fusion(f32[2048,128]{1,0:T(8,128)} %param.4, f32[512,128]{1,0:T(8,128)} %param.5, f32[512]{0:T(512)S(1)} %multiply_reduce_fusion.4, f32[2048]{0:T(1024)S(1)} %multiply_reduce_fusion), kind=kOutput, calls=%fused_computation.134 | convolution fusion | flops 812644352 | bytes 5523456 | tf_op jit(solution)/shard_map/dot_general | solution.py:95
  13.5 1.7 %exponential_reduce_fusion.15 = f32[2048]{0:T(1024)S(1)} fusion(f32[2048,512]{1,0:T(8,128)S(1)} %get-tuple-element.62.refs_1_, f32[2048]{0:T(1024)S(1)} %get-tuple-element.61), kind=kLoop, calls=%fused_computation.22 | loop fusion | flops 2095104 | bytes 4210688 | tf_op jit(solution)/shard_map/reduce_sum | solution.py:176
  15.4 2.6 %fusion.25 = (f32[2048]{0:T(1024)S(1)}, f32[2048,512]{1,0:T(8,128)S(1)}) fusion(f32[2048,128]{1,0:T(8,128)S(1)} %copy-done.8, f32[512,128]{1,0:T(8,128)S(1)} %collective-permute-done.2, f32[512]{0:T(512)S(1)} %multiply_reduce_fusion.1, f32[2048]{0:T(1024)S(1)} %multiply_reduce_fusion), kind=kOutput, calls=%fused_computation.136 | convolution fusion | flops 812644352 | bytes 5523456 | tf_op jit(solution)/shard_map/dot_general | solution.py:95
  17.9 1.7 %exponential_reduce_fusion.12 = f32[2048]{0:T(1024)S(1)} fusion(f32[2048,512]{1,0:T(8,128)S(1)} %get-tuple-element.66.refs_4_, f32[2048]{0:T(1024)S(1)} %get-tuple-element.65), kind=kLoop, calls=%fused_computation.16 | loop fusion | flops 2095104 | bytes 4210688 | tf_op jit(solution)/shard_map/reduce_sum | solution.py:176
  19.6 8.6 %collective-permute-done.1 = f32[512,128]{1,0:T(8,128)S(1)} collective-permute-done((f32[512,128]{1,0:T(8,128)}, f32[512,128]{1,0:T(8,128)S(1)}, u32[]{:S(2)}, u32[]{:S(2)}) %collective-permute-start.1) | collective-permute-done | bytes 262176 | tf_op jit(solution)/shard_map/ppermute | solution.py:162
  28.4 2.6 %fusion.24 = (f32[2048]{0:T(1024)S(1)}, f32[2048,512]{1,0:T(8,128)S(1)}) fusion(f32[2048,128]{1,0:T(8,128)S(1)} %copy-done.8, f32[512,128]{1,0:T(8,128)S(1)} %collective-permute-done.1, f32[512]{0:T(512)S(1)} %multiply_reduce_fusion.2, f32[2048]{0:T(1024)S(1)} %multiply_reduce_fusion), kind=kOutput, calls=%fused_computation.135 | convolution fusion | flops 812644352 | bytes 5523456 | tf_op jit(solution)/shard_map/dot_general | solution.py:95
  31.0 1.9 %exponential_reduce_fusion.13 = f32[2048]{0:T(1024)S(1)} fusion(f32[2048,512]{1,0:T(8,128)S(1)} %get-tuple-element.64.refs_3_, f32[2048]{0:T(1024)S(1)} %get-tuple-element.63), kind=kLoop, calls=%fused_computation.18 | loop fusion | flops 2095104 | bytes 4210688 | tf_op jit(solution)/shard_map/reduce_sum | solution.py:176
  33.0 2.6 %fusion.22 = (f32[2048]{0:T(1024)S(1)}, f32[2048,512]{1,0:T(8,128)S(1)}) fusion(f32[2048,128]{1,0:T(8,128)S(1)} %copy-done.8, f32[512,128]{1,0:T(8,128)S(1)} %collective-permute-done, f32[512]{0:T(512)S(1)} %multiply_reduce_fusion.3, f32[2048]{0:T(1024)S(1)} %multiply_reduce_fusion), kind=kOutput, calls=%fused_computation.133 | convolution fusion | flops 812644352 | bytes 5523456 | tf_op jit(solution)/shard_map/dot_general | solution.py:95
  35.6 1.7 %exponential_reduce_fusion.14 = f32[2048]{0:T(1024)S(1)} fusion(f32[2048,512]{1,0:T(8,128)S(1)} %get-tuple-element.60.refs_2_, f32[2048]{0:T(1024)S(1)} %get-tuple-element.59), kind=kLoop, calls=%fused_computation.20 | loop fusion | flops 2095104 | bytes 4210688 | tf_op jit(solution)/shard_map/reduce_sum | solution.py:176
  42.3 1.7 %exponential_reduce_fusion.11 = (f32[512]{0:T(512)S(1)}, f32[512]{0:T(512)S(1)}, f32[512]{0:T(512)S(1)}, f32[512]{0:T(512)S(1)}) fusion(f32[2048,512]{1,0:T(8,128)S(1)} %get-tuple-element.62.refs_1_, f32[512]{0:T(512)S(1)} %add_reduce_fusion.11, f32[2048]{0:T(1024)S(1)} %add_multiply_fusion.5, f32[2048,512]{1,0:T(8,128)S(1)} %get-tuple-element.60.refs_2_, ...), kind=kLoop, calls=%fused_computation.15 | loop fusion | flops 9435136 | bytes 16795648 | tf_op jit(solution)/shard_map/reduce_sum | solution.py:188
  44.0 2.3 %exponential_reduce_fusion.10 = (f32[512]{0:T(512)S(1)}, f32[512]{0:T(512)S(1)}, f32[512]{0:T(512)S(1)}) fusion(f32[2048,512]{1,0:T(8,128)S(1)} %get-tuple-element.60.refs_2_, f32[512]{0:T(512)S(1)} %get-tuple-element.18, f32[2048]{0:T(1024)S(1)} %add_multiply_fusion.5, f32[512]{0:T(512)S(1)} %get-tuple-element.20, ...), kind=kLoop, calls=%fused_computation.14 | loop fusion | flops 9435648 | bytes 12603392 | tf_op jit(solution)/shard_map/reduce_sum | solution.py:188
  47.5 3.3 %collective-permute-start.8 = (f32[2048]{0:T(1024)S(1)}, f32[2048]{0:T(1024)S(1)}, u32[]{:S(2)}, u32[]{:S(2)}) collective-permute-start(f32[2048]{0:T(1024)S(1)} %bitcast.111), channel_id=1, source_target_pairs={{0,12},{4,0},{8,4},{12,8},{1,13},{5,1},{9,5},{13,9},{2,14},{6,2},{... | collective-permute-start | bytes 24584 | tf_op jit(solution)/shard_map/ppermute | solution.py:108
  50.8 1.6 %collective-permute-done.6 = f32[2048]{0:T(1024)S(1)} collective-permute-done((f32[2048]{0:T(1024)S(1)}, f32[2048]{0:T(1024)S(1)}, u32[]{:S(2)}, u32[]{:S(2)}) %collective-permute-start.6) | collective-permute-done | bytes 8224 | tf_op jit(solution)/shard_map/ppermute | solution.py:108
  53.8 2.7 %add_reduce_fusion.4 = f32[2048]{0:T(1024)S(1)} fusion(f32[2048,512]{1,0:T(8,128)} %copy-done, f32[512]{0:T(512)S(1)} %bitcast.136), kind=kLoop, calls=%fused_computation.28 | loop fusion | flops 2095104 | bytes 4204544 | tf_op jit(solution)/shard_map/reduce_max | solution.py:175
  66.2 2.2 %collective-permute-done.10 = f32[2048]{0:T(1024)S(1)} collective-permute-done((f32[2048]{0:T(1024)S(1)}, f32[2048]{0:T(1024)S(1)}, u32[]{:S(2)}, u32[]{:S(2)}) %collective-permute-start.10) | collective-permute-done | bytes 8224 | tf_op jit(solution)/shard_map/ppermute | solution.py:108
  69.2 1.7 %exponential_reduce_fusion.3 = (f32[512]{0:T(512)S(1)}, f32[512]{0:T(512)S(1)}, f32[512]{0:T(512)S(1)}, f32[512]{0:T(512)S(1)}) fusion(f32[2048,512]{1,0:T(8,128)S(1)} %copy-done.7, f32[512]{0:T(512)S(1)} %add_reduce_fusion.3, f32[2048]{0:T(1024)S(1)} %add_multiply_fusion.3, f32[2048,512]{1,0:T(8,128)S(1)} %copy-done.5, f32[2048,512]{1,0:T(8,128)S(1)} %copy-done.3, ...), kind=kLoop, calls=%fused_computation.7 | loop fusion | flops 9435136 | bytes 16795648 | tf_op jit(solution)/shard_map/reduce_sum | solution.py:188
  70.9 2.2 %exponential_reduce_fusion.2 = (f32[512]{0:T(512)S(1)}, f32[512]{0:T(512)S(1)}, f32[512]{0:T(512)S(1)}) fusion(f32[2048,512]{1,0:T(8,128)S(1)} %copy-done.5, f32[512]{0:T(512)S(1)} %get-tuple-element.11, f32[2048]{0:T(1024)S(1)} %add_multiply_fusion.3, f32[512]{0:T(512)S(1)} %get-tuple-element.13, f32[2048,512]{1,0:T(8,128)S(1)} %copy-done.1, ...), kind=kLoop, calls=%fused_computation.6 | loop fusion | flops 9435648 | bytes 12603392 | tf_op jit(solution)/shard_map/reduce_sum | solution.py:188
  73.9 1.9 %collective-permute-start.12 = (f32[2048]{0:T(1024)S(1)}, f32[2048]{0:T(1024)S(1)}, u32[]{:S(2)}, u32[]{:S(2)}) collective-permute-start(f32[2048]{0:T(1024)S(1)} %bitcast.113), channel_id=1, source_target_pairs={{0,4},{4,8},{8,12},{12,0},{1,5},{5,9},{9,13},{13,1},{2,6},{6,10},{... | collective-permute-start | bytes 24584 | tf_op jit(solution)/shard_map/ppermute | solution.py:108
  75.8 1.9 %collective-permute-start.13 = (f32[2048]{0:T(1024)S(1)}, f32[2048]{0:T(1024)S(1)}, u32[]{:S(2)}, u32[]{:S(2)}) collective-permute-start(f32[2048]{0:T(1024)S(1)} %bitcast.114), channel_id=1, source_target_pairs={{0,8},{4,12},{8,0},{12,4},{1,9},{5,13},{9,1},{13,5},{2,10},{6,14},... | collective-permute-start | bytes 24584 | tf_op jit(solution)/shard_map/ppermute | solution.py:108
  83.4 21.4 %shard_map.49 = (f32[2048,1]{1,0:T(8,128)}, f32[2048,1]{1,0:T(8,128)}, f32[2048,128]{1,0:T(8,128)}) custom-call(f32[1,2048]{1,0:T(1,128)} %bitcast.108, f32[2048,512]{1,0:T(8,128)} %copy-done.6, f32[2048,512]{1,0:T(8,128)} %copy-done.4, f32[2048,512]{1,0:T(8,128)} %copy-done.2, f32[2048,512]{1,0:T(8,128)} %copy-done, f32[2048,128]{1,0:T(8,128)} %pad_maximum_fusion.refs_5_), custom_call_target="tpu_custom_call" | custom-call | tf_op jit(solution)/shard_map/pallas_call | solution.py:70
  104.8 1.6 %reduce.29 = f32[2048]{0:T(1024)S(1)} reduce(f32[2048,1]{1,0:T(8,128)} %get-tuple-element.9, f32[]{:T(128)} %constant.125), dimensions={1}, to_apply=%get-tuple-element.9.reduce_sub_computation | reduce | bytes 16388 | tf_op jit(solution)/shard_map/pallas_call | solution.py:70
  117.0 7.2 %collective-permute-done.20 = f32[512,128]{1,0:T(8,128)S(1)} collective-permute-done((f32[512,128]{1,0:T(8,128)S(1)}, f32[512,128]{1,0:T(8,128)S(1)}, u32[]{:S(2)}, u32[]{:S(2)}) %collective-permute-start.20) | collective-permute-done | bytes 262176 | tf_op jit(solution)/shard_map/ppermute | solution.py:143
  (141 shorter events, 38.4 us)
Async XLA Ops:
  0.6 14.6 %collective-permute-start.2 = (f32[512,128]{1,0:T(8,128)}, f32[512,128]{1,0:T(8,128)S(1)}, u32[]{:S(2)}, u32[]{:S(2)}) collective-permute-start(f32[512,128]{1,0:T(8,128)} %param.5), channel_id=1, source_target_pairs={{0,12},{4,0},{8,4},{12,8},{1,13},{5,1},{9,5},{13,9},{2,14},{6,2},{... | collective-permute-start | bytes 786440 | tf_op jit(solution)/shard_map/ppermute | solution.py:162
  5.8 22.5 %collective-permute-start.1 = (f32[512,128]{1,0:T(8,128)}, f32[512,128]{1,0:T(8,128)S(1)}, u32[]{:S(2)}, u32[]{:S(2)}) collective-permute-start(f32[512,128]{1,0:T(8,128)} %param.5), channel_id=1, source_target_pairs={{0,8},{4,12},{8,0},{12,4},{1,9},{5,13},{9,1},{13,5},{2,10},{6,14},... | collective-permute-start | bytes 786440 | tf_op jit(solution)/shard_map/ppermute | solution.py:162
  5.8 27.1 %collective-permute-start = (f32[512,128]{1,0:T(8,128)}, f32[512,128]{1,0:T(8,128)S(1)}, u32[]{:S(2)}, u32[]{:S(2)}) collective-permute-start(f32[512,128]{1,0:T(8,128)} %param.5), channel_id=1, source_target_pairs={{0,4},{4,8},{8,12},{12,0},{1,5},{5,9},{9,13},{13,1},{2,6},{6,10},{... | collective-permute-start | bytes 786440 | tf_op jit(solution)/shard_map/ppermute | solution.py:162
  13.5 28.8 %copy-start.6 = (f32[2048,512]{1,0:T(8,128)}, f32[2048,512]{1,0:T(8,128)S(1)}, u32[]{:S(2)}) copy-start(f32[2048,512]{1,0:T(8,128)S(1)} %get-tuple-element.62.refs_1_) | copy-start | bytes 12582916
  17.9 26.0 %copy-start = (f32[2048,512]{1,0:T(8,128)}, f32[2048,512]{1,0:T(8,128)S(1)}, u32[]{:S(2)}) copy-start(f32[2048,512]{1,0:T(8,128)S(1)} %get-tuple-element.66.refs_4_) | copy-start | bytes 12582916
  37.4 3.1 %collective-permute-start.3 = (f32[2048]{0:T(1024)S(1)}, f32[2048]{0:T(1024)S(1)}, u32[]{:S(2)}, u32[]{:S(2)}) collective-permute-start(f32[2048]{0:T(1024)S(1)} %get-tuple-element.56), channel_id=1, source_target_pairs={{0,1},{1,2},{2,3},{3,0},{4,5},{5,6},{6,7},{7,4},{8,9},{9,10},{10,1... | collective-permute-start | bytes 24584 | tf_op jit(solution)/shard_map/ppermute | solution.py:108
  37.5 3.7 %collective-permute-start.4 = (f32[2048]{0:T(1024)S(1)}, f32[2048]{0:T(1024)S(1)}, u32[]{:S(2)}, u32[]{:S(2)}) collective-permute-start(f32[2048]{0:T(1024)S(1)} %get-tuple-element.56), channel_id=1, source_target_pairs={{0,2},{1,3},{2,0},{3,1},{4,6},{5,7},{6,4},{7,5},{8,10},{9,11},{10,... | collective-permute-start | bytes 24584 | tf_op jit(solution)/shard_map/ppermute | solution.py:108
  39.1 2.8 %collective-permute-start.5 = (f32[2048]{0:T(1024)S(1)}, f32[2048]{0:T(1024)S(1)}, u32[]{:S(2)}, u32[]{:S(2)}) collective-permute-start(f32[2048]{0:T(1024)S(1)} %get-tuple-element.56), channel_id=1, source_target_pairs={{0,3},{1,0},{2,1},{3,2},{4,7},{5,4},{6,5},{7,6},{8,11},{9,8},{10,9... | collective-permute-start | bytes 24584 | tf_op jit(solution)/shard_map/ppermute | solution.py:108
  47.0 5.5 %collective-permute-start.6 = (f32[2048]{0:T(1024)S(1)}, f32[2048]{0:T(1024)S(1)}, u32[]{:S(2)}, u32[]{:S(2)}) collective-permute-start(f32[2048]{0:T(1024)S(1)} %bitcast.109), channel_id=1, source_target_pairs={{0,4},{4,8},{8,12},{12,0},{1,5},{5,9},{9,13},{13,1},{2,6},{6,10},{... | collective-permute-start | bytes 24584 | tf_op jit(solution)/shard_map/ppermute | solution.py:108
  47.5 4.9 %collective-permute-start.7 = (f32[2048]{0:T(1024)S(1)}, f32[2048]{0:T(1024)S(1)}, u32[]{:S(2)}, u32[]{:S(2)}) collective-permute-start(f32[2048]{0:T(1024)S(1)} %bitcast.110), channel_id=1, source_target_pairs={{0,8},{4,12},{8,0},{12,4},{1,9},{5,13},{9,1},{13,5},{2,10},{6,14},... | collective-permute-start | bytes 24584 | tf_op jit(solution)/shard_map/ppermute | solution.py:108
  47.5 5.5 %collective-permute-start.8 = (f32[2048]{0:T(1024)S(1)}, f32[2048]{0:T(1024)S(1)}, u32[]{:S(2)}, u32[]{:S(2)}) collective-permute-start(f32[2048]{0:T(1024)S(1)} %bitcast.111), channel_id=1, source_target_pairs={{0,12},{4,0},{8,4},{12,8},{1,13},{5,1},{9,5},{13,9},{2,14},{6,2},{... | collective-permute-start | bytes 24584 | tf_op jit(solution)/shard_map/ppermute | solution.py:108
  64.6 3.7 %collective-permute-start.10 = (f32[2048]{0:T(1024)S(1)}, f32[2048]{0:T(1024)S(1)}, u32[]{:S(2)}, u32[]{:S(2)}) collective-permute-start(f32[2048]{0:T(1024)S(1)} %get-tuple-element.50), channel_id=1, source_target_pairs={{0,2},{1,3},{2,0},{3,1},{4,6},{5,7},{6,4},{7,5},{8,10},{9,11},{10,... | collective-permute-start | bytes 24584 | tf_op jit(solution)/shard_map/ppermute | solution.py:108
  65.6 2.7 %collective-permute-start.11 = (f32[2048]{0:T(1024)S(1)}, f32[2048]{0:T(1024)S(1)}, u32[]{:S(2)}, u32[]{:S(2)}) collective-permute-start(f32[2048]{0:T(1024)S(1)} %get-tuple-element.50), channel_id=1, source_target_pairs={{0,3},{1,0},{2,1},{3,2},{4,7},{5,4},{6,5},{7,6},{8,11},{9,8},{10,9... | collective-permute-start | bytes 24584 | tf_op jit(solution)/shard_map/ppermute | solution.py:108
  65.6 3.1 %collective-permute-start.9 = (f32[2048]{0:T(1024)S(1)}, f32[2048]{0:T(1024)S(1)}, u32[]{:S(2)}, u32[]{:S(2)}) collective-permute-start(f32[2048]{0:T(1024)S(1)} %get-tuple-element.50), channel_id=1, source_target_pairs={{0,1},{1,2},{2,3},{3,0},{4,5},{5,6},{6,7},{7,4},{8,9},{9,10},{10,1... | collective-permute-start | bytes 24584 | tf_op jit(solution)/shard_map/ppermute | solution.py:108
  73.9 5.5 %collective-permute-start.12 = (f32[2048]{0:T(1024)S(1)}, f32[2048]{0:T(1024)S(1)}, u32[]{:S(2)}, u32[]{:S(2)}) collective-permute-start(f32[2048]{0:T(1024)S(1)} %bitcast.113), channel_id=1, source_target_pairs={{0,4},{4,8},{8,12},{12,0},{1,5},{5,9},{9,13},{13,1},{2,6},{6,10},{... | collective-permute-start | bytes 24584 | tf_op jit(solution)/shard_map/ppermute | solution.py:108
  75.8 4.5 %collective-permute-start.13 = (f32[2048]{0:T(1024)S(1)}, f32[2048]{0:T(1024)S(1)}, u32[]{:S(2)}, u32[]{:S(2)}) collective-permute-start(f32[2048]{0:T(1024)S(1)} %bitcast.114), channel_id=1, source_target_pairs={{0,8},{4,12},{8,0},{12,4},{1,9},{5,13},{9,1},{13,5},{2,10},{6,14},... | collective-permute-start | bytes 24584 | tf_op jit(solution)/shard_map/ppermute | solution.py:108
  77.7 3.7 %collective-permute-start.14 = (f32[2048]{0:T(1024)S(1)}, f32[2048]{0:T(1024)S(1)}, u32[]{:S(2)}, u32[]{:S(2)}) collective-permute-start(f32[2048]{0:T(1024)S(1)} %bitcast.115), channel_id=1, source_target_pairs={{0,12},{4,0},{8,4},{12,8},{1,13},{5,1},{9,5},{13,9},{2,14},{6,2},{... | collective-permute-start | bytes 24584 | tf_op jit(solution)/shard_map/ppermute | solution.py:108
  106.4 7.0 %collective-permute-start.17 = (f32[2048]{0:T(1024)S(1)}, f32[2048]{0:T(1024)S(1)}, u32[]{:S(2)}, u32[]{:S(2)}) collective-permute-start(f32[2048]{0:T(1024)S(1)} %reduce.29), channel_id=1, source_target_pairs={{0,1},{1,2},{2,3},{3,0},{4,5},{5,6},{6,7},{7,4},{8,9},{9,10},{10,1... | collective-permute-start | bytes 24584 | tf_op jit(solution)/shard_map/ppermute | solution.py:108
  106.4 6.9 %collective-permute-start.18 = (f32[2048]{0:T(1024)S(1)}, f32[2048]{0:T(1024)S(1)}, u32[]{:S(2)}, u32[]{:S(2)}) collective-permute-start(f32[2048]{0:T(1024)S(1)} %reduce.29), channel_id=1, source_target_pairs={{0,2},{1,3},{2,0},{3,1},{4,6},{5,7},{6,4},{7,5},{8,10},{9,11},{10,... | collective-permute-start | bytes 24584 | tf_op jit(solution)/shard_map/ppermute | solution.py:108
  107.9 5.5 %collective-permute-start.19 = (f32[2048]{0:T(1024)S(1)}, f32[2048]{0:T(1024)S(1)}, u32[]{:S(2)}, u32[]{:S(2)}) collective-permute-start(f32[2048]{0:T(1024)S(1)} %reduce.29), channel_id=1, source_target_pairs={{0,3},{1,0},{2,1},{3,2},{4,7},{5,4},{6,5},{7,6},{8,11},{9,8},{10,9... | collective-permute-start | bytes 24584 | tf_op jit(solution)/shard_map/ppermute | solution.py:108
  110.9 1.7 %collective-permute-start.15 = (f32[2,512]{1,0:T(2,128)S(1)}, f32[2,512]{1,0:T(2,128)S(1)}, u32[]{:S(2)}, u32[]{:S(2)}) collective-permute-start(f32[2,512]{1,0:T(2,128)S(1)} %bitcast.139), channel_id=1, source_target_pairs={{0,1},{1,0},{2,3},{3,2},{4,5},{5,4},{6,7},{7,6},{8,9},{9,8},{10,11... | collective-permute-start | bytes 12296 | tf_op jit(solution)/shard_map/ppermute | solution.py:134
  112.0 2.1 %collective-permute-start.16 = (f32[2,512,128]{2,1,0:T(8,128)S(1)}, f32[2,512,128]{2,1,0:T(8,128)S(1)}, u32[]{:S(2)}, u32[]{:S(2)}) collective-permute-start(f32[2,512,128]{2,1,0:T(8,128)S(1)} %dynamic-slice_bitcast_fusion), channel_id=1, source_target_pairs={{0,1},{1,0},{2,3},{3,2},{4,5},{5,4},{6,7},{7,6},{8,9},{9,8},{10,11... | collective-permute-start | bytes 1572872 | tf_op jit(solution)/shard_map/ppermute | solution.py:133
  112.6 4.3 %collective-permute-start.21 = (f32[512]{0:T(512)S(1)}, f32[512]{0:T(512)S(1)}, u32[]{:S(2)}, u32[]{:S(2)}) collective-permute-start(f32[512]{0:T(512)S(1)} %bitcast.140), channel_id=1, source_target_pairs={{0,2},{1,3},{2,0},{3,1},{4,6},{5,7},{6,4},{7,5},{8,10},{9,11},{10,... | collective-permute-start | bytes 6152 | tf_op jit(solution)/shard_map/ppermute | solution.py:144
  115.5 8.7 %collective-permute-start.20 = (f32[512,128]{1,0:T(8,128)S(1)}, f32[512,128]{1,0:T(8,128)S(1)}, u32[]{:S(2)}, u32[]{:S(2)}) collective-permute-start(f32[512,128]{1,0:T(8,128)S(1)} %dynamic-slice_bitcast_fusion.1), channel_id=1, source_target_pairs={{0,2},{1,3},{2,0},{3,1},{4,6},{5,7},{6,4},{7,5},{8,10},{9,11},{10,... | collective-permute-start | bytes 786440 | tf_op jit(solution)/shard_map/ppermute | solution.py:143
  (8 other events, 47.0 us)
where the time goes:
time: 126 us; the launch traced here: 125 us
  other arithmetic  36.5 us (29%)
  waiting for transfers between devices  24.6 us (20%)
  starting transfers between devices  23.9 us (19%)
  Pallas kernels  21.4 us (17%)
  matrix products  11.6 us (9%)
  local copies, waits for them, and re-layouts  5.91 us (5%)
    pallas_call x1, Pallas kernels, final_local(): pl.pallas_call(_final_kernel, grid=(R // tr,), in_specs=[pl.BlockSpec((1,...  21.4 us
    ppermute x15, starting transfers between devices, lse_across(): lax.ppermute(local_lse, axis, shift_pairs(n, s))  15.6 us
    reduce_sum x8, other arithmetic, row_lse(): jnp.sum(jnp.exp(scores - peaks[:, None]), axis=1)  12.2 us
    dot_general x4, matrix products, pair_scores(): lax.dot_general(block_rows, columns, (((1,), (1,)), ((), ())), precision=...  11.6 us
    ppermute x3, waiting for transfers between devices, on_device(): lax.ppermute(obs_days, 'mod', shift_pairs(n_mod, s))  8.64 us
    ppermute x15, waiting for transfers between devices, lse_across(): lax.ppermute(local_lse, axis, shift_pairs(n, s))  8.13 us
    reduce_sum x4, other arithmetic, col_lse(): jnp.sum(jnp.exp(col_scores - col_peaks[None, :]), axis=0)  7.86 us
    ppermute x1, waiting for transfers between devices, scatter_obs(): lax.ppermute(lax.dynamic_index_in_dim(acc, j, axis=0, keepdims=False), 'o...  7.18 us
  transfers between devices with their start and end apart: 22, of which 12 were waited for; matrix products, arithmetic and copies ran while one was open for 19% of the time, Pallas kernels for 0%

commit v1 on v0

--- a/solution.py
+++ b/solution.py
@@ -18,9 +18,9 @@
 
 def _final_kernel(*refs):
     h_ref = refs[0]
-    nb = len(refs) - 8
+    nb = len(refs) - 9
     c_refs = refs[1:1 + nb]
-    y_ref, m_ref, l_ref, p_ref, w_ref, m_scr, t_scr = refs[1 + nb:]
+    y_ref, m_ref, l_ref, p_ref, w_ref, m_scr, t_scr, r_scr = refs[1 + nb:]
     tr = c_refs[0].shape[0]
     width = c_refs[0].shape[1]
 
@@ -36,11 +36,12 @@
         m_scr[pl.ds(r, RB), :] = m
         return carry
     lax.fori_loop(0, tr // RB, p1, 0, unroll=4)
-    m_ref[...] = jnp.max(m_scr[...], axis=1, keepdims=True)
+    r_scr[...] = jnp.max(m_scr[...], axis=1, keepdims=True)
+    m_ref[...] = jnp.max(m_scr[...].T, axis=0, keepdims=True)
 
     def p2(i, carry):
         r = pl.multiple_of(i * RB, RB)
-        mr = m_ref[pl.ds(r, RB), :]
+        mr = r_scr[pl.ds(r, RB), :]
         t = None
         for k, sc in enumerate(scores(r)):
             w = jnp.exp(sc - mr)
@@ -50,7 +51,7 @@
         t_scr[pl.ds(r, RB), :] = t
         return carry
     lax.fori_loop(0, tr // RB, p2, 0, unroll=4)
-    l_ref[...] = m_ref[...] + jnp.log(jnp.sum(t_scr[...], axis=1, keepdims=True))
+    l_ref[...] = m_ref[...] + jnp.log(jnp.sum(t_scr[...].T, axis=0, keepdims=True))
     w = w_ref[...]
     wh = w.astype(jnp.bfloat16)
     wl = (w - wh.astype(jnp.float32)).astype(jnp.bfloat16)
@@ -73,12 +74,12 @@
         in_specs=[pl.BlockSpec((1, C), lambda i: (0, 0))]
         + [pl.BlockSpec((tr, width), lambda i: (i, 0)) for _ in blocks]
         + [pl.BlockSpec((C, F), lambda i: (0, 0))],
-        out_specs=[pl.BlockSpec((tr, 1), lambda i: (i, 0)), pl.BlockSpec((tr, 1), lambda i: (i, 0)),
+        out_specs=[pl.BlockSpec((1, tr), lambda i: (0, i)), pl.BlockSpec((1, tr), lambda i: (0, i)),
                    pl.BlockSpec((tr, F), lambda i: (i, 0))],
-        out_shape=[jax.ShapeDtypeStruct((R, 1), jnp.float32), jax.ShapeDtypeStruct((R, 1), jnp.float32),
+        out_shape=[jax.ShapeDtypeStruct((1, R), jnp.float32), jax.ShapeDtypeStruct((1, R), jnp.float32),
                    jax.ShapeDtypeStruct((R, F), jnp.float32)],
         scratch_shapes=[pltpu.VMEM((tr, C), jnp.float32), pltpu.VMEM((tr, 128), jnp.float32),
-                        pltpu.VMEM((tr, 128), jnp.float32)],
+                        pltpu.VMEM((tr, 128), jnp.float32), pltpu.VMEM((tr, 1), jnp.float32)],
     )(h.reshape(1, C), *blocks, y)
     return m.reshape(R), l.reshape(R), p
 

time: 126 us -> 125 us (level)
  waiting for transfers between devices: 24.6 us -> 22 us
    ppermute x1, waiting for transfers between devices: 7.18 us -> 5.2 us  [scatter_obs(): lax.ppermute(lax.dynamic_index_in_dim(acc, j, axis=0, keepdims=False), 'o...]
    pallas_call x2 -> x1, other arithmetic: 3.12 us -> 1.36 us  [final_local(): pl.pallas_call(_final_kernel, grid=(R // tr,), in_specs=[pl.BlockSpec((1,...]
  transfers between devices with their start and end apart: 22 -> 22, of which waited for: 12 -> 11; matrix products, arithmetic and copies ran while one was open for 19% -> 21% of each run, Pallas kernels for 0% -> 0%
where the time goes in v1:
time: 125 us; the launch traced here: 124 us
  other arithmetic  36.9 us (30%)
  starting transfers between devices  24.5 us (20%)
  waiting for transfers between devices  22 us (18%)
  Pallas kernels  21.9 us (18%)
  matrix products  11.6 us (9%)
  local copies, waits for them, and re-layouts  6.42 us (5%)
    pallas_call x1, Pallas kernels, final_local(): pl.pallas_call(_final_kernel, grid=(R // tr,), in_specs=[pl.BlockSpec((1,...  21.9 us
    ppermute x15, starting transfers between devices, lse_across(): lax.ppermute(local_lse, axis, shift_pairs(n, s))  15.6 us
    reduce_sum x8, other arithmetic, row_lse(): jnp.sum(jnp.exp(scores - peaks[:, None]), axis=1)  12.2 us
    dot_general x4, matrix products, pair_scores(): lax.dot_general(block_rows, columns, (((1,), (1,)), ((), ())), precision=...  11.6 us
    ppermute x3, waiting for transfers between devices, on_device(): lax.ppermute(obs_days, 'mod', shift_pairs(n_mod, s))  8.64 us
    ppermute x15, waiting for transfers between devices, lse_across(): lax.ppermute(local_lse, axis, shift_pairs(n, s))  8.13 us
    reduce_sum x4, other arithmetic, col_lse(): jnp.sum(jnp.exp(col_scores - col_peaks[None, :]), axis=0)  7.86 us
    ppermute x3, starting transfers between devices, on_device(): lax.ppermute(obs_days, 'mod', shift_pairs(n_mod, s))  6.14 us
  transfers between devices with their start and end apart: 22, of which 11 were waited for; matrix products, arithmetic and copies ran while one was open for 21% of the time, Pallas kernels for 0%

profile of v1, /device:TPU:0, one launch (start us, length us, event | category | flops | bytes accessed | tf_op | source)
XLA Modules:
  0.0 124.4 jit_solution(7530400317003117315)
XLA Ops:
  0.6 5.1 %collective-permute-start.2 = (f32[512,128]{1,0:T(8,128)}, f32[512,128]{1,0:T(8,128)S(1)}, u32[]{:S(2)}, u32[]{:S(2)}) collective-permute-start(f32[512,128]{1,0:T(8,128)} %param.5), channel_id=1, source_target_pairs={{0,12},{4,0},{8,4},{12,8},{1,13},{5,1},{9,5},{13,9},{2,14},{6,2},{... | collective-permute-start | bytes 786440 | tf_op jit(solution)/shard_map/ppermute | solution.py:163
  7.9 1.6 %multiply_reduce_fusion = f32[2048]{0:T(1024)S(1)} fusion(f32[2048,128]{1,0:T(8,128)} %param.4), kind=kLoop, calls=%fused_computation.37 | loop fusion | flops 522240 | bytes 1056768 | tf_op jit(solution)/shard_map/reduce_sum | solution.py:155
  9.5 3.9 %fusion.23 = (f32[2048]{0:T(1024)S(1)}, f32[2048,512]{1,0:T(8,128)S(1)}) fusion(f32[2048,128]{1,0:T(8,128)} %param.4, f32[512,128]{1,0:T(8,128)} %param.5, f32[512]{0:T(512)S(1)} %multiply_reduce_fusion.4, f32[2048]{0:T(1024)S(1)} %multiply_reduce_fusion), kind=kOutput, calls=%fused_computation.134 | convolution fusion | flops 812644352 | bytes 5523456 | tf_op jit(solution)/shard_map/dot_general | solution.py:96
  13.5 1.7 %exponential_reduce_fusion.15 = f32[2048]{0:T(1024)S(1)} fusion(f32[2048,512]{1,0:T(8,128)S(1)} %get-tuple-element.62.refs_1_, f32[2048]{0:T(1024)S(1)} %get-tuple-element.61), kind=kLoop, calls=%fused_computation.22 | loop fusion | flops 2095104 | bytes 4210688 | tf_op jit(solution)/shard_map/reduce_sum | solution.py:177
  15.4 2.6 %fusion.25 = (f32[2048]{0:T(1024)S(1)}, f32[2048,512]{1,0:T(8,128)S(1)}) fusion(f32[2048,128]{1,0:T(8,128)S(1)} %copy-done.8, f32[512,128]{1,0:T(8,128)S(1)} %collective-permute-done.2, f32[512]{0:T(512)S(1)} %multiply_reduce_fusion.1, f32[2048]{0:T(1024)S(1)} %multiply_reduce_fusion), kind=kOutput, calls=%fused_computation.136 | convolution fusion | flops 812644352 | bytes 5523456 | tf_op jit(solution)/shard_map/dot_general | solution.py:96
  17.9 1.7 %exponential_reduce_fusion.12 = f32[2048]{0:T(1024)S(1)} fusion(f32[2048,512]{1,0:T(8,128)S(1)} %get-tuple-element.66.refs_4_, f32[2048]{0:T(1024)S(1)} %get-tuple-element.65), kind=kLoop, calls=%fused_computation.16 | loop fusion | flops 2095104 | bytes 4210688 | tf_op jit(solution)/shard_map/reduce_sum | solution.py:177
  19.6 8.6 %collective-permute-done.1 = f32[512,128]{1,0:T(8,128)S(1)} collective-permute-done((f32[512,128]{1,0:T(8,128)}, f32[512,128]{1,0:T(8,128)S(1)}, u32[]{:S(2)}, u32[]{:S(2)}) %collective-permute-start.1) | collective-permute-done | bytes 262176 | tf_op jit(solution)/shard_map/ppermute | solution.py:163
  28.4 2.6 %fusion.24 = (f32[2048]{0:T(1024)S(1)}, f32[2048,512]{1,0:T(8,128)S(1)}) fusion(f32[2048,128]{1,0:T(8,128)S(1)} %copy-done.8, f32[512,128]{1,0:T(8,128)S(1)} %collective-permute-done.1, f32[512]{0:T(512)S(1)} %multiply_reduce_fusion.2, f32[2048]{0:T(1024)S(1)} %multiply_reduce_fusion), kind=kOutput, calls=%fused_computation.135 | convolution fusion | flops 812644352 | bytes 5523456 | tf_op jit(solution)/shard_map/dot_general | solution.py:96
  31.0 1.9 %exponential_reduce_fusion.13 = f32[2048]{0:T(1024)S(1)} fusion(f32[2048,512]{1,0:T(8,128)S(1)} %get-tuple-element.64.refs_3_, f32[2048]{0:T(1024)S(1)} %get-tuple-element.63), kind=kLoop, calls=%fused_computation.18 | loop fusion | flops 2095104 | bytes 4210688 | tf_op jit(solution)/shard_map/reduce_sum | solution.py:177
  33.0 2.6 %fusion.22 = (f32[2048]{0:T(1024)S(1)}, f32[2048,512]{1,0:T(8,128)S(1)}) fusion(f32[2048,128]{1,0:T(8,128)S(1)} %copy-done.8, f32[512,128]{1,0:T(8,128)S(1)} %collective-permute-done, f32[512]{0:T(512)S(1)} %multiply_reduce_fusion.3, f32[2048]{0:T(1024)S(1)} %multiply_reduce_fusion), kind=kOutput, calls=%fused_computation.133 | convolution fusion | flops 812644352 | bytes 5523456 | tf_op jit(solution)/shard_map/dot_general | solution.py:96
  35.6 1.7 %exponential_reduce_fusion.14 = f32[2048]{0:T(1024)S(1)} fusion(f32[2048,512]{1,0:T(8,128)S(1)} %get-tuple-element.60.refs_2_, f32[2048]{0:T(1024)S(1)} %get-tuple-element.59), kind=kLoop, calls=%fused_computation.20 | loop fusion | flops 2095104 | bytes 4210688 | tf_op jit(solution)/shard_map/reduce_sum | solution.py:177
  37.5 1.6 %collective-permute-start.4 = (f32[2048]{0:T(1024)S(1)}, f32[2048]{0:T(1024)S(1)}, u32[]{:S(2)}, u32[]{:S(2)}) collective-permute-start(f32[2048]{0:T(1024)S(1)} %get-tuple-element.56), channel_id=1, source_target_pairs={{0,2},{1,3},{2,0},{3,1},{4,6},{5,7},{6,4},{7,5},{8,10},{9,11},{10,... | collective-permute-start | bytes 24584 | tf_op jit(solution)/shard_map/ppermute | solution.py:109
  42.3 1.7 %exponential_reduce_fusion.11 = (f32[512]{0:T(512)S(1)}, f32[512]{0:T(512)S(1)}, f32[512]{0:T(512)S(1)}, f32[512]{0:T(512)S(1)}) fusion(f32[2048,512]{1,0:T(8,128)S(1)} %get-tuple-element.62.refs_1_, f32[512]{0:T(512)S(1)} %add_reduce_fusion.11, f32[2048]{0:T(1024)S(1)} %add_multiply_fusion.5, f32[2048,512]{1,0:T(8,128)S(1)} %get-tuple-element.60.refs_2_, ...), kind=kLoop, calls=%fused_computation.15 | loop fusion | flops 9435136 | bytes 16795648 | tf_op jit(solution)/shard_map/reduce_sum | solution.py:189
  44.0 2.3 %exponential_reduce_fusion.10 = (f32[512]{0:T(512)S(1)}, f32[512]{0:T(512)S(1)}, f32[512]{0:T(512)S(1)}) fusion(f32[2048,512]{1,0:T(8,128)S(1)} %get-tuple-element.60.refs_2_, f32[512]{0:T(512)S(1)} %get-tuple-element.18, f32[2048]{0:T(1024)S(1)} %add_multiply_fusion.5, f32[512]{0:T(512)S(1)} %get-tuple-element.20, ...), kind=kLoop, calls=%fused_computation.14 | loop fusion | flops 9435648 | bytes 12603392 | tf_op jit(solution)/shard_map/reduce_sum | solution.py:189
  47.5 3.3 %collective-permute-start.8 = (f32[2048]{0:T(1024)S(1)}, f32[2048]{0:T(1024)S(1)}, u32[]{:S(2)}, u32[]{:S(2)}) collective-permute-start(f32[2048]{0:T(1024)S(1)} %bitcast.121), channel_id=1, source_target_pairs={{0,12},{4,0},{8,4},{12,8},{1,13},{5,1},{9,5},{13,9},{2,14},{6,2},{... | collective-permute-start | bytes 24584 | tf_op jit(solution)/shard_map/ppermute | solution.py:109
  50.8 1.6 %collective-permute-done.6 = f32[2048]{0:T(1024)S(1)} collective-permute-done((f32[2048]{0:T(1024)S(1)}, f32[2048]{0:T(1024)S(1)}, u32[]{:S(2)}, u32[]{:S(2)}) %collective-permute-start.6) | collective-permute-done | bytes 8224 | tf_op jit(solution)/shard_map/ppermute | solution.py:109
  53.8 2.7 %add_reduce_fusion.4 = f32[2048]{0:T(1024)S(1)} fusion(f32[2048,512]{1,0:T(8,128)} %copy-done, f32[512]{0:T(512)S(1)} %bitcast.144), kind=kLoop, calls=%fused_computation.28 | loop fusion | flops 2095104 | bytes 4204544 | tf_op jit(solution)/shard_map/reduce_max | solution.py:176
  66.2 2.2 %collective-permute-done.10 = f32[2048]{0:T(1024)S(1)} collective-permute-done((f32[2048]{0:T(1024)S(1)}, f32[2048]{0:T(1024)S(1)}, u32[]{:S(2)}, u32[]{:S(2)}) %collective-permute-start.10) | collective-permute-done | bytes 8224 | tf_op jit(solution)/shard_map/ppermute | solution.py:109
  69.2 1.7 %exponential_reduce_fusion.3 = (f32[512]{0:T(512)S(1)}, f32[512]{0:T(512)S(1)}, f32[512]{0:T(512)S(1)}, f32[512]{0:T(512)S(1)}) fusion(f32[2048,512]{1,0:T(8,128)S(1)} %copy-done.7, f32[512]{0:T(512)S(1)} %add_reduce_fusion.3, f32[2048]{0:T(1024)S(1)} %add_multiply_fusion.3, f32[2048,512]{1,0:T(8,128)S(1)} %copy-done.5, f32[2048,512]{1,0:T(8,128)S(1)} %copy-done.3, ...), kind=kLoop, calls=%fused_computation.7 | loop fusion | flops 9435136 | bytes 16795648 | tf_op jit(solution)/shard_map/reduce_sum | solution.py:189
  70.9 2.2 %exponential_reduce_fusion.2 = (f32[512]{0:T(512)S(1)}, f32[512]{0:T(512)S(1)}, f32[512]{0:T(512)S(1)}) fusion(f32[2048,512]{1,0:T(8,128)S(1)} %copy-done.5, f32[512]{0:T(512)S(1)} %get-tuple-element.11, f32[2048]{0:T(1024)S(1)} %add_multiply_fusion.3, f32[512]{0:T(512)S(1)} %get-tuple-element.13, f32[2048,512]{1,0:T(8,128)S(1)} %copy-done.1, ...), kind=kLoop, calls=%fused_computation.6 | loop fusion | flops 9435648 | bytes 12603392 | tf_op jit(solution)/shard_map/reduce_sum | solution.py:189
  73.9 1.9 %collective-permute-start.12 = (f32[2048]{0:T(1024)S(1)}, f32[2048]{0:T(1024)S(1)}, u32[]{:S(2)}, u32[]{:S(2)}) collective-permute-start(f32[2048]{0:T(1024)S(1)} %bitcast.123), channel_id=1, source_target_pairs={{0,4},{4,8},{8,12},{12,0},{1,5},{5,9},{9,13},{13,1},{2,6},{6,10},{... | collective-permute-start | bytes 24584 | tf_op jit(solution)/shard_map/ppermute | solution.py:109
  75.8 1.9 %collective-permute-start.13 = (f32[2048]{0:T(1024)S(1)}, f32[2048]{0:T(1024)S(1)}, u32[]{:S(2)}, u32[]{:S(2)}) collective-permute-start(f32[2048]{0:T(1024)S(1)} %bitcast.124), channel_id=1, source_target_pairs={{0,8},{4,12},{8,0},{12,4},{1,9},{5,13},{9,1},{13,5},{2,10},{6,14},... | collective-permute-start | bytes 24584 | tf_op jit(solution)/shard_map/ppermute | solution.py:109
  83.4 21.9 %shard_map.49 = (f32[1,2048]{1,0:T(1,128)}, f32[1,2048]{1,0:T(1,128)}, f32[2048,128]{1,0:T(8,128)}) custom-call(f32[1,2048]{1,0:T(1,128)} %bitcast.118, f32[2048,512]{1,0:T(8,128)} %copy-done.6, f32[2048,512]{1,0:T(8,128)} %copy-done.4, f32[2048,512]{1,0:T(8,128)} %copy-done.2, f32[2048,512]{1,0:T(8,128)} %copy-done, f32[2048,128]{1,0:T(8,128)} %pad_maximum_fusion.refs_5_), custom_call_target="tpu_custom_call" | custom-call | tf_op jit(solution)/shard_map/pallas_call | solution.py:71
  118.3 5.2 %collective-permute-done.20 = f32[512,128]{1,0:T(8,128)S(1)} collective-permute-done((f32[512,128]{1,0:T(8,128)S(1)}, f32[512,128]{1,0:T(8,128)S(1)}, u32[]{:S(2)}, u32[]{:S(2)}) %collective-permute-start.20) | collective-permute-done | bytes 262176 | tf_op jit(solution)/shard_map/ppermute | solution.py:144
  (141 shorter events, 39.2 us)
Async XLA Ops:
  0.6 14.6 %collective-permute-start.2 = (f32[512,128]{1,0:T(8,128)}, f32[512,128]{1,0:T(8,128)S(1)}, u32[]{:S(2)}, u32[]{:S(2)}) collective-permute-start(f32[512,128]{1,0:T(8,128)} %param.5), channel_id=1, source_target_pairs={{0,12},{4,0},{8,4},{12,8},{1,13},{5,1},{9,5},{13,9},{2,14},{6,2},{... | collective-permute-start | bytes 786440 | tf_op jit(solution)/shard_map/ppermute | solution.py:163
  5.8 22.5 %collective-permute-start.1 = (f32[512,128]{1,0:T(8,128)}, f32[512,128]{1,0:T(8,128)S(1)}, u32[]{:S(2)}, u32[]{:S(2)}) collective-permute-start(f32[512,128]{1,0:T(8,128)} %param.5), channel_id=1, source_target_pairs={{0,8},{4,12},{8,0},{12,4},{1,9},{5,13},{9,1},{13,5},{2,10},{6,14},... | collective-permute-start | bytes 786440 | tf_op jit(solution)/shard_map/ppermute | solution.py:163
  5.8 27.1 %collective-permute-start = (f32[512,128]{1,0:T(8,128)}, f32[512,128]{1,0:T(8,128)S(1)}, u32[]{:S(2)}, u32[]{:S(2)}) collective-permute-start(f32[512,128]{1,0:T(8,128)} %param.5), channel_id=1, source_target_pairs={{0,4},{4,8},{8,12},{12,0},{1,5},{5,9},{9,13},{13,1},{2,6},{6,10},{... | collective-permute-start | bytes 786440 | tf_op jit(solution)/shard_map/ppermute | solution.py:163
  13.5 28.8 %copy-start.6 = (f32[2048,512]{1,0:T(8,128)}, f32[2048,512]{1,0:T(8,128)S(1)}, u32[]{:S(2)}) copy-start(f32[2048,512]{1,0:T(8,128)S(1)} %get-tuple-element.62.refs_1_) | copy-start | bytes 12582916
  17.9 26.0 %copy-start = (f32[2048,512]{1,0:T(8,128)}, f32[2048,512]{1,0:T(8,128)S(1)}, u32[]{:S(2)}) copy-start(f32[2048,512]{1,0:T(8,128)S(1)} %get-tuple-element.66.refs_4_) | copy-start | bytes 12582916
  37.4 3.1 %collective-permute-start.3 = (f32[2048]{0:T(1024)S(1)}, f32[2048]{0:T(1024)S(1)}, u32[]{:S(2)}, u32[]{:S(2)}) collective-permute-start(f32[2048]{0:T(1024)S(1)} %get-tuple-element.56), channel_id=1, source_target_pairs={{0,1},{1,2},{2,3},{3,0},{4,5},{5,6},{6,7},{7,4},{8,9},{9,10},{10,1... | collective-permute-start | bytes 24584 | tf_op jit(solution)/shard_map/ppermute | solution.py:109
  37.5 3.7 %collective-permute-start.4 = (f32[2048]{0:T(1024)S(1)}, f32[2048]{0:T(1024)S(1)}, u32[]{:S(2)}, u32[]{:S(2)}) collective-permute-start(f32[2048]{0:T(1024)S(1)} %get-tuple-element.56), channel_id=1, source_target_pairs={{0,2},{1,3},{2,0},{3,1},{4,6},{5,7},{6,4},{7,5},{8,10},{9,11},{10,... | collective-permute-start | bytes 24584 | tf_op jit(solution)/shard_map/ppermute | solution.py:109
  39.1 2.8 %collective-permute-start.5 = (f32[2048]{0:T(1024)S(1)}, f32[2048]{0:T(1024)S(1)}, u32[]{:S(2)}, u32[]{:S(2)}) collective-permute-start(f32[2048]{0:T(1024)S(1)} %get-tuple-element.56), channel_id=1, source_target_pairs={{0,3},{1,0},{2,1},{3,2},{4,7},{5,4},{6,5},{7,6},{8,11},{9,8},{10,9... | collective-permute-start | bytes 24584 | tf_op jit(solution)/shard_map/ppermute | solution.py:109
  47.0 5.5 %collective-permute-start.6 = (f32[2048]{0:T(1024)S(1)}, f32[2048]{0:T(1024)S(1)}, u32[]{:S(2)}, u32[]{:S(2)}) collective-permute-start(f32[2048]{0:T(1024)S(1)} %bitcast.119), channel_id=1, source_target_pairs={{0,4},{4,8},{8,12},{12,0},{1,5},{5,9},{9,13},{13,1},{2,6},{6,10},{... | collective-permute-start | bytes 24584 | tf_op jit(solution)/shard_map/ppermute | solution.py:109
  47.5 4.9 %collective-permute-start.7 = (f32[2048]{0:T(1024)S(1)}, f32[2048]{0:T(1024)S(1)}, u32[]{:S(2)}, u32[]{:S(2)}) collective-permute-start(f32[2048]{0:T(1024)S(1)} %bitcast.120), channel_id=1, source_target_pairs={{0,8},{4,12},{8,0},{12,4},{1,9},{5,13},{9,1},{13,5},{2,10},{6,14},... | collective-permute-start | bytes 24584 | tf_op jit(solution)/shard_map/ppermute | solution.py:109
  47.5 5.5 %collective-permute-start.8 = (f32[2048]{0:T(1024)S(1)}, f32[2048]{0:T(1024)S(1)}, u32[]{:S(2)}, u32[]{:S(2)}) collective-permute-start(f32[2048]{0:T(1024)S(1)} %bitcast.121), channel_id=1, source_target_pairs={{0,12},{4,0},{8,4},{12,8},{1,13},{5,1},{9,5},{13,9},{2,14},{6,2},{... | collective-permute-start | bytes 24584 | tf_op jit(solution)/shard_map/ppermute | solution.py:109
  64.6 3.7 %collective-permute-start.10 = (f32[2048]{0:T(1024)S(1)}, f32[2048]{0:T(1024)S(1)}, u32[]{:S(2)}, u32[]{:S(2)}) collective-permute-start(f32[2048]{0:T(1024)S(1)} %get-tuple-element.50), channel_id=1, source_target_pairs={{0,2},{1,3},{2,0},{3,1},{4,6},{5,7},{6,4},{7,5},{8,10},{9,11},{10,... | collective-permute-start | bytes 24584 | tf_op jit(solution)/shard_map/ppermute | solution.py:109
  65.6 2.7 %collective-permute-start.11 = (f32[2048]{0:T(1024)S(1)}, f32[2048]{0:T(1024)S(1)}, u32[]{:S(2)}, u32[]{:S(2)}) collective-permute-start(f32[2048]{0:T(1024)S(1)} %get-tuple-element.50), channel_id=1, source_target_pairs={{0,3},{1,0},{2,1},{3,2},{4,7},{5,4},{6,5},{7,6},{8,11},{9,8},{10,9... | collective-permute-start | bytes 24584 | tf_op jit(solution)/shard_map/ppermute | solution.py:109
  65.6 3.1 %collective-permute-start.9 = (f32[2048]{0:T(1024)S(1)}, f32[2048]{0:T(1024)S(1)}, u32[]{:S(2)}, u32[]{:S(2)}) collective-permute-start(f32[2048]{0:T(1024)S(1)} %get-tuple-element.50), channel_id=1, source_target_pairs={{0,1},{1,2},{2,3},{3,0},{4,5},{5,6},{6,7},{7,4},{8,9},{9,10},{10,1... | collective-permute-start | bytes 24584 | tf_op jit(solution)/shard_map/ppermute | solution.py:109
  73.9 5.5 %collective-permute-start.12 = (f32[2048]{0:T(1024)S(1)}, f32[2048]{0:T(1024)S(1)}, u32[]{:S(2)}, u32[]{:S(2)}) collective-permute-start(f32[2048]{0:T(1024)S(1)} %bitcast.123), channel_id=1, source_target_pairs={{0,4},{4,8},{8,12},{12,0},{1,5},{5,9},{9,13},{13,1},{2,6},{6,10},{... | collective-permute-start | bytes 24584 | tf_op jit(solution)/shard_map/ppermute | solution.py:109
  75.8 4.5 %collective-permute-start.13 = (f32[2048]{0:T(1024)S(1)}, f32[2048]{0:T(1024)S(1)}, u32[]{:S(2)}, u32[]{:S(2)}) collective-permute-start(f32[2048]{0:T(1024)S(1)} %bitcast.124), channel_id=1, source_target_pairs={{0,8},{4,12},{8,0},{12,4},{1,9},{5,13},{9,1},{13,5},{2,10},{6,14},... | collective-permute-start | bytes 24584 | tf_op jit(solution)/shard_map/ppermute | solution.py:109
  77.7 3.7 %collective-permute-start.14 = (f32[2048]{0:T(1024)S(1)}, f32[2048]{0:T(1024)S(1)}, u32[]{:S(2)}, u32[]{:S(2)}) collective-permute-start(f32[2048]{0:T(1024)S(1)} %bitcast.125), channel_id=1, source_target_pairs={{0,12},{4,0},{8,4},{12,8},{1,13},{5,1},{9,5},{13,9},{2,14},{6,2},{... | collective-permute-start | bytes 24584 | tf_op jit(solution)/shard_map/ppermute | solution.py:109
  105.3 7.2 %collective-permute-start.17 = (f32[2048]{0:T(1024)}, f32[2048]{0:T(1024)S(1)}, u32[]{:S(2)}, u32[]{:S(2)}) collective-permute-start(f32[2048]{0:T(1024)} %bitcast.86), channel_id=1, source_target_pairs={{0,1},{1,2},{2,3},{3,0},{4,5},{5,6},{6,7},{7,4},{8,9},{9,10},{10,1... | collective-permute-start | bytes 24584 | tf_op jit(solution)/shard_map/ppermute | solution.py:109
  105.3 7.2 %collective-permute-start.18 = (f32[2048]{0:T(1024)}, f32[2048]{0:T(1024)S(1)}, u32[]{:S(2)}, u32[]{:S(2)}) collective-permute-start(f32[2048]{0:T(1024)} %bitcast.87), channel_id=1, source_target_pairs={{0,2},{1,3},{2,0},{3,1},{4,6},{5,7},{6,4},{7,5},{8,10},{9,11},{10,... | collective-permute-start | bytes 24584 | tf_op jit(solution)/shard_map/ppermute | solution.py:109
  106.7 5.8 %collective-permute-start.19 = (f32[2048]{0:T(1024)}, f32[2048]{0:T(1024)S(1)}, u32[]{:S(2)}, u32[]{:S(2)}) collective-permute-start(f32[2048]{0:T(1024)} %bitcast.88), channel_id=1, source_target_pairs={{0,3},{1,0},{2,1},{3,2},{4,7},{5,4},{6,5},{7,6},{8,11},{9,8},{10,9... | collective-permute-start | bytes 24584 | tf_op jit(solution)/shard_map/ppermute | solution.py:109
  110.0 1.7 %collective-permute-start.15 = (f32[2,512]{1,0:T(2,128)S(1)}, f32[2,512]{1,0:T(2,128)S(1)}, u32[]{:S(2)}, u32[]{:S(2)}) collective-permute-start(f32[2,512]{1,0:T(2,128)S(1)} %bitcast.147), channel_id=1, source_target_pairs={{0,1},{1,0},{2,3},{3,2},{4,5},{5,4},{6,7},{7,6},{8,9},{9,8},{10,11... | collective-permute-start | bytes 12296 | tf_op jit(solution)/shard_map/ppermute | solution.py:135
  111.2 2.8 %collective-permute-start.16 = (f32[2,512,128]{2,1,0:T(8,128)S(1)}, f32[2,512,128]{2,1,0:T(8,128)S(1)}, u32[]{:S(2)}, u32[]{:S(2)}) collective-permute-start(f32[2,512,128]{2,1,0:T(8,128)S(1)} %dynamic-slice_bitcast_fusion), channel_id=1, source_target_pairs={{0,1},{1,0},{2,3},{3,2},{4,5},{5,4},{6,7},{7,6},{8,9},{9,8},{10,11... | collective-permute-start | bytes 1572872 | tf_op jit(solution)/shard_map/ppermute | solution.py:134
  111.8 6.4 %collective-permute-start.21 = (f32[512]{0:T(512)S(1)}, f32[512]{0:T(512)S(1)}, u32[]{:S(2)}, u32[]{:S(2)}) collective-permute-start(f32[512]{0:T(512)S(1)} %bitcast.148), channel_id=1, source_target_pairs={{0,2},{1,3},{2,0},{3,1},{4,6},{5,7},{6,4},{7,5},{8,10},{9,11},{10,... | collective-permute-start | bytes 6152 | tf_op jit(solution)/shard_map/ppermute | solution.py:145
  115.4 8.0 %collective-permute-start.20 = (f32[512,128]{1,0:T(8,128)S(1)}, f32[512,128]{1,0:T(8,128)S(1)}, u32[]{:S(2)}, u32[]{:S(2)}) collective-permute-start(f32[512,128]{1,0:T(8,128)S(1)} %dynamic-slice_bitcast_fusion.1), channel_id=1, source_target_pairs={{0,2},{1,3},{2,0},{3,1},{4,6},{5,7},{6,4},{7,5},{8,10},{9,11},{10,... | collective-permute-start | bytes 786440 | tf_op jit(solution)/shard_map/ppermute | solution.py:144
  (8 other events, 47.0 us)

commit v2 on v1

--- a/solution.py
+++ b/solution.py
@@ -64,7 +64,7 @@
     p_ref[...] = acc
 
 
-def final_local(h, blocks, y, tr=256):
+def final_local(h, blocks, y, tr=512):
     R, width = blocks[0].shape
     C = width * len(blocks)
     F = y.shape[1]

time: 125 us -> 124 us (level)
  no operation moved by 1% of the time
where the time goes in v2:
time: 124 us
  other arithmetic  36.9 us (30%)
  starting transfers between devices  24.5 us (20%)
  waiting for transfers between devices  22 us (18%)
  Pallas kernels  21.3 us (17%)
  matrix products  11.6 us (9%)
  local copies, waits for them, and re-layouts  6.42 us (5%)
    pallas_call x1, Pallas kernels, final_local(): pl.pallas_call(_final_kernel, grid=(R // tr,), in_specs=[pl.BlockSpec((1,...  21.3 us
    ppermute x15, starting transfers between devices, lse_across(): lax.ppermute(local_lse, axis, shift_pairs(n, s))  15.5 us
    reduce_sum x8, other arithmetic, row_lse(): jnp.sum(jnp.exp(scores - peaks[:, None]), axis=1)  12.2 us
    dot_general x4, matrix products, pair_scores(): lax.dot_general(block_rows, columns, (((1,), (1,)), ((), ())), precision=...  11.6 us
    ppermute x3, waiting for transfers between devices, on_device(): lax.ppermute(obs_days, 'mod', shift_pairs(n_mod, s))  8.64 us
    ppermute x15, waiting for transfers between devices, lse_across(): lax.ppermute(local_lse, axis, shift_pairs(n, s))  8.13 us
    reduce_sum x4, other arithmetic, col_lse(): jnp.sum(jnp.exp(col_scores - col_peaks[None, :]), axis=0)  7.86 us
    ppermute x3, starting transfers between devices, on_device(): lax.ppermute(obs_days, 'mod', shift_pairs(n_mod, s))  6.14 us
  transfers between devices with their start and end apart: 22, of which 11 were waited for; matrix products, arithmetic and copies ran while one was open for 21% of the time, Pallas kernels for 0%

profile of v2, /device:TPU:0, one launch (start us, length us, event | category | flops | bytes accessed | tf_op | source)
XLA Modules:
  0.0 123.9 jit_solution(10912353199710587619)
XLA Ops:
  0.6 5.1 %collective-permute-start.2 = (f32[512,128]{1,0:T(8,128)}, f32[512,128]{1,0:T(8,128)S(1)}, u32[]{:S(2)}, u32[]{:S(2)}) collective-permute-start(f32[512,128]{1,0:T(8,128)} %param.5), channel_id=1, source_target_pairs={{0,12},{4,0},{8,4},{12,8},{1,13},{5,1},{9,5},{13,9},{2,14},{6,2},{... | collective-permute-start | bytes 786440 | tf_op jit(solution)/shard_map/ppermute | solution.py:163
  7.9 1.6 %multiply_reduce_fusion = f32[2048]{0:T(1024)S(1)} fusion(f32[2048,128]{1,0:T(8,128)} %param.4), kind=kLoop, calls=%fused_computation.37 | loop fusion | flops 522240 | bytes 1056768 | tf_op jit(solution)/shard_map/reduce_sum | solution.py:155
  9.5 3.9 %fusion.23 = (f32[2048]{0:T(1024)S(1)}, f32[2048,512]{1,0:T(8,128)S(1)}) fusion(f32[2048,128]{1,0:T(8,128)} %param.4, f32[512,128]{1,0:T(8,128)} %param.5, f32[512]{0:T(512)S(1)} %multiply_reduce_fusion.4, f32[2048]{0:T(1024)S(1)} %multiply_reduce_fusion), kind=kOutput, calls=%fused_computation.134 | convolution fusion | flops 812644352 | bytes 5523456 | tf_op jit(solution)/shard_map/dot_general | solution.py:96
  13.5 1.7 %exponential_reduce_fusion.15 = f32[2048]{0:T(1024)S(1)} fusion(f32[2048,512]{1,0:T(8,128)S(1)} %get-tuple-element.62.refs_1_, f32[2048]{0:T(1024)S(1)} %get-tuple-element.61), kind=kLoop, calls=%fused_computation.22 | loop fusion | flops 2095104 | bytes 4210688 | tf_op jit(solution)/shard_map/reduce_sum | solution.py:177
  15.4 2.6 %fusion.25 = (f32[2048]{0:T(1024)S(1)}, f32[2048,512]{1,0:T(8,128)S(1)}) fusion(f32[2048,128]{1,0:T(8,128)S(1)} %copy-done.8, f32[512,128]{1,0:T(8,128)S(1)} %collective-permute-done.2, f32[512]{0:T(512)S(1)} %multiply_reduce_fusion.1, f32[2048]{0:T(1024)S(1)} %multiply_reduce_fusion), kind=kOutput, calls=%fused_computation.136 | convolution fusion | flops 812644352 | bytes 5523456 | tf_op jit(solution)/shard_map/dot_general | solution.py:96
  17.9 1.7 %exponential_reduce_fusion.12 = f32[2048]{0:T(1024)S(1)} fusion(f32[2048,512]{1,0:T(8,128)S(1)} %get-tuple-element.66.refs_4_, f32[2048]{0:T(1024)S(1)} %get-tuple-element.65), kind=kLoop, calls=%fused_computation.16 | loop fusion | flops 2095104 | bytes 4210688 | tf_op jit(solution)/shard_map/reduce_sum | solution.py:177
  19.6 8.6 %collective-permute-done.1 = f32[512,128]{1,0:T(8,128)S(1)} collective-permute-done((f32[512,128]{1,0:T(8,128)}, f32[512,128]{1,0:T(8,128)S(1)}, u32[]{:S(2)}, u32[]{:S(2)}) %collective-permute-start.1) | collective-permute-done | bytes 262176 | tf_op jit(solution)/shard_map/ppermute | solution.py:163
  28.4 2.6 %fusion.24 = (f32[2048]{0:T(1024)S(1)}, f32[2048,512]{1,0:T(8,128)S(1)}) fusion(f32[2048,128]{1,0:T(8,128)S(1)} %copy-done.8, f32[512,128]{1,0:T(8,128)S(1)} %collective-permute-done.1, f32[512]{0:T(512)S(1)} %multiply_reduce_fusion.2, f32[2048]{0:T(1024)S(1)} %multiply_reduce_fusion), kind=kOutput, calls=%fused_computation.135 | convolution fusion | flops 812644352 | bytes 5523456 | tf_op jit(solution)/shard_map/dot_general | solution.py:96
  31.0 1.9 %exponential_reduce_fusion.13 = f32[2048]{0:T(1024)S(1)} fusion(f32[2048,512]{1,0:T(8,128)S(1)} %get-tuple-element.64.refs_3_, f32[2048]{0:T(1024)S(1)} %get-tuple-element.63), kind=kLoop, calls=%fused_computation.18 | loop fusion | flops 2095104 | bytes 4210688 | tf_op jit(solution)/shard_map/reduce_sum | solution.py:177
  33.0 2.6 %fusion.22 = (f32[2048]{0:T(1024)S(1)}, f32[2048,512]{1,0:T(8,128)S(1)}) fusion(f32[2048,128]{1,0:T(8,128)S(1)} %copy-done.8, f32[512,128]{1,0:T(8,128)S(1)} %collective-permute-done, f32[512]{0:T(512)S(1)} %multiply_reduce_fusion.3, f32[2048]{0:T(1024)S(1)} %multiply_reduce_fusion), kind=kOutput, calls=%fused_computation.133 | convolution fusion | flops 812644352 | bytes 5523456 | tf_op jit(solution)/shard_map/dot_general | solution.py:96
  35.6 1.7 %exponential_reduce_fusion.14 = f32[2048]{0:T(1024)S(1)} fusion(f32[2048,512]{1,0:T(8,128)S(1)} %get-tuple-element.60.refs_2_, f32[2048]{0:T(1024)S(1)} %get-tuple-element.59), kind=kLoop, calls=%fused_computation.20 | loop fusion | flops 2095104 | bytes 4210688 | tf_op jit(solution)/shard_map/reduce_sum | solution.py:177
  37.5 1.6 %collective-permute-start.4 = (f32[2048]{0:T(1024)S(1)}, f32[2048]{0:T(1024)S(1)}, u32[]{:S(2)}, u32[]{:S(2)}) collective-permute-start(f32[2048]{0:T(1024)S(1)} %get-tuple-element.56), channel_id=1, source_target_pairs={{0,2},{1,3},{2,0},{3,1},{4,6},{5,7},{6,4},{7,5},{8,10},{9,11},{10,... | collective-permute-start | bytes 24584 | tf_op jit(solution)/shard_map/ppermute | solution.py:109
  42.3 1.7 %exponential_reduce_fusion.11 = (f32[512]{0:T(512)S(1)}, f32[512]{0:T(512)S(1)}, f32[512]{0:T(512)S(1)}, f32[512]{0:T(512)S(1)}) fusion(f32[2048,512]{1,0:T(8,128)S(1)} %get-tuple-element.62.refs_1_, f32[512]{0:T(512)S(1)} %add_reduce_fusion.11, f32[2048]{0:T(1024)S(1)} %add_multiply_fusion.5, f32[2048,512]{1,0:T(8,128)S(1)} %get-tuple-element.60.refs_2_, ...), kind=kLoop, calls=%fused_computation.15 | loop fusion | flops 9435136 | bytes 16795648 | tf_op jit(solution)/shard_map/reduce_sum | solution.py:189
  44.0 2.3 %exponential_reduce_fusion.10 = (f32[512]{0:T(512)S(1)}, f32[512]{0:T(512)S(1)}, f32[512]{0:T(512)S(1)}) fusion(f32[2048,512]{1,0:T(8,128)S(1)} %get-tuple-element.60.refs_2_, f32[512]{0:T(512)S(1)} %get-tuple-element.18, f32[2048]{0:T(1024)S(1)} %add_multiply_fusion.5, f32[512]{0:T(512)S(1)} %get-tuple-element.20, ...), kind=kLoop, calls=%fused_computation.14 | loop fusion | flops 9435648 | bytes 12603392 | tf_op jit(solution)/shard_map/reduce_sum | solution.py:189
  47.5 3.3 %collective-permute-start.8 = (f32[2048]{0:T(1024)S(1)}, f32[2048]{0:T(1024)S(1)}, u32[]{:S(2)}, u32[]{:S(2)}) collective-permute-start(f32[2048]{0:T(1024)S(1)} %bitcast.121), channel_id=1, source_target_pairs={{0,12},{4,0},{8,4},{12,8},{1,13},{5,1},{9,5},{13,9},{2,14},{6,2},{... | collective-permute-start | bytes 24584 | tf_op jit(solution)/shard_map/ppermute | solution.py:109
  50.8 1.6 %collective-permute-done.6 = f32[2048]{0:T(1024)S(1)} collective-permute-done((f32[2048]{0:T(1024)S(1)}, f32[2048]{0:T(1024)S(1)}, u32[]{:S(2)}, u32[]{:S(2)}) %collective-permute-start.6) | collective-permute-done | bytes 8224 | tf_op jit(solution)/shard_map/ppermute | solution.py:109
  53.8 2.7 %add_reduce_fusion.4 = f32[2048]{0:T(1024)S(1)} fusion(f32[2048,512]{1,0:T(8,128)} %copy-done, f32[512]{0:T(512)S(1)} %bitcast.144), kind=kLoop, calls=%fused_computation.28 | loop fusion | flops 2095104 | bytes 4204544 | tf_op jit(solution)/shard_map/reduce_max | solution.py:176
  66.2 2.2 %collective-permute-done.10 = f32[2048]{0:T(1024)S(1)} collective-permute-done((f32[2048]{0:T(1024)S(1)}, f32[2048]{0:T(1024)S(1)}, u32[]{:S(2)}, u32[]{:S(2)}) %collective-permute-start.10) | collective-permute-done | bytes 8224 | tf_op jit(solution)/shard_map/ppermute | solution.py:109
  69.2 1.7 %exponential_reduce_fusion.3 = (f32[512]{0:T(512)S(1)}, f32[512]{0:T(512)S(1)}, f32[512]{0:T(512)S(1)}, f32[512]{0:T(512)S(1)}) fusion(f32[2048,512]{1,0:T(8,128)S(1)} %copy-done.7, f32[512]{0:T(512)S(1)} %add_reduce_fusion.3, f32[2048]{0:T(1024)S(1)} %add_multiply_fusion.3, f32[2048,512]{1,0:T(8,128)S(1)} %copy-done.5, f32[2048,512]{1,0:T(8,128)S(1)} %copy-done.3, ...), kind=kLoop, calls=%fused_computation.7 | loop fusion | flops 9435136 | bytes 16795648 | tf_op jit(solution)/shard_map/reduce_sum | solution.py:189
  70.9 2.2 %exponential_reduce_fusion.2 = (f32[512]{0:T(512)S(1)}, f32[512]{0:T(512)S(1)}, f32[512]{0:T(512)S(1)}) fusion(f32[2048,512]{1,0:T(8,128)S(1)} %copy-done.5, f32[512]{0:T(512)S(1)} %get-tuple-element.11, f32[2048]{0:T(1024)S(1)} %add_multiply_fusion.3, f32[512]{0:T(512)S(1)} %get-tuple-element.13, f32[2048,512]{1,0:T(8,128)S(1)} %copy-done.1, ...), kind=kLoop, calls=%fused_computation.6 | loop fusion | flops 9435648 | bytes 12603392 | tf_op jit(solution)/shard_map/reduce_sum | solution.py:189
  73.9 1.9 %collective-permute-start.12 = (f32[2048]{0:T(1024)S(1)}, f32[2048]{0:T(1024)S(1)}, u32[]{:S(2)}, u32[]{:S(2)}) collective-permute-start(f32[2048]{0:T(1024)S(1)} %bitcast.123), channel_id=1, source_target_pairs={{0,4},{4,8},{8,12},{12,0},{1,5},{5,9},{9,13},{13,1},{2,6},{6,10},{... | collective-permute-start | bytes 24584 | tf_op jit(solution)/shard_map/ppermute | solution.py:109
  75.8 1.9 %collective-permute-start.13 = (f32[2048]{0:T(1024)S(1)}, f32[2048]{0:T(1024)S(1)}, u32[]{:S(2)}, u32[]{:S(2)}) collective-permute-start(f32[2048]{0:T(1024)S(1)} %bitcast.124), channel_id=1, source_target_pairs={{0,8},{4,12},{8,0},{12,4},{1,9},{5,13},{9,1},{13,5},{2,10},{6,14},... | collective-permute-start | bytes 24584 | tf_op jit(solution)/shard_map/ppermute | solution.py:109
  83.4 21.3 %shard_map.49 = (f32[1,2048]{1,0:T(1,128)}, f32[1,2048]{1,0:T(1,128)}, f32[2048,128]{1,0:T(8,128)}) custom-call(f32[1,2048]{1,0:T(1,128)} %bitcast.118, f32[2048,512]{1,0:T(8,128)} %copy-done.6, f32[2048,512]{1,0:T(8,128)} %copy-done.4, f32[2048,512]{1,0:T(8,128)} %copy-done.2, f32[2048,512]{1,0:T(8,128)} %copy-done, f32[2048,128]{1,0:T(8,128)} %pad_maximum_fusion.refs_5_), custom_call_target="tpu_custom_call" | custom-call | tf_op jit(solution)/shard_map/pallas_call | solution.py:71
  117.7 5.2 %collective-permute-done.20 = f32[512,128]{1,0:T(8,128)S(1)} collective-permute-done((f32[512,128]{1,0:T(8,128)S(1)}, f32[512,128]{1,0:T(8,128)S(1)}, u32[]{:S(2)}, u32[]{:S(2)}) %collective-permute-start.20) | collective-permute-done | bytes 262176 | tf_op jit(solution)/shard_map/ppermute | solution.py:144
  (141 shorter events, 39.2 us)
Async XLA Ops:
  0.6 14.6 %collective-permute-start.2 = (f32[512,128]{1,0:T(8,128)}, f32[512,128]{1,0:T(8,128)S(1)}, u32[]{:S(2)}, u32[]{:S(2)}) collective-permute-start(f32[512,128]{1,0:T(8,128)} %param.5), channel_id=1, source_target_pairs={{0,12},{4,0},{8,4},{12,8},{1,13},{5,1},{9,5},{13,9},{2,14},{6,2},{... | collective-permute-start | bytes 786440 | tf_op jit(solution)/shard_map/ppermute | solution.py:163
  5.8 22.5 %collective-permute-start.1 = (f32[512,128]{1,0:T(8,128)}, f32[512,128]{1,0:T(8,128)S(1)}, u32[]{:S(2)}, u32[]{:S(2)}) collective-permute-start(f32[512,128]{1,0:T(8,128)} %param.5), channel_id=1, source_target_pairs={{0,8},{4,12},{8,0},{12,4},{1,9},{5,13},{9,1},{13,5},{2,10},{6,14},... | collective-permute-start | bytes 786440 | tf_op jit(solution)/shard_map/ppermute | solution.py:163
  5.8 27.1 %collective-permute-start = (f32[512,128]{1,0:T(8,128)}, f32[512,128]{1,0:T(8,128)S(1)}, u32[]{:S(2)}, u32[]{:S(2)}) collective-permute-start(f32[512,128]{1,0:T(8,128)} %param.5), channel_id=1, source_target_pairs={{0,4},{4,8},{8,12},{12,0},{1,5},{5,9},{9,13},{13,1},{2,6},{6,10},{... | collective-permute-start | bytes 786440 | tf_op jit(solution)/shard_map/ppermute | solution.py:163
  13.5 28.8 %copy-start.6 = (f32[2048,512]{1,0:T(8,128)}, f32[2048,512]{1,0:T(8,128)S(1)}, u32[]{:S(2)}) copy-start(f32[2048,512]{1,0:T(8,128)S(1)} %get-tuple-element.62.refs_1_) | copy-start | bytes 12582916
  17.9 26.0 %copy-start = (f32[2048,512]{1,0:T(8,128)}, f32[2048,512]{1,0:T(8,128)S(1)}, u32[]{:S(2)}) copy-start(f32[2048,512]{1,0:T(8,128)S(1)} %get-tuple-element.66.refs_4_) | copy-start | bytes 12582916
  37.4 3.1 %collective-permute-start.3 = (f32[2048]{0:T(1024)S(1)}, f32[2048]{0:T(1024)S(1)}, u32[]{:S(2)}, u32[]{:S(2)}) collective-permute-start(f32[2048]{0:T(1024)S(1)} %get-tuple-element.56), channel_id=1, source_target_pairs={{0,1},{1,2},{2,3},{3,0},{4,5},{5,6},{6,7},{7,4},{8,9},{9,10},{10,1... | collective-permute-start | bytes 24584 | tf_op jit(solution)/shard_map/ppermute | solution.py:109
  37.5 3.7 %collective-permute-start.4 = (f32[2048]{0:T(1024)S(1)}, f32[2048]{0:T(1024)S(1)}, u32[]{:S(2)}, u32[]{:S(2)}) collective-permute-start(f32[2048]{0:T(1024)S(1)} %get-tuple-element.56), channel_id=1, source_target_pairs={{0,2},{1,3},{2,0},{3,1},{4,6},{5,7},{6,4},{7,5},{8,10},{9,11},{10,... | collective-permute-start | bytes 24584 | tf_op jit(solution)/shard_map/ppermute | solution.py:109
  39.1 2.8 %collective-permute-start.5 = (f32[2048]{0:T(1024)S(1)}, f32[2048]{0:T(1024)S(1)}, u32[]{:S(2)}, u32[]{:S(2)}) collective-permute-start(f32[2048]{0:T(1024)S(1)} %get-tuple-element.56), channel_id=1, source_target_pairs={{0,3},{1,0},{2,1},{3,2},{4,7},{5,4},{6,5},{7,6},{8,11},{9,8},{10,9... | collective-permute-start | bytes 24584 | tf_op jit(solution)/shard_map/ppermute | solution.py:109
  47.0 5.5 %collective-permute-start.6 = (f32[2048]{0:T(1024)S(1)}, f32[2048]{0:T(1024)S(1)}, u32[]{:S(2)}, u32[]{:S(2)}) collective-permute-start(f32[2048]{0:T(1024)S(1)} %bitcast.119), channel_id=1, source_target_pairs={{0,4},{4,8},{8,12},{12,0},{1,5},{5,9},{9,13},{13,1},{2,6},{6,10},{... | collective-permute-start | bytes 24584 | tf_op jit(solution)/shard_map/ppermute | solution.py:109
  47.5 4.9 %collective-permute-start.7 = (f32[2048]{0:T(1024)S(1)}, f32[2048]{0:T(1024)S(1)}, u32[]{:S(2)}, u32[]{:S(2)}) collective-permute-start(f32[2048]{0:T(1024)S(1)} %bitcast.120), channel_id=1, source_target_pairs={{0,8},{4,12},{8,0},{12,4},{1,9},{5,13},{9,1},{13,5},{2,10},{6,14},... | collective-permute-start | bytes 24584 | tf_op jit(solution)/shard_map/ppermute | solution.py:109
  47.5 5.5 %collective-permute-start.8 = (f32[2048]{0:T(1024)S(1)}, f32[2048]{0:T(1024)S(1)}, u32[]{:S(2)}, u32[]{:S(2)}) collective-permute-start(f32[2048]{0:T(1024)S(1)} %bitcast.121), channel_id=1, source_target_pairs={{0,12},{4,0},{8,4},{12,8},{1,13},{5,1},{9,5},{13,9},{2,14},{6,2},{... | collective-permute-start | bytes 24584 | tf_op jit(solution)/shard_map/ppermute | solution.py:109
  64.6 3.7 %collective-permute-start.10 = (f32[2048]{0:T(1024)S(1)}, f32[2048]{0:T(1024)S(1)}, u32[]{:S(2)}, u32[]{:S(2)}) collective-permute-start(f32[2048]{0:T(1024)S(1)} %get-tuple-element.50), channel_id=1, source_target_pairs={{0,2},{1,3},{2,0},{3,1},{4,6},{5,7},{6,4},{7,5},{8,10},{9,11},{10,... | collective-permute-start | bytes 24584 | tf_op jit(solution)/shard_map/ppermute | solution.py:109
  65.6 2.7 %collective-permute-start.11 = (f32[2048]{0:T(1024)S(1)}, f32[2048]{0:T(1024)S(1)}, u32[]{:S(2)}, u32[]{:S(2)}) collective-permute-start(f32[2048]{0:T(1024)S(1)} %get-tuple-element.50), channel_id=1, source_target_pairs={{0,3},{1,0},{2,1},{3,2},{4,7},{5,4},{6,5},{7,6},{8,11},{9,8},{10,9... | collective-permute-start | bytes 24584 | tf_op jit(solution)/shard_map/ppermute | solution.py:109
  65.6 3.1 %collective-permute-start.9 = (f32[2048]{0:T(1024)S(1)}, f32[2048]{0:T(1024)S(1)}, u32[]{:S(2)}, u32[]{:S(2)}) collective-permute-start(f32[2048]{0:T(1024)S(1)} %get-tuple-element.50), channel_id=1, source_target_pairs={{0,1},{1,2},{2,3},{3,0},{4,5},{5,6},{6,7},{7,4},{8,9},{9,10},{10,1... | collective-permute-start | bytes 24584 | tf_op jit(solution)/shard_map/ppermute | solution.py:109
  73.9 5.5 %collective-permute-start.12 = (f32[2048]{0:T(1024)S(1)}, f32[2048]{0:T(1024)S(1)}, u32[]{:S(2)}, u32[]{:S(2)}) collective-permute-start(f32[2048]{0:T(1024)S(1)} %bitcast.123), channel_id=1, source_target_pairs={{0,4},{4,8},{8,12},{12,0},{1,5},{5,9},{9,13},{13,1},{2,6},{6,10},{... | collective-permute-start | bytes 24584 | tf_op jit(solution)/shard_map/ppermute | solution.py:109
  75.8 4.5 %collective-permute-start.13 = (f32[2048]{0:T(1024)S(1)}, f32[2048]{0:T(1024)S(1)}, u32[]{:S(2)}, u32[]{:S(2)}) collective-permute-start(f32[2048]{0:T(1024)S(1)} %bitcast.124), channel_id=1, source_target_pairs={{0,8},{4,12},{8,0},{12,4},{1,9},{5,13},{9,1},{13,5},{2,10},{6,14},... | collective-permute-start | bytes 24584 | tf_op jit(solution)/shard_map/ppermute | solution.py:109
  77.7 3.7 %collective-permute-start.14 = (f32[2048]{0:T(1024)S(1)}, f32[2048]{0:T(1024)S(1)}, u32[]{:S(2)}, u32[]{:S(2)}) collective-permute-start(f32[2048]{0:T(1024)S(1)} %bitcast.125), channel_id=1, source_target_pairs={{0,12},{4,0},{8,4},{12,8},{1,13},{5,1},{9,5},{13,9},{2,14},{6,2},{... | collective-permute-start | bytes 24584 | tf_op jit(solution)/shard_map/ppermute | solution.py:109
  104.8 7.2 %collective-permute-start.17 = (f32[2048]{0:T(1024)}, f32[2048]{0:T(1024)S(1)}, u32[]{:S(2)}, u32[]{:S(2)}) collective-permute-start(f32[2048]{0:T(1024)} %bitcast.86), channel_id=1, source_target_pairs={{0,1},{1,2},{2,3},{3,0},{4,5},{5,6},{6,7},{7,4},{8,9},{9,10},{10,1... | collective-permute-start | bytes 24584 | tf_op jit(solution)/shard_map/ppermute | solution.py:109
  104.8 7.2 %collective-permute-start.18 = (f32[2048]{0:T(1024)}, f32[2048]{0:T(1024)S(1)}, u32[]{:S(2)}, u32[]{:S(2)}) collective-permute-start(f32[2048]{0:T(1024)} %bitcast.87), channel_id=1, source_target_pairs={{0,2},{1,3},{2,0},{3,1},{4,6},{5,7},{6,4},{7,5},{8,10},{9,11},{10,... | collective-permute-start | bytes 24584 | tf_op jit(solution)/shard_map/ppermute | solution.py:109
  106.2 5.8 %collective-permute-start.19 = (f32[2048]{0:T(1024)}, f32[2048]{0:T(1024)S(1)}, u32[]{:S(2)}, u32[]{:S(2)}) collective-permute-start(f32[2048]{0:T(1024)} %bitcast.88), channel_id=1, source_target_pairs={{0,3},{1,0},{2,1},{3,2},{4,7},{5,4},{6,5},{7,6},{8,11},{9,8},{10,9... | collective-permute-start | bytes 24584 | tf_op jit(solution)/shard_map/ppermute | solution.py:109
  109.5 1.7 %collective-permute-start.15 = (f32[2,512]{1,0:T(2,128)S(1)}, f32[2,512]{1,0:T(2,128)S(1)}, u32[]{:S(2)}, u32[]{:S(2)}) collective-permute-start(f32[2,512]{1,0:T(2,128)S(1)} %bitcast.147), channel_id=1, source_target_pairs={{0,1},{1,0},{2,3},{3,2},{4,5},{5,4},{6,7},{7,6},{8,9},{9,8},{10,11... | collective-permute-start | bytes 12296 | tf_op jit(solution)/shard_map/ppermute | solution.py:135
  110.7 2.8 %collective-permute-start.16 = (f32[2,512,128]{2,1,0:T(8,128)S(1)}, f32[2,512,128]{2,1,0:T(8,128)S(1)}, u32[]{:S(2)}, u32[]{:S(2)}) collective-permute-start(f32[2,512,128]{2,1,0:T(8,128)S(1)} %dynamic-slice_bitcast_fusion), channel_id=1, source_target_pairs={{0,1},{1,0},{2,3},{3,2},{4,5},{5,4},{6,7},{7,6},{8,9},{9,8},{10,11... | collective-permute-start | bytes 1572872 | tf_op jit(solution)/shard_map/ppermute | solution.py:134
  111.3 6.4 %collective-permute-start.21 = (f32[512]{0:T(512)S(1)}, f32[512]{0:T(512)S(1)}, u32[]{:S(2)}, u32[]{:S(2)}) collective-permute-start(f32[512]{0:T(512)S(1)} %bitcast.148), channel_id=1, source_target_pairs={{0,2},{1,3},{2,0},{3,1},{4,6},{5,7},{6,4},{7,5},{8,10},{9,11},{10,... | collective-permute-start | bytes 6152 | tf_op jit(solution)/shard_map/ppermute | solution.py:145
  114.9 8.0 %collective-permute-start.20 = (f32[512,128]{1,0:T(8,128)S(1)}, f32[512,128]{1,0:T(8,128)S(1)}, u32[]{:S(2)}, u32[]{:S(2)}) collective-permute-start(f32[512,128]{1,0:T(8,128)S(1)} %dynamic-slice_bitcast_fusion.1), channel_id=1, source_target_pairs={{0,2},{1,3},{2,0},{3,1},{4,6},{5,7},{6,4},{7,5},{8,10},{9,11},{10,... | collective-permute-start | bytes 786440 | tf_op jit(solution)/shard_map/ppermute | solution.py:144
  (8 other events, 47.0 us)

commit v3 on v2

--- a/solution.py
+++ b/solution.py
@@ -117,7 +117,7 @@
     return jnp.take(vec.reshape(n, -1), order, axis=0).reshape(-1)
 
 
-def scatter_obs(partial, peaks, final_lse):
+def scatter_obs(partial, peaks, local):
     n = lax.axis_size("obs")
     half = n // 2
     o = lax.axis_index("obs")
@@ -135,6 +135,8 @@
     m_got = lax.ppermute(m_give, "obs", partner)
     top = jnp.maximum(m_keep, m_got)
     acc = keep * jnp.exp(m_keep - top)[..., None] + got * jnp.exp(m_got - top)[..., None]
+    acc, top, local = lax.optimization_barrier((acc, top, local))
+    final_lse = lse_across(local, "obs")
     pieces = [(lax.dynamic_index_in_dim(acc, x, axis=0, keepdims=False),
                lax.dynamic_index_in_dim(top, x, axis=0, keepdims=False))]
     for k in range(1, half):
@@ -148,7 +150,7 @@
     total = pieces[0][0] * jnp.exp(pieces[0][1] - own_lse)[:, None]
     for piece, piece_top in pieces[1:]:
         total = total + piece * jnp.exp(piece_top - own_lse)[:, None]
-    return total
+    return total, final_lse
 
 
 def on_device(model_days, obs_days):
@@ -197,9 +199,8 @@
         col_potential = -entropy_scale * (col_global - log_model)
         col_shift = reorder(col_potential, order)
     peaks, local, partial_map = final_local(col_shift / entropy_scale, base_blocks, gathered)
-    final_lse = lse_across(local, "obs")
+    mapped, final_lse = scatter_obs(partial_map, peaks, local)
     row_potential = -entropy_scale * (final_lse - log_obs)
-    mapped = scatter_obs(partial_map, peaks, final_lse)
     return (mapped, row_potential, col_potential)
 
 

time: 124 us -> 123 us (level)
  transfers between devices with their start and end apart: 22 -> 22, of which waited for: 11 -> 12; matrix products, arithmetic and copies ran while one was open for 21% -> 18% of each run, Pallas kernels for 0% -> 0%
where the time goes in v3:
time: 123 us
  other arithmetic  36.2 us (29%)
  starting transfers between devices  24.5 us (20%)
  waiting for transfers between devices  21.8 us (18%)
  Pallas kernels  21.3 us (17%)
  matrix products  11.6 us (9%)
  local copies, waits for them, and re-layouts  6.4 us (5%)
    pallas_call x1, Pallas kernels, final_local(): pl.pallas_call(_final_kernel, grid=(R // tr,), in_specs=[pl.BlockSpec((1,...  21.3 us
    ppermute x15, starting transfers between devices, lse_across(): lax.ppermute(local_lse, axis, shift_pairs(n, s))  15.6 us
    reduce_sum x8, other arithmetic, row_lse(): jnp.sum(jnp.exp(scores - peaks[:, None]), axis=1)  12.2 us
    dot_general x4, matrix products, pair_scores(): lax.dot_general(block_rows, columns, (((1,), (1,)), ((), ())), precision=...  11.6 us
    ppermute x3, waiting for transfers between devices, on_device(): lax.ppermute(obs_days, 'mod', shift_pairs(n_mod, s))  8.64 us
    ppermute x15, waiting for transfers between devices, lse_across(): lax.ppermute(local_lse, axis, shift_pairs(n, s))  8.13 us
    reduce_sum x4, other arithmetic, col_lse(): jnp.sum(jnp.exp(col_scores - col_peaks[None, :]), axis=0)  7.86 us
    ppermute x3, starting transfers between devices, on_device(): lax.ppermute(obs_days, 'mod', shift_pairs(n_mod, s))  6.14 us
  transfers between devices with their start and end apart: 22, of which 12 were waited for; matrix products, arithmetic and copies ran while one was open for 18% of the time, Pallas kernels for 0%

profile of v3, /device:TPU:0, one launch (start us, length us, event | category | flops | bytes accessed | tf_op | source)
XLA Modules:
  0.0 122.9 jit_solution(17592267585816609389)
XLA Ops:
  0.6 5.1 %collective-permute-start.2 = (f32[512,128]{1,0:T(8,128)}, f32[512,128]{1,0:T(8,128)S(1)}, u32[]{:S(2)}, u32[]{:S(2)}) collective-permute-start(f32[512,128]{1,0:T(8,128)} %param.5), channel_id=1, source_target_pairs={{0,12},{4,0},{8,4},{12,8},{1,13},{5,1},{9,5},{13,9},{2,14},{6,2},{... | collective-permute-start | bytes 786440 | tf_op jit(solution)/shard_map/ppermute | solution.py:165
  7.9 1.6 %multiply_reduce_fusion = f32[2048]{0:T(1024)S(1)} fusion(f32[2048,128]{1,0:T(8,128)} %param.4), kind=kLoop, calls=%fused_computation.37 | loop fusion | flops 522240 | bytes 1056768 | tf_op jit(solution)/shard_map/reduce_sum | solution.py:157
  9.5 3.9 %fusion.23 = (f32[2048]{0:T(1024)S(1)}, f32[2048,512]{1,0:T(8,128)S(1)}) fusion(f32[2048,128]{1,0:T(8,128)} %param.4, f32[512,128]{1,0:T(8,128)} %param.5, f32[512]{0:T(512)S(1)} %multiply_reduce_fusion.4, f32[2048]{0:T(1024)S(1)} %multiply_reduce_fusion), kind=kOutput, calls=%fused_computation.134 | convolution fusion | flops 812644352 | bytes 5523456 | tf_op jit(solution)/shard_map/dot_general | solution.py:96
  13.5 1.7 %exponential_reduce_fusion.15 = f32[2048]{0:T(1024)S(1)} fusion(f32[2048,512]{1,0:T(8,128)S(1)} %get-tuple-element.68.refs_1_, f32[2048]{0:T(1024)S(1)} %get-tuple-element.67), kind=kLoop, calls=%fused_computation.22 | loop fusion | flops 2095104 | bytes 4210688 | tf_op jit(solution)/shard_map/reduce_sum | solution.py:179
  15.4 2.6 %fusion.25 = (f32[2048]{0:T(1024)S(1)}, f32[2048,512]{1,0:T(8,128)S(1)}) fusion(f32[2048,128]{1,0:T(8,128)S(1)} %copy-done.8, f32[512,128]{1,0:T(8,128)S(1)} %collective-permute-done.2, f32[512]{0:T(512)S(1)} %multiply_reduce_fusion.1, f32[2048]{0:T(1024)S(1)} %multiply_reduce_fusion), kind=kOutput, calls=%fused_computation.136 | convolution fusion | flops 812644352 | bytes 5523456 | tf_op jit(solution)/shard_map/dot_general | solution.py:96
  17.9 1.7 %exponential_reduce_fusion.12 = f32[2048]{0:T(1024)S(1)} fusion(f32[2048,512]{1,0:T(8,128)S(1)} %get-tuple-element.72.refs_4_, f32[2048]{0:T(1024)S(1)} %get-tuple-element.71), kind=kLoop, calls=%fused_computation.16 | loop fusion | flops 2095104 | bytes 4210688 | tf_op jit(solution)/shard_map/reduce_sum | solution.py:179
  19.6 8.6 %collective-permute-done.1 = f32[512,128]{1,0:T(8,128)S(1)} collective-permute-done((f32[512,128]{1,0:T(8,128)}, f32[512,128]{1,0:T(8,128)S(1)}, u32[]{:S(2)}, u32[]{:S(2)}) %collective-permute-start.1) | collective-permute-done | bytes 262176 | tf_op jit(solution)/shard_map/ppermute | solution.py:165
  28.4 2.6 %fusion.24 = (f32[2048]{0:T(1024)S(1)}, f32[2048,512]{1,0:T(8,128)S(1)}) fusion(f32[2048,128]{1,0:T(8,128)S(1)} %copy-done.8, f32[512,128]{1,0:T(8,128)S(1)} %collective-permute-done.1, f32[512]{0:T(512)S(1)} %multiply_reduce_fusion.2, f32[2048]{0:T(1024)S(1)} %multiply_reduce_fusion), kind=kOutput, calls=%fused_computation.135 | convolution fusion | flops 812644352 | bytes 5523456 | tf_op jit(solution)/shard_map/dot_general | solution.py:96
  31.0 1.9 %exponential_reduce_fusion.13 = f32[2048]{0:T(1024)S(1)} fusion(f32[2048,512]{1,0:T(8,128)S(1)} %get-tuple-element.70.refs_3_, f32[2048]{0:T(1024)S(1)} %get-tuple-element.69), kind=kLoop, calls=%fused_computation.18 | loop fusion | flops 2095104 | bytes 4210688 | tf_op jit(solution)/shard_map/reduce_sum | solution.py:179
  33.0 2.6 %fusion.22 = (f32[2048]{0:T(1024)S(1)}, f32[2048,512]{1,0:T(8,128)S(1)}) fusion(f32[2048,128]{1,0:T(8,128)S(1)} %copy-done.8, f32[512,128]{1,0:T(8,128)S(1)} %collective-permute-done, f32[512]{0:T(512)S(1)} %multiply_reduce_fusion.3, f32[2048]{0:T(1024)S(1)} %multiply_reduce_fusion), kind=kOutput, calls=%fused_computation.133 | convolution fusion | flops 812644352 | bytes 5523456 | tf_op jit(solution)/shard_map/dot_general | solution.py:96
  35.6 1.7 %exponential_reduce_fusion.14 = f32[2048]{0:T(1024)S(1)} fusion(f32[2048,512]{1,0:T(8,128)S(1)} %get-tuple-element.66.refs_2_, f32[2048]{0:T(1024)S(1)} %get-tuple-element.65), kind=kLoop, calls=%fused_computation.20 | loop fusion | flops 2095104 | bytes 4210688 | tf_op jit(solution)/shard_map/reduce_sum | solution.py:179
  37.5 1.6 %collective-permute-start.4 = (f32[2048]{0:T(1024)S(1)}, f32[2048]{0:T(1024)S(1)}, u32[]{:S(2)}, u32[]{:S(2)}) collective-permute-start(f32[2048]{0:T(1024)S(1)} %get-tuple-element.62), channel_id=1, source_target_pairs={{0,2},{1,3},{2,0},{3,1},{4,6},{5,7},{6,4},{7,5},{8,10},{9,11},{10,... | collective-permute-start | bytes 24584 | tf_op jit(solution)/shard_map/ppermute | solution.py:109
  42.3 1.7 %exponential_reduce_fusion.11 = (f32[512]{0:T(512)S(1)}, f32[512]{0:T(512)S(1)}, f32[512]{0:T(512)S(1)}, f32[512]{0:T(512)S(1)}) fusion(f32[2048,512]{1,0:T(8,128)S(1)} %get-tuple-element.68.refs_1_, f32[512]{0:T(512)S(1)} %add_reduce_fusion.11, f32[2048]{0:T(1024)S(1)} %add_multiply_fusion.5, f32[2048,512]{1,0:T(8,128)S(1)} %get-tuple-element.66.refs_2_, ...), kind=kLoop, calls=%fused_computation.15 | loop fusion | flops 9435136 | bytes 16795648 | tf_op jit(solution)/shard_map/reduce_sum | solution.py:191
  44.0 2.3 %exponential_reduce_fusion.10 = (f32[512]{0:T(512)S(1)}, f32[512]{0:T(512)S(1)}, f32[512]{0:T(512)S(1)}) fusion(f32[2048,512]{1,0:T(8,128)S(1)} %get-tuple-element.66.refs_2_, f32[512]{0:T(512)S(1)} %get-tuple-element.24, f32[2048]{0:T(1024)S(1)} %add_multiply_fusion.5, f32[512]{0:T(512)S(1)} %get-tuple-element.26, ...), kind=kLoop, calls=%fused_computation.14 | loop fusion | flops 9435648 | bytes 12603392 | tf_op jit(solution)/shard_map/reduce_sum | solution.py:191
  47.5 3.3 %collective-permute-start.8 = (f32[2048]{0:T(1024)S(1)}, f32[2048]{0:T(1024)S(1)}, u32[]{:S(2)}, u32[]{:S(2)}) collective-permute-start(f32[2048]{0:T(1024)S(1)} %bitcast.111), channel_id=1, source_target_pairs={{0,12},{4,0},{8,4},{12,8},{1,13},{5,1},{9,5},{13,9},{2,14},{6,2},{... | collective-permute-start | bytes 24584 | tf_op jit(solution)/shard_map/ppermute | solution.py:109
  50.8 1.6 %collective-permute-done.6 = f32[2048]{0:T(1024)S(1)} collective-permute-done((f32[2048]{0:T(1024)S(1)}, f32[2048]{0:T(1024)S(1)}, u32[]{:S(2)}, u32[]{:S(2)}) %collective-permute-start.6) | collective-permute-done | bytes 8224 | tf_op jit(solution)/shard_map/ppermute | solution.py:109
  53.8 2.7 %add_reduce_fusion.4 = f32[2048]{0:T(1024)S(1)} fusion(f32[2048,512]{1,0:T(8,128)} %copy-done, f32[512]{0:T(512)S(1)} %bitcast.140), kind=kLoop, calls=%fused_computation.28 | loop fusion | flops 2095104 | bytes 4204544 | tf_op jit(solution)/shard_map/reduce_max | solution.py:178
  66.2 2.2 %collective-permute-done.10 = f32[2048]{0:T(1024)S(1)} collective-permute-done((f32[2048]{0:T(1024)S(1)}, f32[2048]{0:T(1024)S(1)}, u32[]{:S(2)}, u32[]{:S(2)}) %collective-permute-start.10) | collective-permute-done | bytes 8224 | tf_op jit(solution)/shard_map/ppermute | solution.py:109
  69.2 1.7 %exponential_reduce_fusion.3 = (f32[512]{0:T(512)S(1)}, f32[512]{0:T(512)S(1)}, f32[512]{0:T(512)S(1)}, f32[512]{0:T(512)S(1)}) fusion(f32[2048,512]{1,0:T(8,128)S(1)} %copy-done.7, f32[512]{0:T(512)S(1)} %add_reduce_fusion.3, f32[2048]{0:T(1024)S(1)} %add_multiply_fusion.3, f32[2048,512]{1,0:T(8,128)S(1)} %copy-done.5, f32[2048,512]{1,0:T(8,128)S(1)} %copy-done.3, ...), kind=kLoop, calls=%fused_computation.7 | loop fusion | flops 9435136 | bytes 16795648 | tf_op jit(solution)/shard_map/reduce_sum | solution.py:191
  70.9 2.2 %exponential_reduce_fusion.2 = (f32[512]{0:T(512)S(1)}, f32[512]{0:T(512)S(1)}, f32[512]{0:T(512)S(1)}) fusion(f32[2048,512]{1,0:T(8,128)S(1)} %copy-done.5, f32[512]{0:T(512)S(1)} %get-tuple-element.17, f32[2048]{0:T(1024)S(1)} %add_multiply_fusion.3, f32[512]{0:T(512)S(1)} %get-tuple-element.19, f32[2048,512]{1,0:T(8,128)S(1)} %copy-done.1, ...), kind=kLoop, calls=%fused_computation.6 | loop fusion | flops 9435648 | bytes 12603392 | tf_op jit(solution)/shard_map/reduce_sum | solution.py:191
  73.9 1.9 %collective-permute-start.12 = (f32[2048]{0:T(1024)S(1)}, f32[2048]{0:T(1024)S(1)}, u32[]{:S(2)}, u32[]{:S(2)}) collective-permute-start(f32[2048]{0:T(1024)S(1)} %bitcast.113), channel_id=1, source_target_pairs={{0,4},{4,8},{8,12},{12,0},{1,5},{5,9},{9,13},{13,1},{2,6},{6,10},{... | collective-permute-start | bytes 24584 | tf_op jit(solution)/shard_map/ppermute | solution.py:109
  75.8 1.9 %collective-permute-start.13 = (f32[2048]{0:T(1024)S(1)}, f32[2048]{0:T(1024)S(1)}, u32[]{:S(2)}, u32[]{:S(2)}) collective-permute-start(f32[2048]{0:T(1024)S(1)} %bitcast.114), channel_id=1, source_target_pairs={{0,8},{4,12},{8,0},{12,4},{1,9},{5,13},{9,1},{13,5},{2,10},{6,14},... | collective-permute-start | bytes 24584 | tf_op jit(solution)/shard_map/ppermute | solution.py:109
  83.4 21.3 %shard_map.49 = (f32[1,2048]{1,0:T(1,128)}, f32[1,2048]{1,0:T(1,128)}, f32[2048,128]{1,0:T(8,128)}) custom-call(f32[1,2048]{1,0:T(1,128)} %bitcast.108, f32[2048,512]{1,0:T(8,128)} %copy-done.6, f32[2048,512]{1,0:T(8,128)} %copy-done.4, f32[2048,512]{1,0:T(8,128)} %copy-done.2, f32[2048,512]{1,0:T(8,128)} %copy-done, f32[2048,128]{1,0:T(8,128)} %pad_maximum_fusion.refs_5_), custom_call_target="tpu_custom_call" | custom-call | tf_op jit(solution)/shard_map/pallas_call | solution.py:71
  117.9 4.2 %collective-permute-done.20 = f32[512,128]{1,0:T(8,128)S(1)} collective-permute-done((f32[512,128]{1,0:T(8,128)S(1)}, f32[512,128]{1,0:T(8,128)S(1)}, u32[]{:S(2)}, u32[]{:S(2)}) %collective-permute-start.20) | collective-permute-done | bytes 262176 | tf_op jit(solution)/shard_map/ppermute | solution.py:146
  (141 shorter events, 39.3 us)
Async XLA Ops:
  0.6 14.6 %collective-permute-start.2 = (f32[512,128]{1,0:T(8,128)}, f32[512,128]{1,0:T(8,128)S(1)}, u32[]{:S(2)}, u32[]{:S(2)}) collective-permute-start(f32[512,128]{1,0:T(8,128)} %param.5), channel_id=1, source_target_pairs={{0,12},{4,0},{8,4},{12,8},{1,13},{5,1},{9,5},{13,9},{2,14},{6,2},{... | collective-permute-start | bytes 786440 | tf_op jit(solution)/shard_map/ppermute | solution.py:165
  5.8 22.5 %collective-permute-start.1 = (f32[512,128]{1,0:T(8,128)}, f32[512,128]{1,0:T(8,128)S(1)}, u32[]{:S(2)}, u32[]{:S(2)}) collective-permute-start(f32[512,128]{1,0:T(8,128)} %param.5), channel_id=1, source_target_pairs={{0,8},{4,12},{8,0},{12,4},{1,9},{5,13},{9,1},{13,5},{2,10},{6,14},... | collective-permute-start | bytes 786440 | tf_op jit(solution)/shard_map/ppermute | solution.py:165
  5.8 27.1 %collective-permute-start = (f32[512,128]{1,0:T(8,128)}, f32[512,128]{1,0:T(8,128)S(1)}, u32[]{:S(2)}, u32[]{:S(2)}) collective-permute-start(f32[512,128]{1,0:T(8,128)} %param.5), channel_id=1, source_target_pairs={{0,4},{4,8},{8,12},{12,0},{1,5},{5,9},{9,13},{13,1},{2,6},{6,10},{... | collective-permute-start | bytes 786440 | tf_op jit(solution)/shard_map/ppermute | solution.py:165
  13.5 28.8 %copy-start.6 = (f32[2048,512]{1,0:T(8,128)}, f32[2048,512]{1,0:T(8,128)S(1)}, u32[]{:S(2)}) copy-start(f32[2048,512]{1,0:T(8,128)S(1)} %get-tuple-element.68.refs_1_) | copy-start | bytes 12582916
  17.9 26.0 %copy-start = (f32[2048,512]{1,0:T(8,128)}, f32[2048,512]{1,0:T(8,128)S(1)}, u32[]{:S(2)}) copy-start(f32[2048,512]{1,0:T(8,128)S(1)} %get-tuple-element.72.refs_4_) | copy-start | bytes 12582916
  37.4 3.1 %collective-permute-start.3 = (f32[2048]{0:T(1024)S(1)}, f32[2048]{0:T(1024)S(1)}, u32[]{:S(2)}, u32[]{:S(2)}) collective-permute-start(f32[2048]{0:T(1024)S(1)} %get-tuple-element.62), channel_id=1, source_target_pairs={{0,1},{1,2},{2,3},{3,0},{4,5},{5,6},{6,7},{7,4},{8,9},{9,10},{10,1... | collective-permute-start | bytes 24584 | tf_op jit(solution)/shard_map/ppermute | solution.py:109
  37.5 3.7 %collective-permute-start.4 = (f32[2048]{0:T(1024)S(1)}, f32[2048]{0:T(1024)S(1)}, u32[]{:S(2)}, u32[]{:S(2)}) collective-permute-start(f32[2048]{0:T(1024)S(1)} %get-tuple-element.62), channel_id=1, source_target_pairs={{0,2},{1,3},{2,0},{3,1},{4,6},{5,7},{6,4},{7,5},{8,10},{9,11},{10,... | collective-permute-start | bytes 24584 | tf_op jit(solution)/shard_map/ppermute | solution.py:109
  39.1 2.8 %collective-permute-start.5 = (f32[2048]{0:T(1024)S(1)}, f32[2048]{0:T(1024)S(1)}, u32[]{:S(2)}, u32[]{:S(2)}) collective-permute-start(f32[2048]{0:T(1024)S(1)} %get-tuple-element.62), channel_id=1, source_target_pairs={{0,3},{1,0},{2,1},{3,2},{4,7},{5,4},{6,5},{7,6},{8,11},{9,8},{10,9... | collective-permute-start | bytes 24584 | tf_op jit(solution)/shard_map/ppermute | solution.py:109
  47.0 5.5 %collective-permute-start.6 = (f32[2048]{0:T(1024)S(1)}, f32[2048]{0:T(1024)S(1)}, u32[]{:S(2)}, u32[]{:S(2)}) collective-permute-start(f32[2048]{0:T(1024)S(1)} %bitcast.109), channel_id=1, source_target_pairs={{0,4},{4,8},{8,12},{12,0},{1,5},{5,9},{9,13},{13,1},{2,6},{6,10},{... | collective-permute-start | bytes 24584 | tf_op jit(solution)/shard_map/ppermute | solution.py:109
  47.5 4.9 %collective-permute-start.7 = (f32[2048]{0:T(1024)S(1)}, f32[2048]{0:T(1024)S(1)}, u32[]{:S(2)}, u32[]{:S(2)}) collective-permute-start(f32[2048]{0:T(1024)S(1)} %bitcast.110), channel_id=1, source_target_pairs={{0,8},{4,12},{8,0},{12,4},{1,9},{5,13},{9,1},{13,5},{2,10},{6,14},... | collective-permute-start | bytes 24584 | tf_op jit(solution)/shard_map/ppermute | solution.py:109
  47.5 5.5 %collective-permute-start.8 = (f32[2048]{0:T(1024)S(1)}, f32[2048]{0:T(1024)S(1)}, u32[]{:S(2)}, u32[]{:S(2)}) collective-permute-start(f32[2048]{0:T(1024)S(1)} %bitcast.111), channel_id=1, source_target_pairs={{0,12},{4,0},{8,4},{12,8},{1,13},{5,1},{9,5},{13,9},{2,14},{6,2},{... | collective-permute-start | bytes 24584 | tf_op jit(solution)/shard_map/ppermute | solution.py:109
  64.6 3.7 %collective-permute-start.10 = (f32[2048]{0:T(1024)S(1)}, f32[2048]{0:T(1024)S(1)}, u32[]{:S(2)}, u32[]{:S(2)}) collective-permute-start(f32[2048]{0:T(1024)S(1)} %get-tuple-element.56), channel_id=1, source_target_pairs={{0,2},{1,3},{2,0},{3,1},{4,6},{5,7},{6,4},{7,5},{8,10},{9,11},{10,... | collective-permute-start | bytes 24584 | tf_op jit(solution)/shard_map/ppermute | solution.py:109
  65.6 2.7 %collective-permute-start.11 = (f32[2048]{0:T(1024)S(1)}, f32[2048]{0:T(1024)S(1)}, u32[]{:S(2)}, u32[]{:S(2)}) collective-permute-start(f32[2048]{0:T(1024)S(1)} %get-tuple-element.56), channel_id=1, source_target_pairs={{0,3},{1,0},{2,1},{3,2},{4,7},{5,4},{6,5},{7,6},{8,11},{9,8},{10,9... | collective-permute-start | bytes 24584 | tf_op jit(solution)/shard_map/ppermute | solution.py:109
  65.6 3.1 %collective-permute-start.9 = (f32[2048]{0:T(1024)S(1)}, f32[2048]{0:T(1024)S(1)}, u32[]{:S(2)}, u32[]{:S(2)}) collective-permute-start(f32[2048]{0:T(1024)S(1)} %get-tuple-element.56), channel_id=1, source_target_pairs={{0,1},{1,2},{2,3},{3,0},{4,5},{5,6},{6,7},{7,4},{8,9},{9,10},{10,1... | collective-permute-start | bytes 24584 | tf_op jit(solution)/shard_map/ppermute | solution.py:109
  73.9 5.5 %collective-permute-start.12 = (f32[2048]{0:T(1024)S(1)}, f32[2048]{0:T(1024)S(1)}, u32[]{:S(2)}, u32[]{:S(2)}) collective-permute-start(f32[2048]{0:T(1024)S(1)} %bitcast.113), channel_id=1, source_target_pairs={{0,4},{4,8},{8,12},{12,0},{1,5},{5,9},{9,13},{13,1},{2,6},{6,10},{... | collective-permute-start | bytes 24584 | tf_op jit(solution)/shard_map/ppermute | solution.py:109
  75.8 4.5 %collective-permute-start.13 = (f32[2048]{0:T(1024)S(1)}, f32[2048]{0:T(1024)S(1)}, u32[]{:S(2)}, u32[]{:S(2)}) collective-permute-start(f32[2048]{0:T(1024)S(1)} %bitcast.114), channel_id=1, source_target_pairs={{0,8},{4,12},{8,0},{12,4},{1,9},{5,13},{9,1},{13,5},{2,10},{6,14},... | collective-permute-start | bytes 24584 | tf_op jit(solution)/shard_map/ppermute | solution.py:109
  77.7 3.7 %collective-permute-start.14 = (f32[2048]{0:T(1024)S(1)}, f32[2048]{0:T(1024)S(1)}, u32[]{:S(2)}, u32[]{:S(2)}) collective-permute-start(f32[2048]{0:T(1024)S(1)} %bitcast.115), channel_id=1, source_target_pairs={{0,12},{4,0},{8,4},{12,8},{1,13},{5,1},{9,5},{13,9},{2,14},{6,2},{... | collective-permute-start | bytes 24584 | tf_op jit(solution)/shard_map/ppermute | solution.py:109
  105.8 3.4 %collective-permute-start.16 = (f32[2,512,128]{2,1,0:T(8,128)S(1)}, f32[2,512,128]{2,1,0:T(8,128)S(1)}, u32[]{:S(2)}, u32[]{:S(2)}) collective-permute-start(f32[2,512,128]{2,1,0:T(8,128)S(1)} %dynamic-slice_bitcast_fusion), channel_id=1, source_target_pairs={{0,1},{1,0},{2,3},{3,2},{4,5},{5,4},{6,7},{7,6},{8,9},{9,8},{10,11... | collective-permute-start | bytes 1572872 | tf_op jit(solution)/shard_map/ppermute | solution.py:134
  107.8 1.4 %collective-permute-start.15 = (f32[2,512]{1,0:T(2,128)S(1)}, f32[2,512]{1,0:T(2,128)S(1)}, u32[]{:S(2)}, u32[]{:S(2)}) collective-permute-start(f32[2,512]{1,0:T(2,128)S(1)} %bitcast.143), channel_id=1, source_target_pairs={{0,1},{1,0},{2,3},{3,2},{4,5},{5,4},{6,7},{7,6},{8,9},{9,8},{10,11... | collective-permute-start | bytes 12296 | tf_op jit(solution)/shard_map/ppermute | solution.py:135
  110.6 5.1 %collective-permute-start.17 = (f32[2048]{0:T(1024)}, f32[2048]{0:T(1024)S(1)}, u32[]{:S(2)}, u32[]{:S(2)}) collective-permute-start(f32[2048]{0:T(1024)} %bitcast.117), channel_id=1, source_target_pairs={{0,1},{1,2},{2,3},{3,0},{4,5},{5,6},{6,7},{7,4},{8,9},{9,10},{10,1... | collective-permute-start | bytes 24584 | tf_op jit(solution)/shard_map/ppermute | solution.py:109
  111.0 4.7 %collective-permute-start.18 = (f32[2048]{0:T(1024)}, f32[2048]{0:T(1024)S(1)}, u32[]{:S(2)}, u32[]{:S(2)}) collective-permute-start(f32[2048]{0:T(1024)} %bitcast.118), channel_id=1, source_target_pairs={{0,2},{1,3},{2,0},{3,1},{4,6},{5,7},{6,4},{7,5},{8,10},{9,11},{10,... | collective-permute-start | bytes 24584 | tf_op jit(solution)/shard_map/ppermute | solution.py:109
  112.4 3.3 %collective-permute-start.19 = (f32[2048]{0:T(1024)}, f32[2048]{0:T(1024)S(1)}, u32[]{:S(2)}, u32[]{:S(2)}) collective-permute-start(f32[2048]{0:T(1024)} %bitcast.119), channel_id=1, source_target_pairs={{0,3},{1,0},{2,1},{3,2},{4,7},{5,4},{6,5},{7,6},{8,11},{9,8},{10,9... | collective-permute-start | bytes 24584 | tf_op jit(solution)/shard_map/ppermute | solution.py:109
  113.5 4.3 %collective-permute-start.21 = (f32[512]{0:T(512)S(1)}, f32[512]{0:T(512)S(1)}, u32[]{:S(2)}, u32[]{:S(2)}) collective-permute-start(f32[512]{0:T(512)S(1)} %bitcast.144), channel_id=1, source_target_pairs={{0,2},{1,3},{2,0},{3,1},{4,6},{5,7},{6,4},{7,5},{8,10},{9,11},{10,... | collective-permute-start | bytes 6152 | tf_op jit(solution)/shard_map/ppermute | solution.py:147
  114.3 7.7 %collective-permute-start.20 = (f32[512,128]{1,0:T(8,128)S(1)}, f32[512,128]{1,0:T(8,128)S(1)}, u32[]{:S(2)}, u32[]{:S(2)}) collective-permute-start(f32[512,128]{1,0:T(8,128)S(1)} %dynamic-slice_bitcast_fusion.1), channel_id=1, source_target_pairs={{0,2},{1,3},{2,0},{3,1},{4,6},{5,7},{6,4},{7,5},{8,10},{9,11},{10,... | collective-permute-start | bytes 786440 | tf_op jit(solution)/shard_map/ppermute | solution.py:146
  (8 other events, 47.0 us)

commit v4 on v3

--- a/solution.py
+++ b/solution.py
@@ -35,7 +35,7 @@
             m = jnp.maximum(m, t)
         m_scr[pl.ds(r, RB), :] = m
         return carry
-    lax.fori_loop(0, tr // RB, p1, 0, unroll=4)
+    lax.fori_loop(0, tr // RB, p1, 0, unroll=8)
     r_scr[...] = jnp.max(m_scr[...], axis=1, keepdims=True)
     m_ref[...] = jnp.max(m_scr[...].T, axis=0, keepdims=True)
 
@@ -50,7 +50,7 @@
                 t = u if t is None else t + u
         t_scr[pl.ds(r, RB), :] = t
         return carry
-    lax.fori_loop(0, tr // RB, p2, 0, unroll=4)
+    lax.fori_loop(0, tr // RB, p2, 0, unroll=8)
     l_ref[...] = m_ref[...] + jnp.log(jnp.sum(t_scr[...].T, axis=0, keepdims=True))
     w = w_ref[...]
     wh = w.astype(jnp.bfloat16)

time: 123 us -> 120 us (0.976)
  Pallas kernels: 21.3 us -> 18.2 us
    pallas_call x1, Pallas kernels: 21.3 us -> 18.2 us  [final_local(): pl.pallas_call(_final_kernel, grid=(R // tr,), in_specs=[pl.BlockSpec((1,...]
  transfers between devices with their start and end apart: 22 -> 22, of which waited for: 12 -> 12; matrix products, arithmetic and copies ran while one was open for 18% -> 19% of each run, Pallas kernels for 0% -> 0%
where the time goes in v4:
time: 120 us
  other arithmetic  36.2 us (30%)
  starting transfers between devices  24.5 us (20%)
  waiting for transfers between devices  21.8 us (18%)
  Pallas kernels  18.2 us (15%)
  matrix products  11.6 us (10%)
  local copies, waits for them, and re-layouts  6.4 us (5%)
    pallas_call x1, Pallas kernels, final_local(): pl.pallas_call(_final_kernel, grid=(R // tr,), in_specs=[pl.BlockSpec((1,...  18.2 us
    ppermute x15, starting transfers between devices, lse_across(): lax.ppermute(local_lse, axis, shift_pairs(n, s))  15.6 us
    reduce_sum x8, other arithmetic, row_lse(): jnp.sum(jnp.exp(scores - peaks[:, None]), axis=1)  12.2 us
    dot_general x4, matrix products, pair_scores(): lax.dot_general(block_rows, columns, (((1,), (1,)), ((), ())), precision=...  11.6 us
    ppermute x3, waiting for transfers between devices, on_device(): lax.ppermute(obs_days, 'mod', shift_pairs(n_mod, s))  8.64 us
    ppermute x15, waiting for transfers between devices, lse_across(): lax.ppermute(local_lse, axis, shift_pairs(n, s))  8.13 us
    reduce_sum x4, other arithmetic, col_lse(): jnp.sum(jnp.exp(col_scores - col_peaks[None, :]), axis=0)  7.86 us
    ppermute x3, starting transfers between devices, on_device(): lax.ppermute(obs_days, 'mod', shift_pairs(n_mod, s))  6.14 us
  transfers between devices with their start and end apart: 22, of which 12 were waited for; matrix products, arithmetic and copies ran while one was open for 19% of the time, Pallas kernels for 0%

profile of v4, /device:TPU:0, one launch (start us, length us, event | category | flops | bytes accessed | tf_op | source)
XLA Modules:
  0.0 119.8 jit_solution(5040963392162393839)
XLA Ops:
  0.6 5.1 %collective-permute-start.2 = (f32[512,128]{1,0:T(8,128)}, f32[512,128]{1,0:T(8,128)S(1)}, u32[]{:S(2)}, u32[]{:S(2)}) collective-permute-start(f32[512,128]{1,0:T(8,128)} %param.5), channel_id=1, source_target_pairs={{0,12},{4,0},{8,4},{12,8},{1,13},{5,1},{9,5},{13,9},{2,14},{6,2},{... | collective-permute-start | bytes 786440 | tf_op jit(solution)/shard_map/ppermute | solution.py:165
  7.9 1.6 %multiply_reduce_fusion = f32[2048]{0:T(1024)S(1)} fusion(f32[2048,128]{1,0:T(8,128)} %param.4), kind=kLoop, calls=%fused_computation.37 | loop fusion | flops 522240 | bytes 1056768 | tf_op jit(solution)/shard_map/reduce_sum | solution.py:157
  9.5 3.9 %fusion.23 = (f32[2048]{0:T(1024)S(1)}, f32[2048,512]{1,0:T(8,128)S(1)}) fusion(f32[2048,128]{1,0:T(8,128)} %param.4, f32[512,128]{1,0:T(8,128)} %param.5, f32[512]{0:T(512)S(1)} %multiply_reduce_fusion.4, f32[2048]{0:T(1024)S(1)} %multiply_reduce_fusion), kind=kOutput, calls=%fused_computation.134 | convolution fusion | flops 812644352 | bytes 5523456 | tf_op jit(solution)/shard_map/dot_general | solution.py:96
  13.5 1.7 %exponential_reduce_fusion.15 = f32[2048]{0:T(1024)S(1)} fusion(f32[2048,512]{1,0:T(8,128)S(1)} %get-tuple-element.68.refs_1_, f32[2048]{0:T(1024)S(1)} %get-tuple-element.67), kind=kLoop, calls=%fused_computation.22 | loop fusion | flops 2095104 | bytes 4210688 | tf_op jit(solution)/shard_map/reduce_sum | solution.py:179
  15.4 2.6 %fusion.25 = (f32[2048]{0:T(1024)S(1)}, f32[2048,512]{1,0:T(8,128)S(1)}) fusion(f32[2048,128]{1,0:T(8,128)S(1)} %copy-done.8, f32[512,128]{1,0:T(8,128)S(1)} %collective-permute-done.2, f32[512]{0:T(512)S(1)} %multiply_reduce_fusion.1, f32[2048]{0:T(1024)S(1)} %multiply_reduce_fusion), kind=kOutput, calls=%fused_computation.136 | convolution fusion | flops 812644352 | bytes 5523456 | tf_op jit(solution)/shard_map/dot_general | solution.py:96
  17.9 1.7 %exponential_reduce_fusion.12 = f32[2048]{0:T(1024)S(1)} fusion(f32[2048,512]{1,0:T(8,128)S(1)} %get-tuple-element.72.refs_4_, f32[2048]{0:T(1024)S(1)} %get-tuple-element.71), kind=kLoop, calls=%fused_computation.16 | loop fusion | flops 2095104 | bytes 4210688 | tf_op jit(solution)/shard_map/reduce_sum | solution.py:179
  19.6 8.6 %collective-permute-done.1 = f32[512,128]{1,0:T(8,128)S(1)} collective-permute-done((f32[512,128]{1,0:T(8,128)}, f32[512,128]{1,0:T(8,128)S(1)}, u32[]{:S(2)}, u32[]{:S(2)}) %collective-permute-start.1) | collective-permute-done | bytes 262176 | tf_op jit(solution)/shard_map/ppermute | solution.py:165
  28.4 2.6 %fusion.24 = (f32[2048]{0:T(1024)S(1)}, f32[2048,512]{1,0:T(8,128)S(1)}) fusion(f32[2048,128]{1,0:T(8,128)S(1)} %copy-done.8, f32[512,128]{1,0:T(8,128)S(1)} %collective-permute-done.1, f32[512]{0:T(512)S(1)} %multiply_reduce_fusion.2, f32[2048]{0:T(1024)S(1)} %multiply_reduce_fusion), kind=kOutput, calls=%fused_computation.135 | convolution fusion | flops 812644352 | bytes 5523456 | tf_op jit(solution)/shard_map/dot_general | solution.py:96
  31.0 1.9 %exponential_reduce_fusion.13 = f32[2048]{0:T(1024)S(1)} fusion(f32[2048,512]{1,0:T(8,128)S(1)} %get-tuple-element.70.refs_3_, f32[2048]{0:T(1024)S(1)} %get-tuple-element.69), kind=kLoop, calls=%fused_computation.18 | loop fusion | flops 2095104 | bytes 4210688 | tf_op jit(solution)/shard_map/reduce_sum | solution.py:179
  33.0 2.6 %fusion.22 = (f32[2048]{0:T(1024)S(1)}, f32[2048,512]{1,0:T(8,128)S(1)}) fusion(f32[2048,128]{1,0:T(8,128)S(1)} %copy-done.8, f32[512,128]{1,0:T(8,128)S(1)} %collective-permute-done, f32[512]{0:T(512)S(1)} %multiply_reduce_fusion.3, f32[2048]{0:T(1024)S(1)} %multiply_reduce_fusion), kind=kOutput, calls=%fused_computation.133 | convolution fusion | flops 812644352 | bytes 5523456 | tf_op jit(solution)/shard_map/dot_general | solution.py:96
  35.6 1.7 %exponential_reduce_fusion.14 = f32[2048]{0:T(1024)S(1)} fusion(f32[2048,512]{1,0:T(8,128)S(1)} %get-tuple-element.66.refs_2_, f32[2048]{0:T(1024)S(1)} %get-tuple-element.65), kind=kLoop, calls=%fused_computation.20 | loop fusion | flops 2095104 | bytes 4210688 | tf_op jit(solution)/shard_map/reduce_sum | solution.py:179
  37.5 1.6 %collective-permute-start.4 = (f32[2048]{0:T(1024)S(1)}, f32[2048]{0:T(1024)S(1)}, u32[]{:S(2)}, u32[]{:S(2)}) collective-permute-start(f32[2048]{0:T(1024)S(1)} %get-tuple-element.62), channel_id=1, source_target_pairs={{0,2},{1,3},{2,0},{3,1},{4,6},{5,7},{6,4},{7,5},{8,10},{9,11},{10,... | collective-permute-start | bytes 24584 | tf_op jit(solution)/shard_map/ppermute | solution.py:109
  42.3 1.7 %exponential_reduce_fusion.11 = (f32[512]{0:T(512)S(1)}, f32[512]{0:T(512)S(1)}, f32[512]{0:T(512)S(1)}, f32[512]{0:T(512)S(1)}) fusion(f32[2048,512]{1,0:T(8,128)S(1)} %get-tuple-element.68.refs_1_, f32[512]{0:T(512)S(1)} %add_reduce_fusion.11, f32[2048]{0:T(1024)S(1)} %add_multiply_fusion.5, f32[2048,512]{1,0:T(8,128)S(1)} %get-tuple-element.66.refs_2_, ...), kind=kLoop, calls=%fused_computation.15 | loop fusion | flops 9435136 | bytes 16795648 | tf_op jit(solution)/shard_map/reduce_sum | solution.py:191
  44.0 2.3 %exponential_reduce_fusion.10 = (f32[512]{0:T(512)S(1)}, f32[512]{0:T(512)S(1)}, f32[512]{0:T(512)S(1)}) fusion(f32[2048,512]{1,0:T(8,128)S(1)} %get-tuple-element.66.refs_2_, f32[512]{0:T(512)S(1)} %get-tuple-element.24, f32[2048]{0:T(1024)S(1)} %add_multiply_fusion.5, f32[512]{0:T(512)S(1)} %get-tuple-element.26, ...), kind=kLoop, calls=%fused_computation.14 | loop fusion | flops 9435648 | bytes 12603392 | tf_op jit(solution)/shard_map/reduce_sum | solution.py:191
  47.5 3.3 %collective-permute-start.8 = (f32[2048]{0:T(1024)S(1)}, f32[2048]{0:T(1024)S(1)}, u32[]{:S(2)}, u32[]{:S(2)}) collective-permute-start(f32[2048]{0:T(1024)S(1)} %bitcast.111), channel_id=1, source_target_pairs={{0,12},{4,0},{8,4},{12,8},{1,13},{5,1},{9,5},{13,9},{2,14},{6,2},{... | collective-permute-start | bytes 24584 | tf_op jit(solution)/shard_map/ppermute | solution.py:109
  50.8 1.6 %collective-permute-done.6 = f32[2048]{0:T(1024)S(1)} collective-permute-done((f32[2048]{0:T(1024)S(1)}, f32[2048]{0:T(1024)S(1)}, u32[]{:S(2)}, u32[]{:S(2)}) %collective-permute-start.6) | collective-permute-done | bytes 8224 | tf_op jit(solution)/shard_map/ppermute | solution.py:109
  53.8 2.7 %add_reduce_fusion.4 = f32[2048]{0:T(1024)S(1)} fusion(f32[2048,512]{1,0:T(8,128)} %copy-done, f32[512]{0:T(512)S(1)} %bitcast.140), kind=kLoop, calls=%fused_computation.28 | loop fusion | flops 2095104 | bytes 4204544 | tf_op jit(solution)/shard_map/reduce_max | solution.py:178
  66.2 2.2 %collective-permute-done.10 = f32[2048]{0:T(1024)S(1)} collective-permute-done((f32[2048]{0:T(1024)S(1)}, f32[2048]{0:T(1024)S(1)}, u32[]{:S(2)}, u32[]{:S(2)}) %collective-permute-start.10) | collective-permute-done | bytes 8224 | tf_op jit(solution)/shard_map/ppermute | solution.py:109
  69.2 1.7 %exponential_reduce_fusion.3 = (f32[512]{0:T(512)S(1)}, f32[512]{0:T(512)S(1)}, f32[512]{0:T(512)S(1)}, f32[512]{0:T(512)S(1)}) fusion(f32[2048,512]{1,0:T(8,128)S(1)} %copy-done.7, f32[512]{0:T(512)S(1)} %add_reduce_fusion.3, f32[2048]{0:T(1024)S(1)} %add_multiply_fusion.3, f32[2048,512]{1,0:T(8,128)S(1)} %copy-done.5, f32[2048,512]{1,0:T(8,128)S(1)} %copy-done.3, ...), kind=kLoop, calls=%fused_computation.7 | loop fusion | flops 9435136 | bytes 16795648 | tf_op jit(solution)/shard_map/reduce_sum | solution.py:191
  70.9 2.2 %exponential_reduce_fusion.2 = (f32[512]{0:T(512)S(1)}, f32[512]{0:T(512)S(1)}, f32[512]{0:T(512)S(1)}) fusion(f32[2048,512]{1,0:T(8,128)S(1)} %copy-done.5, f32[512]{0:T(512)S(1)} %get-tuple-element.17, f32[2048]{0:T(1024)S(1)} %add_multiply_fusion.3, f32[512]{0:T(512)S(1)} %get-tuple-element.19, f32[2048,512]{1,0:T(8,128)S(1)} %copy-done.1, ...), kind=kLoop, calls=%fused_computation.6 | loop fusion | flops 9435648 | bytes 12603392 | tf_op jit(solution)/shard_map/reduce_sum | solution.py:191
  73.9 1.9 %collective-permute-start.12 = (f32[2048]{0:T(1024)S(1)}, f32[2048]{0:T(1024)S(1)}, u32[]{:S(2)}, u32[]{:S(2)}) collective-permute-start(f32[2048]{0:T(1024)S(1)} %bitcast.113), channel_id=1, source_target_pairs={{0,4},{4,8},{8,12},{12,0},{1,5},{5,9},{9,13},{13,1},{2,6},{6,10},{... | collective-permute-start | bytes 24584 | tf_op jit(solution)/shard_map/ppermute | solution.py:109
  75.8 1.9 %collective-permute-start.13 = (f32[2048]{0:T(1024)S(1)}, f32[2048]{0:T(1024)S(1)}, u32[]{:S(2)}, u32[]{:S(2)}) collective-permute-start(f32[2048]{0:T(1024)S(1)} %bitcast.114), channel_id=1, source_target_pairs={{0,8},{4,12},{8,0},{12,4},{1,9},{5,13},{9,1},{13,5},{2,10},{6,14},... | collective-permute-start | bytes 24584 | tf_op jit(solution)/shard_map/ppermute | solution.py:109
  83.4 18.2 %shard_map.49 = (f32[1,2048]{1,0:T(1,128)}, f32[1,2048]{1,0:T(1,128)}, f32[2048,128]{1,0:T(8,128)}) custom-call(f32[1,2048]{1,0:T(1,128)} %bitcast.108, f32[2048,512]{1,0:T(8,128)} %copy-done.6, f32[2048,512]{1,0:T(8,128)} %copy-done.4, f32[2048,512]{1,0:T(8,128)} %copy-done.2, f32[2048,512]{1,0:T(8,128)} %copy-done, f32[2048,128]{1,0:T(8,128)} %pad_maximum_fusion.refs_5_), custom_call_target="tpu_custom_call" | custom-call | tf_op jit(solution)/shard_map/pallas_call | solution.py:71
  114.8 4.2 %collective-permute-done.20 = f32[512,128]{1,0:T(8,128)S(1)} collective-permute-done((f32[512,128]{1,0:T(8,128)S(1)}, f32[512,128]{1,0:T(8,128)S(1)}, u32[]{:S(2)}, u32[]{:S(2)}) %collective-permute-start.20) | collective-permute-done | bytes 262176 | tf_op jit(solution)/shard_map/ppermute | solution.py:146
  (141 shorter events, 39.3 us)
Async XLA Ops:
  0.6 14.6 %collective-permute-start.2 = (f32[512,128]{1,0:T(8,128)}, f32[512,128]{1,0:T(8,128)S(1)}, u32[]{:S(2)}, u32[]{:S(2)}) collective-permute-start(f32[512,128]{1,0:T(8,128)} %param.5), channel_id=1, source_target_pairs={{0,12},{4,0},{8,4},{12,8},{1,13},{5,1},{9,5},{13,9},{2,14},{6,2},{... | collective-permute-start | bytes 786440 | tf_op jit(solution)/shard_map/ppermute | solution.py:165
  5.8 22.5 %collective-permute-start.1 = (f32[512,128]{1,0:T(8,128)}, f32[512,128]{1,0:T(8,128)S(1)}, u32[]{:S(2)}, u32[]{:S(2)}) collective-permute-start(f32[512,128]{1,0:T(8,128)} %param.5), channel_id=1, source_target_pairs={{0,8},{4,12},{8,0},{12,4},{1,9},{5,13},{9,1},{13,5},{2,10},{6,14},... | collective-permute-start | bytes 786440 | tf_op jit(solution)/shard_map/ppermute | solution.py:165
  5.8 27.1 %collective-permute-start = (f32[512,128]{1,0:T(8,128)}, f32[512,128]{1,0:T(8,128)S(1)}, u32[]{:S(2)}, u32[]{:S(2)}) collective-permute-start(f32[512,128]{1,0:T(8,128)} %param.5), channel_id=1, source_target_pairs={{0,4},{4,8},{8,12},{12,0},{1,5},{5,9},{9,13},{13,1},{2,6},{6,10},{... | collective-permute-start | bytes 786440 | tf_op jit(solution)/shard_map/ppermute | solution.py:165
  13.5 28.8 %copy-start.6 = (f32[2048,512]{1,0:T(8,128)}, f32[2048,512]{1,0:T(8,128)S(1)}, u32[]{:S(2)}) copy-start(f32[2048,512]{1,0:T(8,128)S(1)} %get-tuple-element.68.refs_1_) | copy-start | bytes 12582916
  17.9 26.0 %copy-start = (f32[2048,512]{1,0:T(8,128)}, f32[2048,512]{1,0:T(8,128)S(1)}, u32[]{:S(2)}) copy-start(f32[2048,512]{1,0:T(8,128)S(1)} %get-tuple-element.72.refs_4_) | copy-start | bytes 12582916
  37.4 3.1 %collective-permute-start.3 = (f32[2048]{0:T(1024)S(1)}, f32[2048]{0:T(1024)S(1)}, u32[]{:S(2)}, u32[]{:S(2)}) collective-permute-start(f32[2048]{0:T(1024)S(1)} %get-tuple-element.62), channel_id=1, source_target_pairs={{0,1},{1,2},{2,3},{3,0},{4,5},{5,6},{6,7},{7,4},{8,9},{9,10},{10,1... | collective-permute-start | bytes 24584 | tf_op jit(solution)/shard_map/ppermute | solution.py:109
  37.5 3.7 %collective-permute-start.4 = (f32[2048]{0:T(1024)S(1)}, f32[2048]{0:T(1024)S(1)}, u32[]{:S(2)}, u32[]{:S(2)}) collective-permute-start(f32[2048]{0:T(1024)S(1)} %get-tuple-element.62), channel_id=1, source_target_pairs={{0,2},{1,3},{2,0},{3,1},{4,6},{5,7},{6,4},{7,5},{8,10},{9,11},{10,... | collective-permute-start | bytes 24584 | tf_op jit(solution)/shard_map/ppermute | solution.py:109
  39.1 2.8 %collective-permute-start.5 = (f32[2048]{0:T(1024)S(1)}, f32[2048]{0:T(1024)S(1)}, u32[]{:S(2)}, u32[]{:S(2)}) collective-permute-start(f32[2048]{0:T(1024)S(1)} %get-tuple-element.62), channel_id=1, source_target_pairs={{0,3},{1,0},{2,1},{3,2},{4,7},{5,4},{6,5},{7,6},{8,11},{9,8},{10,9... | collective-permute-start | bytes 24584 | tf_op jit(solution)/shard_map/ppermute | solution.py:109
  47.0 5.5 %collective-permute-start.6 = (f32[2048]{0:T(1024)S(1)}, f32[2048]{0:T(1024)S(1)}, u32[]{:S(2)}, u32[]{:S(2)}) collective-permute-start(f32[2048]{0:T(1024)S(1)} %bitcast.109), channel_id=1, source_target_pairs={{0,4},{4,8},{8,12},{12,0},{1,5},{5,9},{9,13},{13,1},{2,6},{6,10},{... | collective-permute-start | bytes 24584 | tf_op jit(solution)/shard_map/ppermute | solution.py:109
  47.5 4.9 %collective-permute-start.7 = (f32[2048]{0:T(1024)S(1)}, f32[2048]{0:T(1024)S(1)}, u32[]{:S(2)}, u32[]{:S(2)}) collective-permute-start(f32[2048]{0:T(1024)S(1)} %bitcast.110), channel_id=1, source_target_pairs={{0,8},{4,12},{8,0},{12,4},{1,9},{5,13},{9,1},{13,5},{2,10},{6,14},... | collective-permute-start | bytes 24584 | tf_op jit(solution)/shard_map/ppermute | solution.py:109
  47.5 5.5 %collective-permute-start.8 = (f32[2048]{0:T(1024)S(1)}, f32[2048]{0:T(1024)S(1)}, u32[]{:S(2)}, u32[]{:S(2)}) collective-permute-start(f32[2048]{0:T(1024)S(1)} %bitcast.111), channel_id=1, source_target_pairs={{0,12},{4,0},{8,4},{12,8},{1,13},{5,1},{9,5},{13,9},{2,14},{6,2},{... | collective-permute-start | bytes 24584 | tf_op jit(solution)/shard_map/ppermute | solution.py:109
  64.6 3.7 %collective-permute-start.10 = (f32[2048]{0:T(1024)S(1)}, f32[2048]{0:T(1024)S(1)}, u32[]{:S(2)}, u32[]{:S(2)}) collective-permute-start(f32[2048]{0:T(1024)S(1)} %get-tuple-element.56), channel_id=1, source_target_pairs={{0,2},{1,3},{2,0},{3,1},{4,6},{5,7},{6,4},{7,5},{8,10},{9,11},{10,... | collective-permute-start | bytes 24584 | tf_op jit(solution)/shard_map/ppermute | solution.py:109
  65.6 2.7 %collective-permute-start.11 = (f32[2048]{0:T(1024)S(1)}, f32[2048]{0:T(1024)S(1)}, u32[]{:S(2)}, u32[]{:S(2)}) collective-permute-start(f32[2048]{0:T(1024)S(1)} %get-tuple-element.56), channel_id=1, source_target_pairs={{0,3},{1,0},{2,1},{3,2},{4,7},{5,4},{6,5},{7,6},{8,11},{9,8},{10,9... | collective-permute-start | bytes 24584 | tf_op jit(solution)/shard_map/ppermute | solution.py:109
  65.6 3.1 %collective-permute-start.9 = (f32[2048]{0:T(1024)S(1)}, f32[2048]{0:T(1024)S(1)}, u32[]{:S(2)}, u32[]{:S(2)}) collective-permute-start(f32[2048]{0:T(1024)S(1)} %get-tuple-element.56), channel_id=1, source_target_pairs={{0,1},{1,2},{2,3},{3,0},{4,5},{5,6},{6,7},{7,4},{8,9},{9,10},{10,1... | collective-permute-start | bytes 24584 | tf_op jit(solution)/shard_map/ppermute | solution.py:109
  73.9 5.5 %collective-permute-start.12 = (f32[2048]{0:T(1024)S(1)}, f32[2048]{0:T(1024)S(1)}, u32[]{:S(2)}, u32[]{:S(2)}) collective-permute-start(f32[2048]{0:T(1024)S(1)} %bitcast.113), channel_id=1, source_target_pairs={{0,4},{4,8},{8,12},{12,0},{1,5},{5,9},{9,13},{13,1},{2,6},{6,10},{... | collective-permute-start | bytes 24584 | tf_op jit(solution)/shard_map/ppermute | solution.py:109
  75.8 4.5 %collective-permute-start.13 = (f32[2048]{0:T(1024)S(1)}, f32[2048]{0:T(1024)S(1)}, u32[]{:S(2)}, u32[]{:S(2)}) collective-permute-start(f32[2048]{0:T(1024)S(1)} %bitcast.114), channel_id=1, source_target_pairs={{0,8},{4,12},{8,0},{12,4},{1,9},{5,13},{9,1},{13,5},{2,10},{6,14},... | collective-permute-start | bytes 24584 | tf_op jit(solution)/shard_map/ppermute | solution.py:109
  77.7 3.7 %collective-permute-start.14 = (f32[2048]{0:T(1024)S(1)}, f32[2048]{0:T(1024)S(1)}, u32[]{:S(2)}, u32[]{:S(2)}) collective-permute-start(f32[2048]{0:T(1024)S(1)} %bitcast.115), channel_id=1, source_target_pairs={{0,12},{4,0},{8,4},{12,8},{1,13},{5,1},{9,5},{13,9},{2,14},{6,2},{... | collective-permute-start | bytes 24584 | tf_op jit(solution)/shard_map/ppermute | solution.py:109
  102.7 3.4 %collective-permute-start.16 = (f32[2,512,128]{2,1,0:T(8,128)S(1)}, f32[2,512,128]{2,1,0:T(8,128)S(1)}, u32[]{:S(2)}, u32[]{:S(2)}) collective-permute-start(f32[2,512,128]{2,1,0:T(8,128)S(1)} %dynamic-slice_bitcast_fusion), channel_id=1, source_target_pairs={{0,1},{1,0},{2,3},{3,2},{4,5},{5,4},{6,7},{7,6},{8,9},{9,8},{10,11... | collective-permute-start | bytes 1572872 | tf_op jit(solution)/shard_map/ppermute | solution.py:134
  104.7 1.4 %collective-permute-start.15 = (f32[2,512]{1,0:T(2,128)S(1)}, f32[2,512]{1,0:T(2,128)S(1)}, u32[]{:S(2)}, u32[]{:S(2)}) collective-permute-start(f32[2,512]{1,0:T(2,128)S(1)} %bitcast.143), channel_id=1, source_target_pairs={{0,1},{1,0},{2,3},{3,2},{4,5},{5,4},{6,7},{7,6},{8,9},{9,8},{10,11... | collective-permute-start | bytes 12296 | tf_op jit(solution)/shard_map/ppermute | solution.py:135
  107.5 5.1 %collective-permute-start.17 = (f32[2048]{0:T(1024)}, f32[2048]{0:T(1024)S(1)}, u32[]{:S(2)}, u32[]{:S(2)}) collective-permute-start(f32[2048]{0:T(1024)} %bitcast.117), channel_id=1, source_target_pairs={{0,1},{1,2},{2,3},{3,0},{4,5},{5,6},{6,7},{7,4},{8,9},{9,10},{10,1... | collective-permute-start | bytes 24584 | tf_op jit(solution)/shard_map/ppermute | solution.py:109
  107.9 4.7 %collective-permute-start.18 = (f32[2048]{0:T(1024)}, f32[2048]{0:T(1024)S(1)}, u32[]{:S(2)}, u32[]{:S(2)}) collective-permute-start(f32[2048]{0:T(1024)} %bitcast.118), channel_id=1, source_target_pairs={{0,2},{1,3},{2,0},{3,1},{4,6},{5,7},{6,4},{7,5},{8,10},{9,11},{10,... | collective-permute-start | bytes 24584 | tf_op jit(solution)/shard_map/ppermute | solution.py:109
  109.3 3.3 %collective-permute-start.19 = (f32[2048]{0:T(1024)}, f32[2048]{0:T(1024)S(1)}, u32[]{:S(2)}, u32[]{:S(2)}) collective-permute-start(f32[2048]{0:T(1024)} %bitcast.119), channel_id=1, source_target_pairs={{0,3},{1,0},{2,1},{3,2},{4,7},{5,4},{6,5},{7,6},{8,11},{9,8},{10,9... | collective-permute-start | bytes 24584 | tf_op jit(solution)/shard_map/ppermute | solution.py:109
  110.4 4.3 %collective-permute-start.21 = (f32[512]{0:T(512)S(1)}, f32[512]{0:T(512)S(1)}, u32[]{:S(2)}, u32[]{:S(2)}) collective-permute-start(f32[512]{0:T(512)S(1)} %bitcast.144), channel_id=1, source_target_pairs={{0,2},{1,3},{2,0},{3,1},{4,6},{5,7},{6,4},{7,5},{8,10},{9,11},{10,... | collective-permute-start | bytes 6152 | tf_op jit(solution)/shard_map/ppermute | solution.py:147
  111.2 7.8 %collective-permute-start.20 = (f32[512,128]{1,0:T(8,128)S(1)}, f32[512,128]{1,0:T(8,128)S(1)}, u32[]{:S(2)}, u32[]{:S(2)}) collective-permute-start(f32[512,128]{1,0:T(8,128)S(1)} %dynamic-slice_bitcast_fusion.1), channel_id=1, source_target_pairs={{0,2},{1,3},{2,0},{3,1},{4,6},{5,7},{6,4},{7,5},{8,10},{9,11},{10,... | collective-permute-start | bytes 786440 | tf_op jit(solution)/shard_map/ppermute | solution.py:146
  (8 other events, 47.0 us)

commit v5 on v4

--- a/solution.py
+++ b/solution.py
@@ -35,7 +35,7 @@
             m = jnp.maximum(m, t)
         m_scr[pl.ds(r, RB), :] = m
         return carry
-    lax.fori_loop(0, tr // RB, p1, 0, unroll=8)
+    lax.fori_loop(0, tr // RB, p1, 0, unroll=16)
     r_scr[...] = jnp.max(m_scr[...], axis=1, keepdims=True)
     m_ref[...] = jnp.max(m_scr[...].T, axis=0, keepdims=True)
 
@@ -50,7 +50,7 @@
                 t = u if t is None else t + u
         t_scr[pl.ds(r, RB), :] = t
         return carry
-    lax.fori_loop(0, tr // RB, p2, 0, unroll=8)
+    lax.fori_loop(0, tr // RB, p2, 0, unroll=16)
     l_ref[...] = m_ref[...] + jnp.log(jnp.sum(t_scr[...].T, axis=0, keepdims=True))
     w = w_ref[...]
     wh = w.astype(jnp.bfloat16)

time: 120 us -> 119 us (level)
  Pallas kernels: 18.2 us -> 16.9 us
    pallas_call x1, Pallas kernels: 18.2 us -> 16.9 us  [final_local(): pl.pallas_call(_final_kernel, grid=(R // tr,), in_specs=[pl.BlockSpec((1,...]
where the time goes in v5:
time: 119 us
  other arithmetic  36.2 us (30%)
  starting transfers between devices  24.5 us (21%)
  waiting for transfers between devices  21.8 us (18%)
  Pallas kernels  16.9 us (14%)
  matrix products  11.6 us (10%)
  local copies, waits for them, and re-layouts  6.4 us (5%)
    pallas_call x1, Pallas kernels, final_local(): pl.pallas_call(_final_kernel, grid=(R // tr,), in_specs=[pl.BlockSpec((1,...  16.9 us
    ppermute x15, starting transfers between devices, lse_across(): lax.ppermute(local_lse, axis, shift_pairs(n, s))  15.6 us
    reduce_sum x8, other arithmetic, row_lse(): jnp.sum(jnp.exp(scores - peaks[:, None]), axis=1)  12.2 us
    dot_general x4, matrix products, pair_scores(): lax.dot_general(block_rows, columns, (((1,), (1,)), ((), ())), precision=...  11.6 us
    ppermute x3, waiting for transfers between devices, on_device(): lax.ppermute(obs_days, 'mod', shift_pairs(n_mod, s))  8.64 us
    ppermute x15, waiting for transfers between devices, lse_across(): lax.ppermute(local_lse, axis, shift_pairs(n, s))  8.13 us
    reduce_sum x4, other arithmetic, col_lse(): jnp.sum(jnp.exp(col_scores - col_peaks[None, :]), axis=0)  7.86 us
    ppermute x3, starting transfers between devices, on_device(): lax.ppermute(obs_days, 'mod', shift_pairs(n_mod, s))  6.14 us
  transfers between devices with their start and end apart: 22, of which 12 were waited for; matrix products, arithmetic and copies ran while one was open for 19% of the time, Pallas kernels for 0%

profile of v5, /device:TPU:0, one launch (start us, length us, event | category | flops | bytes accessed | tf_op | source)
XLA Modules:
  0.0 118.5 jit_solution(3724282020853574161)
XLA Ops:
  0.6 5.1 %collective-permute-start.2 = (f32[512,128]{1,0:T(8,128)}, f32[512,128]{1,0:T(8,128)S(1)}, u32[]{:S(2)}, u32[]{:S(2)}) collective-permute-start(f32[512,128]{1,0:T(8,128)} %param.5), channel_id=1, source_target_pairs={{0,12},{4,0},{8,4},{12,8},{1,13},{5,1},{9,5},{13,9},{2,14},{6,2},{... | collective-permute-start | bytes 786440 | tf_op jit(solution)/shard_map/ppermute | solution.py:165
  7.9 1.6 %multiply_reduce_fusion = f32[2048]{0:T(1024)S(1)} fusion(f32[2048,128]{1,0:T(8,128)} %param.4), kind=kLoop, calls=%fused_computation.37 | loop fusion | flops 522240 | bytes 1056768 | tf_op jit(solution)/shard_map/reduce_sum | solution.py:157
  9.5 3.9 %fusion.23 = (f32[2048]{0:T(1024)S(1)}, f32[2048,512]{1,0:T(8,128)S(1)}) fusion(f32[2048,128]{1,0:T(8,128)} %param.4, f32[512,128]{1,0:T(8,128)} %param.5, f32[512]{0:T(512)S(1)} %multiply_reduce_fusion.4, f32[2048]{0:T(1024)S(1)} %multiply_reduce_fusion), kind=kOutput, calls=%fused_computation.134 | convolution fusion | flops 812644352 | bytes 5523456 | tf_op jit(solution)/shard_map/dot_general | solution.py:96
  13.5 1.7 %exponential_reduce_fusion.15 = f32[2048]{0:T(1024)S(1)} fusion(f32[2048,512]{1,0:T(8,128)S(1)} %get-tuple-element.68.refs_1_, f32[2048]{0:T(1024)S(1)} %get-tuple-element.67), kind=kLoop, calls=%fused_computation.22 | loop fusion | flops 2095104 | bytes 4210688 | tf_op jit(solution)/shard_map/reduce_sum | solution.py:179
  15.4 2.6 %fusion.25 = (f32[2048]{0:T(1024)S(1)}, f32[2048,512]{1,0:T(8,128)S(1)}) fusion(f32[2048,128]{1,0:T(8,128)S(1)} %copy-done.8, f32[512,128]{1,0:T(8,128)S(1)} %collective-permute-done.2, f32[512]{0:T(512)S(1)} %multiply_reduce_fusion.1, f32[2048]{0:T(1024)S(1)} %multiply_reduce_fusion), kind=kOutput, calls=%fused_computation.136 | convolution fusion | flops 812644352 | bytes 5523456 | tf_op jit(solution)/shard_map/dot_general | solution.py:96
  17.9 1.7 %exponential_reduce_fusion.12 = f32[2048]{0:T(1024)S(1)} fusion(f32[2048,512]{1,0:T(8,128)S(1)} %get-tuple-element.72.refs_4_, f32[2048]{0:T(1024)S(1)} %get-tuple-element.71), kind=kLoop, calls=%fused_computation.16 | loop fusion | flops 2095104 | bytes 4210688 | tf_op jit(solution)/shard_map/reduce_sum | solution.py:179
  19.6 8.6 %collective-permute-done.1 = f32[512,128]{1,0:T(8,128)S(1)} collective-permute-done((f32[512,128]{1,0:T(8,128)}, f32[512,128]{1,0:T(8,128)S(1)}, u32[]{:S(2)}, u32[]{:S(2)}) %collective-permute-start.1) | collective-permute-done | bytes 262176 | tf_op jit(solution)/shard_map/ppermute | solution.py:165
  28.4 2.6 %fusion.24 = (f32[2048]{0:T(1024)S(1)}, f32[2048,512]{1,0:T(8,128)S(1)}) fusion(f32[2048,128]{1,0:T(8,128)S(1)} %copy-done.8, f32[512,128]{1,0:T(8,128)S(1)} %collective-permute-done.1, f32[512]{0:T(512)S(1)} %multiply_reduce_fusion.2, f32[2048]{0:T(1024)S(1)} %multiply_reduce_fusion), kind=kOutput, calls=%fused_computation.135 | convolution fusion | flops 812644352 | bytes 5523456 | tf_op jit(solution)/shard_map/dot_general | solution.py:96
  31.0 1.9 %exponential_reduce_fusion.13 = f32[2048]{0:T(1024)S(1)} fusion(f32[2048,512]{1,0:T(8,128)S(1)} %get-tuple-element.70.refs_3_, f32[2048]{0:T(1024)S(1)} %get-tuple-element.69), kind=kLoop, calls=%fused_computation.18 | loop fusion | flops 2095104 | bytes 4210688 | tf_op jit(solution)/shard_map/reduce_sum | solution.py:179
  33.0 2.6 %fusion.22 = (f32[2048]{0:T(1024)S(1)}, f32[2048,512]{1,0:T(8,128)S(1)}) fusion(f32[2048,128]{1,0:T(8,128)S(1)} %copy-done.8, f32[512,128]{1,0:T(8,128)S(1)} %collective-permute-done, f32[512]{0:T(512)S(1)} %multiply_reduce_fusion.3, f32[2048]{0:T(1024)S(1)} %multiply_reduce_fusion), kind=kOutput, calls=%fused_computation.133 | convolution fusion | flops 812644352 | bytes 5523456 | tf_op jit(solution)/shard_map/dot_general | solution.py:96
  35.6 1.7 %exponential_reduce_fusion.14 = f32[2048]{0:T(1024)S(1)} fusion(f32[2048,512]{1,0:T(8,128)S(1)} %get-tuple-element.66.refs_2_, f32[2048]{0:T(1024)S(1)} %get-tuple-element.65), kind=kLoop, calls=%fused_computation.20 | loop fusion | flops 2095104 | bytes 4210688 | tf_op jit(solution)/shard_map/reduce_sum | solution.py:179
  37.5 1.6 %collective-permute-start.4 = (f32[2048]{0:T(1024)S(1)}, f32[2048]{0:T(1024)S(1)}, u32[]{:S(2)}, u32[]{:S(2)}) collective-permute-start(f32[2048]{0:T(1024)S(1)} %get-tuple-element.62), channel_id=1, source_target_pairs={{0,2},{1,3},{2,0},{3,1},{4,6},{5,7},{6,4},{7,5},{8,10},{9,11},{10,... | collective-permute-start | bytes 24584 | tf_op jit(solution)/shard_map/ppermute | solution.py:109
  42.3 1.7 %exponential_reduce_fusion.11 = (f32[512]{0:T(512)S(1)}, f32[512]{0:T(512)S(1)}, f32[512]{0:T(512)S(1)}, f32[512]{0:T(512)S(1)}) fusion(f32[2048,512]{1,0:T(8,128)S(1)} %get-tuple-element.68.refs_1_, f32[512]{0:T(512)S(1)} %add_reduce_fusion.11, f32[2048]{0:T(1024)S(1)} %add_multiply_fusion.5, f32[2048,512]{1,0:T(8,128)S(1)} %get-tuple-element.66.refs_2_, ...), kind=kLoop, calls=%fused_computation.15 | loop fusion | flops 9435136 | bytes 16795648 | tf_op jit(solution)/shard_map/reduce_sum | solution.py:191
  44.0 2.3 %exponential_reduce_fusion.10 = (f32[512]{0:T(512)S(1)}, f32[512]{0:T(512)S(1)}, f32[512]{0:T(512)S(1)}) fusion(f32[2048,512]{1,0:T(8,128)S(1)} %get-tuple-element.66.refs_2_, f32[512]{0:T(512)S(1)} %get-tuple-element.24, f32[2048]{0:T(1024)S(1)} %add_multiply_fusion.5, f32[512]{0:T(512)S(1)} %get-tuple-element.26, ...), kind=kLoop, calls=%fused_computation.14 | loop fusion | flops 9435648 | bytes 12603392 | tf_op jit(solution)/shard_map/reduce_sum | solution.py:191
  47.5 3.3 %collective-permute-start.8 = (f32[2048]{0:T(1024)S(1)}, f32[2048]{0:T(1024)S(1)}, u32[]{:S(2)}, u32[]{:S(2)}) collective-permute-start(f32[2048]{0:T(1024)S(1)} %bitcast.111), channel_id=1, source_target_pairs={{0,12},{4,0},{8,4},{12,8},{1,13},{5,1},{9,5},{13,9},{2,14},{6,2},{... | collective-permute-start | bytes 24584 | tf_op jit(solution)/shard_map/ppermute | solution.py:109
  50.8 1.6 %collective-permute-done.6 = f32[2048]{0:T(1024)S(1)} collective-permute-done((f32[2048]{0:T(1024)S(1)}, f32[2048]{0:T(1024)S(1)}, u32[]{:S(2)}, u32[]{:S(2)}) %collective-permute-start.6) | collective-permute-done | bytes 8224 | tf_op jit(solution)/shard_map/ppermute | solution.py:109
  53.8 2.7 %add_reduce_fusion.4 = f32[2048]{0:T(1024)S(1)} fusion(f32[2048,512]{1,0:T(8,128)} %copy-done, f32[512]{0:T(512)S(1)} %bitcast.140), kind=kLoop, calls=%fused_computation.28 | loop fusion | flops 2095104 | bytes 4204544 | tf_op jit(solution)/shard_map/reduce_max | solution.py:178
  66.2 2.2 %collective-permute-done.10 = f32[2048]{0:T(1024)S(1)} collective-permute-done((f32[2048]{0:T(1024)S(1)}, f32[2048]{0:T(1024)S(1)}, u32[]{:S(2)}, u32[]{:S(2)}) %collective-permute-start.10) | collective-permute-done | bytes 8224 | tf_op jit(solution)/shard_map/ppermute | solution.py:109
  69.2 1.7 %exponential_reduce_fusion.3 = (f32[512]{0:T(512)S(1)}, f32[512]{0:T(512)S(1)}, f32[512]{0:T(512)S(1)}, f32[512]{0:T(512)S(1)}) fusion(f32[2048,512]{1,0:T(8,128)S(1)} %copy-done.7, f32[512]{0:T(512)S(1)} %add_reduce_fusion.3, f32[2048]{0:T(1024)S(1)} %add_multiply_fusion.3, f32[2048,512]{1,0:T(8,128)S(1)} %copy-done.5, f32[2048,512]{1,0:T(8,128)S(1)} %copy-done.3, ...), kind=kLoop, calls=%fused_computation.7 | loop fusion | flops 9435136 | bytes 16795648 | tf_op jit(solution)/shard_map/reduce_sum | solution.py:191
  70.9 2.2 %exponential_reduce_fusion.2 = (f32[512]{0:T(512)S(1)}, f32[512]{0:T(512)S(1)}, f32[512]{0:T(512)S(1)}) fusion(f32[2048,512]{1,0:T(8,128)S(1)} %copy-done.5, f32[512]{0:T(512)S(1)} %get-tuple-element.17, f32[2048]{0:T(1024)S(1)} %add_multiply_fusion.3, f32[512]{0:T(512)S(1)} %get-tuple-element.19, f32[2048,512]{1,0:T(8,128)S(1)} %copy-done.1, ...), kind=kLoop, calls=%fused_computation.6 | loop fusion | flops 9435648 | bytes 12603392 | tf_op jit(solution)/shard_map/reduce_sum | solution.py:191
  73.9 1.9 %collective-permute-start.12 = (f32[2048]{0:T(1024)S(1)}, f32[2048]{0:T(1024)S(1)}, u32[]{:S(2)}, u32[]{:S(2)}) collective-permute-start(f32[2048]{0:T(1024)S(1)} %bitcast.113), channel_id=1, source_target_pairs={{0,4},{4,8},{8,12},{12,0},{1,5},{5,9},{9,13},{13,1},{2,6},{6,10},{... | collective-permute-start | bytes 24584 | tf_op jit(solution)/shard_map/ppermute | solution.py:109
  75.8 1.9 %collective-permute-start.13 = (f32[2048]{0:T(1024)S(1)}, f32[2048]{0:T(1024)S(1)}, u32[]{:S(2)}, u32[]{:S(2)}) collective-permute-start(f32[2048]{0:T(1024)S(1)} %bitcast.114), channel_id=1, source_target_pairs={{0,8},{4,12},{8,0},{12,4},{1,9},{5,13},{9,1},{13,5},{2,10},{6,14},... | collective-permute-start | bytes 24584 | tf_op jit(solution)/shard_map/ppermute | solution.py:109
  83.4 16.9 %shard_map.49 = (f32[1,2048]{1,0:T(1,128)}, f32[1,2048]{1,0:T(1,128)}, f32[2048,128]{1,0:T(8,128)}) custom-call(f32[1,2048]{1,0:T(1,128)} %bitcast.108, f32[2048,512]{1,0:T(8,128)} %copy-done.6, f32[2048,512]{1,0:T(8,128)} %copy-done.4, f32[2048,512]{1,0:T(8,128)} %copy-done.2, f32[2048,512]{1,0:T(8,128)} %copy-done, f32[2048,128]{1,0:T(8,128)} %pad_maximum_fusion.refs_5_), custom_call_target="tpu_custom_call" | custom-call | tf_op jit(solution)/shard_map/pallas_call | solution.py:71
  113.4 4.2 %collective-permute-done.20 = f32[512,128]{1,0:T(8,128)S(1)} collective-permute-done((f32[512,128]{1,0:T(8,128)S(1)}, f32[512,128]{1,0:T(8,128)S(1)}, u32[]{:S(2)}, u32[]{:S(2)}) %collective-permute-start.20) | collective-permute-done | bytes 262176 | tf_op jit(solution)/shard_map/ppermute | solution.py:146
  (141 shorter events, 39.3 us)
Async XLA Ops:
  0.6 14.6 %collective-permute-start.2 = (f32[512,128]{1,0:T(8,128)}, f32[512,128]{1,0:T(8,128)S(1)}, u32[]{:S(2)}, u32[]{:S(2)}) collective-permute-start(f32[512,128]{1,0:T(8,128)} %param.5), channel_id=1, source_target_pairs={{0,12},{4,0},{8,4},{12,8},{1,13},{5,1},{9,5},{13,9},{2,14},{6,2},{... | collective-permute-start | bytes 786440 | tf_op jit(solution)/shard_map/ppermute | solution.py:165
  5.8 22.5 %collective-permute-start.1 = (f32[512,128]{1,0:T(8,128)}, f32[512,128]{1,0:T(8,128)S(1)}, u32[]{:S(2)}, u32[]{:S(2)}) collective-permute-start(f32[512,128]{1,0:T(8,128)} %param.5), channel_id=1, source_target_pairs={{0,8},{4,12},{8,0},{12,4},{1,9},{5,13},{9,1},{13,5},{2,10},{6,14},... | collective-permute-start | bytes 786440 | tf_op jit(solution)/shard_map/ppermute | solution.py:165
  5.8 27.1 %collective-permute-start = (f32[512,128]{1,0:T(8,128)}, f32[512,128]{1,0:T(8,128)S(1)}, u32[]{:S(2)}, u32[]{:S(2)}) collective-permute-start(f32[512,128]{1,0:T(8,128)} %param.5), channel_id=1, source_target_pairs={{0,4},{4,8},{8,12},{12,0},{1,5},{5,9},{9,13},{13,1},{2,6},{6,10},{... | collective-permute-start | bytes 786440 | tf_op jit(solution)/shard_map/ppermute | solution.py:165
  13.5 28.8 %copy-start.6 = (f32[2048,512]{1,0:T(8,128)}, f32[2048,512]{1,0:T(8,128)S(1)}, u32[]{:S(2)}) copy-start(f32[2048,512]{1,0:T(8,128)S(1)} %get-tuple-element.68.refs_1_) | copy-start | bytes 12582916
  17.9 26.0 %copy-start = (f32[2048,512]{1,0:T(8,128)}, f32[2048,512]{1,0:T(8,128)S(1)}, u32[]{:S(2)}) copy-start(f32[2048,512]{1,0:T(8,128)S(1)} %get-tuple-element.72.refs_4_) | copy-start | bytes 12582916
  37.4 3.1 %collective-permute-start.3 = (f32[2048]{0:T(1024)S(1)}, f32[2048]{0:T(1024)S(1)}, u32[]{:S(2)}, u32[]{:S(2)}) collective-permute-start(f32[2048]{0:T(1024)S(1)} %get-tuple-element.62), channel_id=1, source_target_pairs={{0,1},{1,2},{2,3},{3,0},{4,5},{5,6},{6,7},{7,4},{8,9},{9,10},{10,1... | collective-permute-start | bytes 24584 | tf_op jit(solution)/shard_map/ppermute | solution.py:109
  37.5 3.7 %collective-permute-start.4 = (f32[2048]{0:T(1024)S(1)}, f32[2048]{0:T(1024)S(1)}, u32[]{:S(2)}, u32[]{:S(2)}) collective-permute-start(f32[2048]{0:T(1024)S(1)} %get-tuple-element.62), channel_id=1, source_target_pairs={{0,2},{1,3},{2,0},{3,1},{4,6},{5,7},{6,4},{7,5},{8,10},{9,11},{10,... | collective-permute-start | bytes 24584 | tf_op jit(solution)/shard_map/ppermute | solution.py:109
  39.1 2.8 %collective-permute-start.5 = (f32[2048]{0:T(1024)S(1)}, f32[2048]{0:T(1024)S(1)}, u32[]{:S(2)}, u32[]{:S(2)}) collective-permute-start(f32[2048]{0:T(1024)S(1)} %get-tuple-element.62), channel_id=1, source_target_pairs={{0,3},{1,0},{2,1},{3,2},{4,7},{5,4},{6,5},{7,6},{8,11},{9,8},{10,9... | collective-permute-start | bytes 24584 | tf_op jit(solution)/shard_map/ppermute | solution.py:109
  47.0 5.5 %collective-permute-start.6 = (f32[2048]{0:T(1024)S(1)}, f32[2048]{0:T(1024)S(1)}, u32[]{:S(2)}, u32[]{:S(2)}) collective-permute-start(f32[2048]{0:T(1024)S(1)} %bitcast.109), channel_id=1, source_target_pairs={{0,4},{4,8},{8,12},{12,0},{1,5},{5,9},{9,13},{13,1},{2,6},{6,10},{... | collective-permute-start | bytes 24584 | tf_op jit(solution)/shard_map/ppermute | solution.py:109
  47.5 4.9 %collective-permute-start.7 = (f32[2048]{0:T(1024)S(1)}, f32[2048]{0:T(1024)S(1)}, u32[]{:S(2)}, u32[]{:S(2)}) collective-permute-start(f32[2048]{0:T(1024)S(1)} %bitcast.110), channel_id=1, source_target_pairs={{0,8},{4,12},{8,0},{12,4},{1,9},{5,13},{9,1},{13,5},{2,10},{6,14},... | collective-permute-start | bytes 24584 | tf_op jit(solution)/shard_map/ppermute | solution.py:109
  47.5 5.5 %collective-permute-start.8 = (f32[2048]{0:T(1024)S(1)}, f32[2048]{0:T(1024)S(1)}, u32[]{:S(2)}, u32[]{:S(2)}) collective-permute-start(f32[2048]{0:T(1024)S(1)} %bitcast.111), channel_id=1, source_target_pairs={{0,12},{4,0},{8,4},{12,8},{1,13},{5,1},{9,5},{13,9},{2,14},{6,2},{... | collective-permute-start | bytes 24584 | tf_op jit(solution)/shard_map/ppermute | solution.py:109
  64.6 3.7 %collective-permute-start.10 = (f32[2048]{0:T(1024)S(1)}, f32[2048]{0:T(1024)S(1)}, u32[]{:S(2)}, u32[]{:S(2)}) collective-permute-start(f32[2048]{0:T(1024)S(1)} %get-tuple-element.56), channel_id=1, source_target_pairs={{0,2},{1,3},{2,0},{3,1},{4,6},{5,7},{6,4},{7,5},{8,10},{9,11},{10,... | collective-permute-start | bytes 24584 | tf_op jit(solution)/shard_map/ppermute | solution.py:109
  65.6 2.7 %collective-permute-start.11 = (f32[2048]{0:T(1024)S(1)}, f32[2048]{0:T(1024)S(1)}, u32[]{:S(2)}, u32[]{:S(2)}) collective-permute-start(f32[2048]{0:T(1024)S(1)} %get-tuple-element.56), channel_id=1, source_target_pairs={{0,3},{1,0},{2,1},{3,2},{4,7},{5,4},{6,5},{7,6},{8,11},{9,8},{10,9... | collective-permute-start | bytes 24584 | tf_op jit(solution)/shard_map/ppermute | solution.py:109
  65.6 3.1 %collective-permute-start.9 = (f32[2048]{0:T(1024)S(1)}, f32[2048]{0:T(1024)S(1)}, u32[]{:S(2)}, u32[]{:S(2)}) collective-permute-start(f32[2048]{0:T(1024)S(1)} %get-tuple-element.56), channel_id=1, source_target_pairs={{0,1},{1,2},{2,3},{3,0},{4,5},{5,6},{6,7},{7,4},{8,9},{9,10},{10,1... | collective-permute-start | bytes 24584 | tf_op jit(solution)/shard_map/ppermute | solution.py:109
  73.9 5.5 %collective-permute-start.12 = (f32[2048]{0:T(1024)S(1)}, f32[2048]{0:T(1024)S(1)}, u32[]{:S(2)}, u32[]{:S(2)}) collective-permute-start(f32[2048]{0:T(1024)S(1)} %bitcast.113), channel_id=1, source_target_pairs={{0,4},{4,8},{8,12},{12,0},{1,5},{5,9},{9,13},{13,1},{2,6},{6,10},{... | collective-permute-start | bytes 24584 | tf_op jit(solution)/shard_map/ppermute | solution.py:109
  75.8 4.5 %collective-permute-start.13 = (f32[2048]{0:T(1024)S(1)}, f32[2048]{0:T(1024)S(1)}, u32[]{:S(2)}, u32[]{:S(2)}) collective-permute-start(f32[2048]{0:T(1024)S(1)} %bitcast.114), channel_id=1, source_target_pairs={{0,8},{4,12},{8,0},{12,4},{1,9},{5,13},{9,1},{13,5},{2,10},{6,14},... | collective-permute-start | bytes 24584 | tf_op jit(solution)/shard_map/ppermute | solution.py:109
  77.7 3.7 %collective-permute-start.14 = (f32[2048]{0:T(1024)S(1)}, f32[2048]{0:T(1024)S(1)}, u32[]{:S(2)}, u32[]{:S(2)}) collective-permute-start(f32[2048]{0:T(1024)S(1)} %bitcast.115), channel_id=1, source_target_pairs={{0,12},{4,0},{8,4},{12,8},{1,13},{5,1},{9,5},{13,9},{2,14},{6,2},{... | collective-permute-start | bytes 24584 | tf_op jit(solution)/shard_map/ppermute | solution.py:109
  101.4 3.4 %collective-permute-start.16 = (f32[2,512,128]{2,1,0:T(8,128)S(1)}, f32[2,512,128]{2,1,0:T(8,128)S(1)}, u32[]{:S(2)}, u32[]{:S(2)}) collective-permute-start(f32[2,512,128]{2,1,0:T(8,128)S(1)} %dynamic-slice_bitcast_fusion), channel_id=1, source_target_pairs={{0,1},{1,0},{2,3},{3,2},{4,5},{5,4},{6,7},{7,6},{8,9},{9,8},{10,11... | collective-permute-start | bytes 1572872 | tf_op jit(solution)/shard_map/ppermute | solution.py:134
  103.4 1.4 %collective-permute-start.15 = (f32[2,512]{1,0:T(2,128)S(1)}, f32[2,512]{1,0:T(2,128)S(1)}, u32[]{:S(2)}, u32[]{:S(2)}) collective-permute-start(f32[2,512]{1,0:T(2,128)S(1)} %bitcast.143), channel_id=1, source_target_pairs={{0,1},{1,0},{2,3},{3,2},{4,5},{5,4},{6,7},{7,6},{8,9},{9,8},{10,11... | collective-permute-start | bytes 12296 | tf_op jit(solution)/shard_map/ppermute | solution.py:135
  106.2 5.1 %collective-permute-start.17 = (f32[2048]{0:T(1024)}, f32[2048]{0:T(1024)S(1)}, u32[]{:S(2)}, u32[]{:S(2)}) collective-permute-start(f32[2048]{0:T(1024)} %bitcast.117), channel_id=1, source_target_pairs={{0,1},{1,2},{2,3},{3,0},{4,5},{5,6},{6,7},{7,4},{8,9},{9,10},{10,1... | collective-permute-start | bytes 24584 | tf_op jit(solution)/shard_map/ppermute | solution.py:109
  106.6 4.7 %collective-permute-start.18 = (f32[2048]{0:T(1024)}, f32[2048]{0:T(1024)S(1)}, u32[]{:S(2)}, u32[]{:S(2)}) collective-permute-start(f32[2048]{0:T(1024)} %bitcast.118), channel_id=1, source_target_pairs={{0,2},{1,3},{2,0},{3,1},{4,6},{5,7},{6,4},{7,5},{8,10},{9,11},{10,... | collective-permute-start | bytes 24584 | tf_op jit(solution)/shard_map/ppermute | solution.py:109
  108.0 3.3 %collective-permute-start.19 = (f32[2048]{0:T(1024)}, f32[2048]{0:T(1024)S(1)}, u32[]{:S(2)}, u32[]{:S(2)}) collective-permute-start(f32[2048]{0:T(1024)} %bitcast.119), channel_id=1, source_target_pairs={{0,3},{1,0},{2,1},{3,2},{4,7},{5,4},{6,5},{7,6},{8,11},{9,8},{10,9... | collective-permute-start | bytes 24584 | tf_op jit(solution)/shard_map/ppermute | solution.py:109
  109.1 4.3 %collective-permute-start.21 = (f32[512]{0:T(512)S(1)}, f32[512]{0:T(512)S(1)}, u32[]{:S(2)}, u32[]{:S(2)}) collective-permute-start(f32[512]{0:T(512)S(1)} %bitcast.144), channel_id=1, source_target_pairs={{0,2},{1,3},{2,0},{3,1},{4,6},{5,7},{6,4},{7,5},{8,10},{9,11},{10,... | collective-permute-start | bytes 6152 | tf_op jit(solution)/shard_map/ppermute | solution.py:147
  109.9 7.7 %collective-permute-start.20 = (f32[512,128]{1,0:T(8,128)S(1)}, f32[512,128]{1,0:T(8,128)S(1)}, u32[]{:S(2)}, u32[]{:S(2)}) collective-permute-start(f32[512,128]{1,0:T(8,128)S(1)} %dynamic-slice_bitcast_fusion.1), channel_id=1, source_target_pairs={{0,2},{1,3},{2,0},{3,1},{4,6},{5,7},{6,4},{7,5},{8,10},{9,11},{10,... | collective-permute-start | bytes 786440 | tf_op jit(solution)/shard_map/ppermute | solution.py:146
  (8 other events, 47.0 us)

commit v6 on v5

--- a/solution.py
+++ b/solution.py
@@ -35,7 +35,7 @@
             m = jnp.maximum(m, t)
         m_scr[pl.ds(r, RB), :] = m
         return carry
-    lax.fori_loop(0, tr // RB, p1, 0, unroll=16)
+    lax.fori_loop(0, tr // RB, p1, 0, unroll=32)
     r_scr[...] = jnp.max(m_scr[...], axis=1, keepdims=True)
     m_ref[...] = jnp.max(m_scr[...].T, axis=0, keepdims=True)
 
@@ -50,7 +50,7 @@
                 t = u if t is None else t + u
         t_scr[pl.ds(r, RB), :] = t
         return carry
-    lax.fori_loop(0, tr // RB, p2, 0, unroll=16)
+    lax.fori_loop(0, tr // RB, p2, 0, unroll=32)
     l_ref[...] = m_ref[...] + jnp.log(jnp.sum(t_scr[...].T, axis=0, keepdims=True))
     w = w_ref[...]
     wh = w.astype(jnp.bfloat16)

time: 119 us -> 118 us (level)
  no operation moved by 1% of the time
where the time goes in v6:
time: 118 us
  other arithmetic  36.2 us (31%)
  starting transfers between devices  24.5 us (21%)
  waiting for transfers between devices  21.8 us (18%)
  Pallas kernels  16.3 us (14%)
  matrix products  11.6 us (10%)
  local copies, waits for them, and re-layouts  6.4 us (5%)
    pallas_call x1, Pallas kernels, final_local(): pl.pallas_call(_final_kernel, grid=(R // tr,), in_specs=[pl.BlockSpec((1,...  16.3 us
    ppermute x15, starting transfers between devices, lse_across(): lax.ppermute(local_lse, axis, shift_pairs(n, s))  15.6 us
    reduce_sum x8, other arithmetic, row_lse(): jnp.sum(jnp.exp(scores - peaks[:, None]), axis=1)  12.2 us
    dot_general x4, matrix products, pair_scores(): lax.dot_general(block_rows, columns, (((1,), (1,)), ((), ())), precision=...  11.6 us
    ppermute x3, waiting for transfers between devices, on_device(): lax.ppermute(obs_days, 'mod', shift_pairs(n_mod, s))  8.64 us
    ppermute x15, waiting for transfers between devices, lse_across(): lax.ppermute(local_lse, axis, shift_pairs(n, s))  8.13 us
    reduce_sum x4, other arithmetic, col_lse(): jnp.sum(jnp.exp(col_scores - col_peaks[None, :]), axis=0)  7.86 us
    ppermute x3, starting transfers between devices, on_device(): lax.ppermute(obs_days, 'mod', shift_pairs(n_mod, s))  6.14 us
  transfers between devices with their start and end apart: 22, of which 12 were waited for; matrix products, arithmetic and copies ran while one was open for 19% of the time, Pallas kernels for 0%

profile of v6, /device:TPU:0, one launch (start us, length us, event | category | flops | bytes accessed | tf_op | source)
XLA Modules:
  0.0 117.9 jit_solution(8553132560496998454)
XLA Ops:
  0.6 5.1 %collective-permute-start.2 = (f32[512,128]{1,0:T(8,128)}, f32[512,128]{1,0:T(8,128)S(1)}, u32[]{:S(2)}, u32[]{:S(2)}) collective-permute-start(f32[512,128]{1,0:T(8,128)} %param.5), channel_id=1, source_target_pairs={{0,12},{4,0},{8,4},{12,8},{1,13},{5,1},{9,5},{13,9},{2,14},{6,2},{... | collective-permute-start | bytes 786440 | tf_op jit(solution)/shard_map/ppermute | solution.py:165
  7.9 1.6 %multiply_reduce_fusion = f32[2048]{0:T(1024)S(1)} fusion(f32[2048,128]{1,0:T(8,128)} %param.4), kind=kLoop, calls=%fused_computation.37 | loop fusion | flops 522240 | bytes 1056768 | tf_op jit(solution)/shard_map/reduce_sum | solution.py:157
  9.5 3.9 %fusion.23 = (f32[2048]{0:T(1024)S(1)}, f32[2048,512]{1,0:T(8,128)S(1)}) fusion(f32[2048,128]{1,0:T(8,128)} %param.4, f32[512,128]{1,0:T(8,128)} %param.5, f32[512]{0:T(512)S(1)} %multiply_reduce_fusion.4, f32[2048]{0:T(1024)S(1)} %multiply_reduce_fusion), kind=kOutput, calls=%fused_computation.134 | convolution fusion | flops 812644352 | bytes 5523456 | tf_op jit(solution)/shard_map/dot_general | solution.py:96
  13.5 1.7 %exponential_reduce_fusion.15 = f32[2048]{0:T(1024)S(1)} fusion(f32[2048,512]{1,0:T(8,128)S(1)} %get-tuple-element.68.refs_1_, f32[2048]{0:T(1024)S(1)} %get-tuple-element.67), kind=kLoop, calls=%fused_computation.22 | loop fusion | flops 2095104 | bytes 4210688 | tf_op jit(solution)/shard_map/reduce_sum | solution.py:179
  15.4 2.6 %fusion.25 = (f32[2048]{0:T(1024)S(1)}, f32[2048,512]{1,0:T(8,128)S(1)}) fusion(f32[2048,128]{1,0:T(8,128)S(1)} %copy-done.8, f32[512,128]{1,0:T(8,128)S(1)} %collective-permute-done.2, f32[512]{0:T(512)S(1)} %multiply_reduce_fusion.1, f32[2048]{0:T(1024)S(1)} %multiply_reduce_fusion), kind=kOutput, calls=%fused_computation.136 | convolution fusion | flops 812644352 | bytes 5523456 | tf_op jit(solution)/shard_map/dot_general | solution.py:96
  17.9 1.7 %exponential_reduce_fusion.12 = f32[2048]{0:T(1024)S(1)} fusion(f32[2048,512]{1,0:T(8,128)S(1)} %get-tuple-element.72.refs_4_, f32[2048]{0:T(1024)S(1)} %get-tuple-element.71), kind=kLoop, calls=%fused_computation.16 | loop fusion | flops 2095104 | bytes 4210688 | tf_op jit(solution)/shard_map/reduce_sum | solution.py:179
  19.6 8.6 %collective-permute-done.1 = f32[512,128]{1,0:T(8,128)S(1)} collective-permute-done((f32[512,128]{1,0:T(8,128)}, f32[512,128]{1,0:T(8,128)S(1)}, u32[]{:S(2)}, u32[]{:S(2)}) %collective-permute-start.1) | collective-permute-done | bytes 262176 | tf_op jit(solution)/shard_map/ppermute | solution.py:165
  28.4 2.6 %fusion.24 = (f32[2048]{0:T(1024)S(1)}, f32[2048,512]{1,0:T(8,128)S(1)}) fusion(f32[2048,128]{1,0:T(8,128)S(1)} %copy-done.8, f32[512,128]{1,0:T(8,128)S(1)} %collective-permute-done.1, f32[512]{0:T(512)S(1)} %multiply_reduce_fusion.2, f32[2048]{0:T(1024)S(1)} %multiply_reduce_fusion), kind=kOutput, calls=%fused_computation.135 | convolution fusion | flops 812644352 | bytes 5523456 | tf_op jit(solution)/shard_map/dot_general | solution.py:96
  31.0 1.9 %exponential_reduce_fusion.13 = f32[2048]{0:T(1024)S(1)} fusion(f32[2048,512]{1,0:T(8,128)S(1)} %get-tuple-element.70.refs_3_, f32[2048]{0:T(1024)S(1)} %get-tuple-element.69), kind=kLoop, calls=%fused_computation.18 | loop fusion | flops 2095104 | bytes 4210688 | tf_op jit(solution)/shard_map/reduce_sum | solution.py:179
  33.0 2.6 %fusion.22 = (f32[2048]{0:T(1024)S(1)}, f32[2048,512]{1,0:T(8,128)S(1)}) fusion(f32[2048,128]{1,0:T(8,128)S(1)} %copy-done.8, f32[512,128]{1,0:T(8,128)S(1)} %collective-permute-done, f32[512]{0:T(512)S(1)} %multiply_reduce_fusion.3, f32[2048]{0:T(1024)S(1)} %multiply_reduce_fusion), kind=kOutput, calls=%fused_computation.133 | convolution fusion | flops 812644352 | bytes 5523456 | tf_op jit(solution)/shard_map/dot_general | solution.py:96
  35.6 1.7 %exponential_reduce_fusion.14 = f32[2048]{0:T(1024)S(1)} fusion(f32[2048,512]{1,0:T(8,128)S(1)} %get-tuple-element.66.refs_2_, f32[2048]{0:T(1024)S(1)} %get-tuple-element.65), kind=kLoop, calls=%fused_computation.20 | loop fusion | flops 2095104 | bytes 4210688 | tf_op jit(solution)/shard_map/reduce_sum | solution.py:179
  37.5 1.6 %collective-permute-start.4 = (f32[2048]{0:T(1024)S(1)}, f32[2048]{0:T(1024)S(1)}, u32[]{:S(2)}, u32[]{:S(2)}) collective-permute-start(f32[2048]{0:T(1024)S(1)} %get-tuple-element.62), channel_id=1, source_target_pairs={{0,2},{1,3},{2,0},{3,1},{4,6},{5,7},{6,4},{7,5},{8,10},{9,11},{10,... | collective-permute-start | bytes 24584 | tf_op jit(solution)/shard_map/ppermute | solution.py:109
  42.3 1.7 %exponential_reduce_fusion.11 = (f32[512]{0:T(512)S(1)}, f32[512]{0:T(512)S(1)}, f32[512]{0:T(512)S(1)}, f32[512]{0:T(512)S(1)}) fusion(f32[2048,512]{1,0:T(8,128)S(1)} %get-tuple-element.68.refs_1_, f32[512]{0:T(512)S(1)} %add_reduce_fusion.11, f32[2048]{0:T(1024)S(1)} %add_multiply_fusion.5, f32[2048,512]{1,0:T(8,128)S(1)} %get-tuple-element.66.refs_2_, ...), kind=kLoop, calls=%fused_computation.15 | loop fusion | flops 9435136 | bytes 16795648 | tf_op jit(solution)/shard_map/reduce_sum | solution.py:191
  44.0 2.3 %exponential_reduce_fusion.10 = (f32[512]{0:T(512)S(1)}, f32[512]{0:T(512)S(1)}, f32[512]{0:T(512)S(1)}) fusion(f32[2048,512]{1,0:T(8,128)S(1)} %get-tuple-element.66.refs_2_, f32[512]{0:T(512)S(1)} %get-tuple-element.24, f32[2048]{0:T(1024)S(1)} %add_multiply_fusion.5, f32[512]{0:T(512)S(1)} %get-tuple-element.26, ...), kind=kLoop, calls=%fused_computation.14 | loop fusion | flops 9435648 | bytes 12603392 | tf_op jit(solution)/shard_map/reduce_sum | solution.py:191
  47.5 3.3 %collective-permute-start.8 = (f32[2048]{0:T(1024)S(1)}, f32[2048]{0:T(1024)S(1)}, u32[]{:S(2)}, u32[]{:S(2)}) collective-permute-start(f32[2048]{0:T(1024)S(1)} %bitcast.111), channel_id=1, source_target_pairs={{0,12},{4,0},{8,4},{12,8},{1,13},{5,1},{9,5},{13,9},{2,14},{6,2},{... | collective-permute-start | bytes 24584 | tf_op jit(solution)/shard_map/ppermute | solution.py:109
  50.8 1.6 %collective-permute-done.6 = f32[2048]{0:T(1024)S(1)} collective-permute-done((f32[2048]{0:T(1024)S(1)}, f32[2048]{0:T(1024)S(1)}, u32[]{:S(2)}, u32[]{:S(2)}) %collective-permute-start.6) | collective-permute-done | bytes 8224 | tf_op jit(solution)/shard_map/ppermute | solution.py:109
  53.8 2.7 %add_reduce_fusion.4 = f32[2048]{0:T(1024)S(1)} fusion(f32[2048,512]{1,0:T(8,128)} %copy-done, f32[512]{0:T(512)S(1)} %bitcast.140), kind=kLoop, calls=%fused_computation.28 | loop fusion | flops 2095104 | bytes 4204544 | tf_op jit(solution)/shard_map/reduce_max | solution.py:178
  66.2 2.2 %collective-permute-done.10 = f32[2048]{0:T(1024)S(1)} collective-permute-done((f32[2048]{0:T(1024)S(1)}, f32[2048]{0:T(1024)S(1)}, u32[]{:S(2)}, u32[]{:S(2)}) %collective-permute-start.10) | collective-permute-done | bytes 8224 | tf_op jit(solution)/shard_map/ppermute | solution.py:109
  69.2 1.7 %exponential_reduce_fusion.3 = (f32[512]{0:T(512)S(1)}, f32[512]{0:T(512)S(1)}, f32[512]{0:T(512)S(1)}, f32[512]{0:T(512)S(1)}) fusion(f32[2048,512]{1,0:T(8,128)S(1)} %copy-done.7, f32[512]{0:T(512)S(1)} %add_reduce_fusion.3, f32[2048]{0:T(1024)S(1)} %add_multiply_fusion.3, f32[2048,512]{1,0:T(8,128)S(1)} %copy-done.5, f32[2048,512]{1,0:T(8,128)S(1)} %copy-done.3, ...), kind=kLoop, calls=%fused_computation.7 | loop fusion | flops 9435136 | bytes 16795648 | tf_op jit(solution)/shard_map/reduce_sum | solution.py:191
  70.9 2.2 %exponential_reduce_fusion.2 = (f32[512]{0:T(512)S(1)}, f32[512]{0:T(512)S(1)}, f32[512]{0:T(512)S(1)}) fusion(f32[2048,512]{1,0:T(8,128)S(1)} %copy-done.5, f32[512]{0:T(512)S(1)} %get-tuple-element.17, f32[2048]{0:T(1024)S(1)} %add_multiply_fusion.3, f32[512]{0:T(512)S(1)} %get-tuple-element.19, f32[2048,512]{1,0:T(8,128)S(1)} %copy-done.1, ...), kind=kLoop, calls=%fused_computation.6 | loop fusion | flops 9435648 | bytes 12603392 | tf_op jit(solution)/shard_map/reduce_sum | solution.py:191
  73.9 1.9 %collective-permute-start.12 = (f32[2048]{0:T(1024)S(1)}, f32[2048]{0:T(1024)S(1)}, u32[]{:S(2)}, u32[]{:S(2)}) collective-permute-start(f32[2048]{0:T(1024)S(1)} %bitcast.113), channel_id=1, source_target_pairs={{0,4},{4,8},{8,12},{12,0},{1,5},{5,9},{9,13},{13,1},{2,6},{6,10},{... | collective-permute-start | bytes 24584 | tf_op jit(solution)/shard_map/ppermute | solution.py:109
  75.8 1.9 %collective-permute-start.13 = (f32[2048]{0:T(1024)S(1)}, f32[2048]{0:T(1024)S(1)}, u32[]{:S(2)}, u32[]{:S(2)}) collective-permute-start(f32[2048]{0:T(1024)S(1)} %bitcast.114), channel_id=1, source_target_pairs={{0,8},{4,12},{8,0},{12,4},{1,9},{5,13},{9,1},{13,5},{2,10},{6,14},... | collective-permute-start | bytes 24584 | tf_op jit(solution)/shard_map/ppermute | solution.py:109
  83.4 16.3 %shard_map.49 = (f32[1,2048]{1,0:T(1,128)}, f32[1,2048]{1,0:T(1,128)}, f32[2048,128]{1,0:T(8,128)}) custom-call(f32[1,2048]{1,0:T(1,128)} %bitcast.108, f32[2048,512]{1,0:T(8,128)} %copy-done.6, f32[2048,512]{1,0:T(8,128)} %copy-done.4, f32[2048,512]{1,0:T(8,128)} %copy-done.2, f32[2048,512]{1,0:T(8,128)} %copy-done, f32[2048,128]{1,0:T(8,128)} %pad_maximum_fusion.refs_5_), custom_call_target="tpu_custom_call" | custom-call | tf_op jit(solution)/shard_map/pallas_call | solution.py:71
  112.8 4.2 %collective-permute-done.20 = f32[512,128]{1,0:T(8,128)S(1)} collective-permute-done((f32[512,128]{1,0:T(8,128)S(1)}, f32[512,128]{1,0:T(8,128)S(1)}, u32[]{:S(2)}, u32[]{:S(2)}) %collective-permute-start.20) | collective-permute-done | bytes 262176 | tf_op jit(solution)/shard_map/ppermute | solution.py:146
  (141 shorter events, 39.3 us)
Async XLA Ops:
  0.6 14.6 %collective-permute-start.2 = (f32[512,128]{1,0:T(8,128)}, f32[512,128]{1,0:T(8,128)S(1)}, u32[]{:S(2)}, u32[]{:S(2)}) collective-permute-start(f32[512,128]{1,0:T(8,128)} %param.5), channel_id=1, source_target_pairs={{0,12},{4,0},{8,4},{12,8},{1,13},{5,1},{9,5},{13,9},{2,14},{6,2},{... | collective-permute-start | bytes 786440 | tf_op jit(solution)/shard_map/ppermute | solution.py:165
  5.8 22.5 %collective-permute-start.1 = (f32[512,128]{1,0:T(8,128)}, f32[512,128]{1,0:T(8,128)S(1)}, u32[]{:S(2)}, u32[]{:S(2)}) collective-permute-start(f32[512,128]{1,0:T(8,128)} %param.5), channel_id=1, source_target_pairs={{0,8},{4,12},{8,0},{12,4},{1,9},{5,13},{9,1},{13,5},{2,10},{6,14},... | collective-permute-start | bytes 786440 | tf_op jit(solution)/shard_map/ppermute | solution.py:165
  5.8 27.1 %collective-permute-start = (f32[512,128]{1,0:T(8,128)}, f32[512,128]{1,0:T(8,128)S(1)}, u32[]{:S(2)}, u32[]{:S(2)}) collective-permute-start(f32[512,128]{1,0:T(8,128)} %param.5), channel_id=1, source_target_pairs={{0,4},{4,8},{8,12},{12,0},{1,5},{5,9},{9,13},{13,1},{2,6},{6,10},{... | collective-permute-start | bytes 786440 | tf_op jit(solution)/shard_map/ppermute | solution.py:165
  13.5 28.8 %copy-start.6 = (f32[2048,512]{1,0:T(8,128)}, f32[2048,512]{1,0:T(8,128)S(1)}, u32[]{:S(2)}) copy-start(f32[2048,512]{1,0:T(8,128)S(1)} %get-tuple-element.68.refs_1_) | copy-start | bytes 12582916
  17.9 26.0 %copy-start = (f32[2048,512]{1,0:T(8,128)}, f32[2048,512]{1,0:T(8,128)S(1)}, u32[]{:S(2)}) copy-start(f32[2048,512]{1,0:T(8,128)S(1)} %get-tuple-element.72.refs_4_) | copy-start | bytes 12582916
  37.4 3.1 %collective-permute-start.3 = (f32[2048]{0:T(1024)S(1)}, f32[2048]{0:T(1024)S(1)}, u32[]{:S(2)}, u32[]{:S(2)}) collective-permute-start(f32[2048]{0:T(1024)S(1)} %get-tuple-element.62), channel_id=1, source_target_pairs={{0,1},{1,2},{2,3},{3,0},{4,5},{5,6},{6,7},{7,4},{8,9},{9,10},{10,1... | collective-permute-start | bytes 24584 | tf_op jit(solution)/shard_map/ppermute | solution.py:109
  37.5 3.7 %collective-permute-start.4 = (f32[2048]{0:T(1024)S(1)}, f32[2048]{0:T(1024)S(1)}, u32[]{:S(2)}, u32[]{:S(2)}) collective-permute-start(f32[2048]{0:T(1024)S(1)} %get-tuple-element.62), channel_id=1, source_target_pairs={{0,2},{1,3},{2,0},{3,1},{4,6},{5,7},{6,4},{7,5},{8,10},{9,11},{10,... | collective-permute-start | bytes 24584 | tf_op jit(solution)/shard_map/ppermute | solution.py:109
  39.1 2.8 %collective-permute-start.5 = (f32[2048]{0:T(1024)S(1)}, f32[2048]{0:T(1024)S(1)}, u32[]{:S(2)}, u32[]{:S(2)}) collective-permute-start(f32[2048]{0:T(1024)S(1)} %get-tuple-element.62), channel_id=1, source_target_pairs={{0,3},{1,0},{2,1},{3,2},{4,7},{5,4},{6,5},{7,6},{8,11},{9,8},{10,9... | collective-permute-start | bytes 24584 | tf_op jit(solution)/shard_map/ppermute | solution.py:109
  47.0 5.5 %collective-permute-start.6 = (f32[2048]{0:T(1024)S(1)}, f32[2048]{0:T(1024)S(1)}, u32[]{:S(2)}, u32[]{:S(2)}) collective-permute-start(f32[2048]{0:T(1024)S(1)} %bitcast.109), channel_id=1, source_target_pairs={{0,4},{4,8},{8,12},{12,0},{1,5},{5,9},{9,13},{13,1},{2,6},{6,10},{... | collective-permute-start | bytes 24584 | tf_op jit(solution)/shard_map/ppermute | solution.py:109
  47.5 4.9 %collective-permute-start.7 = (f32[2048]{0:T(1024)S(1)}, f32[2048]{0:T(1024)S(1)}, u32[]{:S(2)}, u32[]{:S(2)}) collective-permute-start(f32[2048]{0:T(1024)S(1)} %bitcast.110), channel_id=1, source_target_pairs={{0,8},{4,12},{8,0},{12,4},{1,9},{5,13},{9,1},{13,5},{2,10},{6,14},... | collective-permute-start | bytes 24584 | tf_op jit(solution)/shard_map/ppermute | solution.py:109
  47.5 5.5 %collective-permute-start.8 = (f32[2048]{0:T(1024)S(1)}, f32[2048]{0:T(1024)S(1)}, u32[]{:S(2)}, u32[]{:S(2)}) collective-permute-start(f32[2048]{0:T(1024)S(1)} %bitcast.111), channel_id=1, source_target_pairs={{0,12},{4,0},{8,4},{12,8},{1,13},{5,1},{9,5},{13,9},{2,14},{6,2},{... | collective-permute-start | bytes 24584 | tf_op jit(solution)/shard_map/ppermute | solution.py:109
  64.6 3.7 %collective-permute-start.10 = (f32[2048]{0:T(1024)S(1)}, f32[2048]{0:T(1024)S(1)}, u32[]{:S(2)}, u32[]{:S(2)}) collective-permute-start(f32[2048]{0:T(1024)S(1)} %get-tuple-element.56), channel_id=1, source_target_pairs={{0,2},{1,3},{2,0},{3,1},{4,6},{5,7},{6,4},{7,5},{8,10},{9,11},{10,... | collective-permute-start | bytes 24584 | tf_op jit(solution)/shard_map/ppermute | solution.py:109
  65.6 2.7 %collective-permute-start.11 = (f32[2048]{0:T(1024)S(1)}, f32[2048]{0:T(1024)S(1)}, u32[]{:S(2)}, u32[]{:S(2)}) collective-permute-start(f32[2048]{0:T(1024)S(1)} %get-tuple-element.56), channel_id=1, source_target_pairs={{0,3},{1,0},{2,1},{3,2},{4,7},{5,4},{6,5},{7,6},{8,11},{9,8},{10,9... | collective-permute-start | bytes 24584 | tf_op jit(solution)/shard_map/ppermute | solution.py:109
  65.6 3.1 %collective-permute-start.9 = (f32[2048]{0:T(1024)S(1)}, f32[2048]{0:T(1024)S(1)}, u32[]{:S(2)}, u32[]{:S(2)}) collective-permute-start(f32[2048]{0:T(1024)S(1)} %get-tuple-element.56), channel_id=1, source_target_pairs={{0,1},{1,2},{2,3},{3,0},{4,5},{5,6},{6,7},{7,4},{8,9},{9,10},{10,1... | collective-permute-start | bytes 24584 | tf_op jit(solution)/shard_map/ppermute | solution.py:109
  73.9 5.5 %collective-permute-start.12 = (f32[2048]{0:T(1024)S(1)}, f32[2048]{0:T(1024)S(1)}, u32[]{:S(2)}, u32[]{:S(2)}) collective-permute-start(f32[2048]{0:T(1024)S(1)} %bitcast.113), channel_id=1, source_target_pairs={{0,4},{4,8},{8,12},{12,0},{1,5},{5,9},{9,13},{13,1},{2,6},{6,10},{... | collective-permute-start | bytes 24584 | tf_op jit(solution)/shard_map/ppermute | solution.py:109
  75.8 4.5 %collective-permute-start.13 = (f32[2048]{0:T(1024)S(1)}, f32[2048]{0:T(1024)S(1)}, u32[]{:S(2)}, u32[]{:S(2)}) collective-permute-start(f32[2048]{0:T(1024)S(1)} %bitcast.114), channel_id=1, source_target_pairs={{0,8},{4,12},{8,0},{12,4},{1,9},{5,13},{9,1},{13,5},{2,10},{6,14},... | collective-permute-start | bytes 24584 | tf_op jit(solution)/shard_map/ppermute | solution.py:109
  77.7 3.7 %collective-permute-start.14 = (f32[2048]{0:T(1024)S(1)}, f32[2048]{0:T(1024)S(1)}, u32[]{:S(2)}, u32[]{:S(2)}) collective-permute-start(f32[2048]{0:T(1024)S(1)} %bitcast.115), channel_id=1, source_target_pairs={{0,12},{4,0},{8,4},{12,8},{1,13},{5,1},{9,5},{13,9},{2,14},{6,2},{... | collective-permute-start | bytes 24584 | tf_op jit(solution)/shard_map/ppermute | solution.py:109
  100.8 3.4 %collective-permute-start.16 = (f32[2,512,128]{2,1,0:T(8,128)S(1)}, f32[2,512,128]{2,1,0:T(8,128)S(1)}, u32[]{:S(2)}, u32[]{:S(2)}) collective-permute-start(f32[2,512,128]{2,1,0:T(8,128)S(1)} %dynamic-slice_bitcast_fusion), channel_id=1, source_target_pairs={{0,1},{1,0},{2,3},{3,2},{4,5},{5,4},{6,7},{7,6},{8,9},{9,8},{10,11... | collective-permute-start | bytes 1572872 | tf_op jit(solution)/shard_map/ppermute | solution.py:134
  102.8 1.4 %collective-permute-start.15 = (f32[2,512]{1,0:T(2,128)S(1)}, f32[2,512]{1,0:T(2,128)S(1)}, u32[]{:S(2)}, u32[]{:S(2)}) collective-permute-start(f32[2,512]{1,0:T(2,128)S(1)} %bitcast.143), channel_id=1, source_target_pairs={{0,1},{1,0},{2,3},{3,2},{4,5},{5,4},{6,7},{7,6},{8,9},{9,8},{10,11... | collective-permute-start | bytes 12296 | tf_op jit(solution)/shard_map/ppermute | solution.py:135
  105.6 5.1 %collective-permute-start.17 = (f32[2048]{0:T(1024)}, f32[2048]{0:T(1024)S(1)}, u32[]{:S(2)}, u32[]{:S(2)}) collective-permute-start(f32[2048]{0:T(1024)} %bitcast.117), channel_id=1, source_target_pairs={{0,1},{1,2},{2,3},{3,0},{4,5},{5,6},{6,7},{7,4},{8,9},{9,10},{10,1... | collective-permute-start | bytes 24584 | tf_op jit(solution)/shard_map/ppermute | solution.py:109
  106.0 4.7 %collective-permute-start.18 = (f32[2048]{0:T(1024)}, f32[2048]{0:T(1024)S(1)}, u32[]{:S(2)}, u32[]{:S(2)}) collective-permute-start(f32[2048]{0:T(1024)} %bitcast.118), channel_id=1, source_target_pairs={{0,2},{1,3},{2,0},{3,1},{4,6},{5,7},{6,4},{7,5},{8,10},{9,11},{10,... | collective-permute-start | bytes 24584 | tf_op jit(solution)/shard_map/ppermute | solution.py:109
  107.4 3.3 %collective-permute-start.19 = (f32[2048]{0:T(1024)}, f32[2048]{0:T(1024)S(1)}, u32[]{:S(2)}, u32[]{:S(2)}) collective-permute-start(f32[2048]{0:T(1024)} %bitcast.119), channel_id=1, source_target_pairs={{0,3},{1,0},{2,1},{3,2},{4,7},{5,4},{6,5},{7,6},{8,11},{9,8},{10,9... | collective-permute-start | bytes 24584 | tf_op jit(solution)/shard_map/ppermute | solution.py:109
  108.5 4.3 %collective-permute-start.21 = (f32[512]{0:T(512)S(1)}, f32[512]{0:T(512)S(1)}, u32[]{:S(2)}, u32[]{:S(2)}) collective-permute-start(f32[512]{0:T(512)S(1)} %bitcast.144), channel_id=1, source_target_pairs={{0,2},{1,3},{2,0},{3,1},{4,6},{5,7},{6,4},{7,5},{8,10},{9,11},{10,... | collective-permute-start | bytes 6152 | tf_op jit(solution)/shard_map/ppermute | solution.py:147
  109.2 7.8 %collective-permute-start.20 = (f32[512,128]{1,0:T(8,128)S(1)}, f32[512,128]{1,0:T(8,128)S(1)}, u32[]{:S(2)}, u32[]{:S(2)}) collective-permute-start(f32[512,128]{1,0:T(8,128)S(1)} %dynamic-slice_bitcast_fusion.1), channel_id=1, source_target_pairs={{0,2},{1,3},{2,0},{3,1},{4,6},{5,7},{6,4},{7,5},{8,10},{9,11},{10,... | collective-permute-start | bytes 786440 | tf_op jit(solution)/shard_map/ppermute | solution.py:146
  (8 other events, 47.0 us)

commit v7 on v5

--- a/solution.py
+++ b/solution.py
@@ -9,7 +9,7 @@
 
 ITERS = 2
 
-RB = 8
+RB = 16
 
 
 def _lane_tiles(s):

time: 119 us -> 118 us (level)
  no operation moved by 1% of the time
where the time goes in v7:
time: 118 us
  other arithmetic  36.2 us (31%)
  starting transfers between devices  24.5 us (21%)
  waiting for transfers between devices  21.8 us (18%)
  Pallas kernels  16.3 us (14%)
  matrix products  11.6 us (10%)
  local copies, waits for them, and re-layouts  6.4 us (5%)
    pallas_call x1, Pallas kernels, final_local(): pl.pallas_call(_final_kernel, grid=(R // tr,), in_specs=[pl.BlockSpec((1,...  16.3 us
    ppermute x15, starting transfers between devices, lse_across(): lax.ppermute(local_lse, axis, shift_pairs(n, s))  15.6 us
    reduce_sum x8, other arithmetic, row_lse(): jnp.sum(jnp.exp(scores - peaks[:, None]), axis=1)  12.2 us
    dot_general x4, matrix products, pair_scores(): lax.dot_general(block_rows, columns, (((1,), (1,)), ((), ())), precision=...  11.6 us
    ppermute x3, waiting for transfers between devices, on_device(): lax.ppermute(obs_days, 'mod', shift_pairs(n_mod, s))  8.64 us
    ppermute x15, waiting for transfers between devices, lse_across(): lax.ppermute(local_lse, axis, shift_pairs(n, s))  8.13 us
    reduce_sum x4, other arithmetic, col_lse(): jnp.sum(jnp.exp(col_scores - col_peaks[None, :]), axis=0)  7.86 us
    ppermute x3, starting transfers between devices, on_device(): lax.ppermute(obs_days, 'mod', shift_pairs(n_mod, s))  6.14 us
  transfers between devices with their start and end apart: 22, of which 12 were waited for; matrix products, arithmetic and copies ran while one was open for 19% of the time, Pallas kernels for 0%

profile of v7, /device:TPU:0, one launch (start us, length us, event | category | flops | bytes accessed | tf_op | source)
XLA Modules:
  0.0 117.9 jit_solution(2226001743267724030)
XLA Ops:
  0.6 5.1 %collective-permute-start.2 = (f32[512,128]{1,0:T(8,128)}, f32[512,128]{1,0:T(8,128)S(1)}, u32[]{:S(2)}, u32[]{:S(2)}) collective-permute-start(f32[512,128]{1,0:T(8,128)} %param.5), channel_id=1, source_target_pairs={{0,12},{4,0},{8,4},{12,8},{1,13},{5,1},{9,5},{13,9},{2,14},{6,2},{... | collective-permute-start | bytes 786440 | tf_op jit(solution)/shard_map/ppermute | solution.py:165
  7.9 1.6 %multiply_reduce_fusion = f32[2048]{0:T(1024)S(1)} fusion(f32[2048,128]{1,0:T(8,128)} %param.4), kind=kLoop, calls=%fused_computation.37 | loop fusion | flops 522240 | bytes 1056768 | tf_op jit(solution)/shard_map/reduce_sum | solution.py:157
  9.5 3.9 %fusion.23 = (f32[2048]{0:T(1024)S(1)}, f32[2048,512]{1,0:T(8,128)S(1)}) fusion(f32[2048,128]{1,0:T(8,128)} %param.4, f32[512,128]{1,0:T(8,128)} %param.5, f32[512]{0:T(512)S(1)} %multiply_reduce_fusion.4, f32[2048]{0:T(1024)S(1)} %multiply_reduce_fusion), kind=kOutput, calls=%fused_computation.134 | convolution fusion | flops 812644352 | bytes 5523456 | tf_op jit(solution)/shard_map/dot_general | solution.py:96
  13.5 1.7 %exponential_reduce_fusion.15 = f32[2048]{0:T(1024)S(1)} fusion(f32[2048,512]{1,0:T(8,128)S(1)} %get-tuple-element.68.refs_1_, f32[2048]{0:T(1024)S(1)} %get-tuple-element.67), kind=kLoop, calls=%fused_computation.22 | loop fusion | flops 2095104 | bytes 4210688 | tf_op jit(solution)/shard_map/reduce_sum | solution.py:179
  15.4 2.6 %fusion.25 = (f32[2048]{0:T(1024)S(1)}, f32[2048,512]{1,0:T(8,128)S(1)}) fusion(f32[2048,128]{1,0:T(8,128)S(1)} %copy-done.8, f32[512,128]{1,0:T(8,128)S(1)} %collective-permute-done.2, f32[512]{0:T(512)S(1)} %multiply_reduce_fusion.1, f32[2048]{0:T(1024)S(1)} %multiply_reduce_fusion), kind=kOutput, calls=%fused_computation.136 | convolution fusion | flops 812644352 | bytes 5523456 | tf_op jit(solution)/shard_map/dot_general | solution.py:96
  17.9 1.7 %exponential_reduce_fusion.12 = f32[2048]{0:T(1024)S(1)} fusion(f32[2048,512]{1,0:T(8,128)S(1)} %get-tuple-element.72.refs_4_, f32[2048]{0:T(1024)S(1)} %get-tuple-element.71), kind=kLoop, calls=%fused_computation.16 | loop fusion | flops 2095104 | bytes 4210688 | tf_op jit(solution)/shard_map/reduce_sum | solution.py:179
  19.6 8.6 %collective-permute-done.1 = f32[512,128]{1,0:T(8,128)S(1)} collective-permute-done((f32[512,128]{1,0:T(8,128)}, f32[512,128]{1,0:T(8,128)S(1)}, u32[]{:S(2)}, u32[]{:S(2)}) %collective-permute-start.1) | collective-permute-done | bytes 262176 | tf_op jit(solution)/shard_map/ppermute | solution.py:165
  28.4 2.6 %fusion.24 = (f32[2048]{0:T(1024)S(1)}, f32[2048,512]{1,0:T(8,128)S(1)}) fusion(f32[2048,128]{1,0:T(8,128)S(1)} %copy-done.8, f32[512,128]{1,0:T(8,128)S(1)} %collective-permute-done.1, f32[512]{0:T(512)S(1)} %multiply_reduce_fusion.2, f32[2048]{0:T(1024)S(1)} %multiply_reduce_fusion), kind=kOutput, calls=%fused_computation.135 | convolution fusion | flops 812644352 | bytes 5523456 | tf_op jit(solution)/shard_map/dot_general | solution.py:96
  31.0 1.9 %exponential_reduce_fusion.13 = f32[2048]{0:T(1024)S(1)} fusion(f32[2048,512]{1,0:T(8,128)S(1)} %get-tuple-element.70.refs_3_, f32[2048]{0:T(1024)S(1)} %get-tuple-element.69), kind=kLoop, calls=%fused_computation.18 | loop fusion | flops 2095104 | bytes 4210688 | tf_op jit(solution)/shard_map/reduce_sum | solution.py:179
  33.0 2.6 %fusion.22 = (f32[2048]{0:T(1024)S(1)}, f32[2048,512]{1,0:T(8,128)S(1)}) fusion(f32[2048,128]{1,0:T(8,128)S(1)} %copy-done.8, f32[512,128]{1,0:T(8,128)S(1)} %collective-permute-done, f32[512]{0:T(512)S(1)} %multiply_reduce_fusion.3, f32[2048]{0:T(1024)S(1)} %multiply_reduce_fusion), kind=kOutput, calls=%fused_computation.133 | convolution fusion | flops 812644352 | bytes 5523456 | tf_op jit(solution)/shard_map/dot_general | solution.py:96
  35.6 1.7 %exponential_reduce_fusion.14 = f32[2048]{0:T(1024)S(1)} fusion(f32[2048,512]{1,0:T(8,128)S(1)} %get-tuple-element.66.refs_2_, f32[2048]{0:T(1024)S(1)} %get-tuple-element.65), kind=kLoop, calls=%fused_computation.20 | loop fusion | flops 2095104 | bytes 4210688 | tf_op jit(solution)/shard_map/reduce_sum | solution.py:179
  37.5 1.6 %collective-permute-start.4 = (f32[2048]{0:T(1024)S(1)}, f32[2048]{0:T(1024)S(1)}, u32[]{:S(2)}, u32[]{:S(2)}) collective-permute-start(f32[2048]{0:T(1024)S(1)} %get-tuple-element.62), channel_id=1, source_target_pairs={{0,2},{1,3},{2,0},{3,1},{4,6},{5,7},{6,4},{7,5},{8,10},{9,11},{10,... | collective-permute-start | bytes 24584 | tf_op jit(solution)/shard_map/ppermute | solution.py:109
  42.3 1.7 %exponential_reduce_fusion.11 = (f32[512]{0:T(512)S(1)}, f32[512]{0:T(512)S(1)}, f32[512]{0:T(512)S(1)}, f32[512]{0:T(512)S(1)}) fusion(f32[2048,512]{1,0:T(8,128)S(1)} %get-tuple-element.68.refs_1_, f32[512]{0:T(512)S(1)} %add_reduce_fusion.11, f32[2048]{0:T(1024)S(1)} %add_multiply_fusion.5, f32[2048,512]{1,0:T(8,128)S(1)} %get-tuple-element.66.refs_2_, ...), kind=kLoop, calls=%fused_computation.15 | loop fusion | flops 9435136 | bytes 16795648 | tf_op jit(solution)/shard_map/reduce_sum | solution.py:191
  44.0 2.3 %exponential_reduce_fusion.10 = (f32[512]{0:T(512)S(1)}, f32[512]{0:T(512)S(1)}, f32[512]{0:T(512)S(1)}) fusion(f32[2048,512]{1,0:T(8,128)S(1)} %get-tuple-element.66.refs_2_, f32[512]{0:T(512)S(1)} %get-tuple-element.24, f32[2048]{0:T(1024)S(1)} %add_multiply_fusion.5, f32[512]{0:T(512)S(1)} %get-tuple-element.26, ...), kind=kLoop, calls=%fused_computation.14 | loop fusion | flops 9435648 | bytes 12603392 | tf_op jit(solution)/shard_map/reduce_sum | solution.py:191
  47.5 3.3 %collective-permute-start.8 = (f32[2048]{0:T(1024)S(1)}, f32[2048]{0:T(1024)S(1)}, u32[]{:S(2)}, u32[]{:S(2)}) collective-permute-start(f32[2048]{0:T(1024)S(1)} %bitcast.111), channel_id=1, source_target_pairs={{0,12},{4,0},{8,4},{12,8},{1,13},{5,1},{9,5},{13,9},{2,14},{6,2},{... | collective-permute-start | bytes 24584 | tf_op jit(solution)/shard_map/ppermute | solution.py:109
  50.8 1.6 %collective-permute-done.6 = f32[2048]{0:T(1024)S(1)} collective-permute-done((f32[2048]{0:T(1024)S(1)}, f32[2048]{0:T(1024)S(1)}, u32[]{:S(2)}, u32[]{:S(2)}) %collective-permute-start.6) | collective-permute-done | bytes 8224 | tf_op jit(solution)/shard_map/ppermute | solution.py:109
  53.8 2.7 %add_reduce_fusion.4 = f32[2048]{0:T(1024)S(1)} fusion(f32[2048,512]{1,0:T(8,128)} %copy-done, f32[512]{0:T(512)S(1)} %bitcast.140), kind=kLoop, calls=%fused_computation.28 | loop fusion | flops 2095104 | bytes 4204544 | tf_op jit(solution)/shard_map/reduce_max | solution.py:178
  66.2 2.2 %collective-permute-done.10 = f32[2048]{0:T(1024)S(1)} collective-permute-done((f32[2048]{0:T(1024)S(1)}, f32[2048]{0:T(1024)S(1)}, u32[]{:S(2)}, u32[]{:S(2)}) %collective-permute-start.10) | collective-permute-done | bytes 8224 | tf_op jit(solution)/shard_map/ppermute | solution.py:109
  69.2 1.7 %exponential_reduce_fusion.3 = (f32[512]{0:T(512)S(1)}, f32[512]{0:T(512)S(1)}, f32[512]{0:T(512)S(1)}, f32[512]{0:T(512)S(1)}) fusion(f32[2048,512]{1,0:T(8,128)S(1)} %copy-done.7, f32[512]{0:T(512)S(1)} %add_reduce_fusion.3, f32[2048]{0:T(1024)S(1)} %add_multiply_fusion.3, f32[2048,512]{1,0:T(8,128)S(1)} %copy-done.5, f32[2048,512]{1,0:T(8,128)S(1)} %copy-done.3, ...), kind=kLoop, calls=%fused_computation.7 | loop fusion | flops 9435136 | bytes 16795648 | tf_op jit(solution)/shard_map/reduce_sum | solution.py:191
  70.9 2.2 %exponential_reduce_fusion.2 = (f32[512]{0:T(512)S(1)}, f32[512]{0:T(512)S(1)}, f32[512]{0:T(512)S(1)}) fusion(f32[2048,512]{1,0:T(8,128)S(1)} %copy-done.5, f32[512]{0:T(512)S(1)} %get-tuple-element.17, f32[2048]{0:T(1024)S(1)} %add_multiply_fusion.3, f32[512]{0:T(512)S(1)} %get-tuple-element.19, f32[2048,512]{1,0:T(8,128)S(1)} %copy-done.1, ...), kind=kLoop, calls=%fused_computation.6 | loop fusion | flops 9435648 | bytes 12603392 | tf_op jit(solution)/shard_map/reduce_sum | solution.py:191
  73.9 1.9 %collective-permute-start.12 = (f32[2048]{0:T(1024)S(1)}, f32[2048]{0:T(1024)S(1)}, u32[]{:S(2)}, u32[]{:S(2)}) collective-permute-start(f32[2048]{0:T(1024)S(1)} %bitcast.113), channel_id=1, source_target_pairs={{0,4},{4,8},{8,12},{12,0},{1,5},{5,9},{9,13},{13,1},{2,6},{6,10},{... | collective-permute-start | bytes 24584 | tf_op jit(solution)/shard_map/ppermute | solution.py:109
  75.8 1.9 %collective-permute-start.13 = (f32[2048]{0:T(1024)S(1)}, f32[2048]{0:T(1024)S(1)}, u32[]{:S(2)}, u32[]{:S(2)}) collective-permute-start(f32[2048]{0:T(1024)S(1)} %bitcast.114), channel_id=1, source_target_pairs={{0,8},{4,12},{8,0},{12,4},{1,9},{5,13},{9,1},{13,5},{2,10},{6,14},... | collective-permute-start | bytes 24584 | tf_op jit(solution)/shard_map/ppermute | solution.py:109
  83.4 16.3 %shard_map.49 = (f32[1,2048]{1,0:T(1,128)}, f32[1,2048]{1,0:T(1,128)}, f32[2048,128]{1,0:T(8,128)}) custom-call(f32[1,2048]{1,0:T(1,128)} %bitcast.108, f32[2048,512]{1,0:T(8,128)} %copy-done.6, f32[2048,512]{1,0:T(8,128)} %copy-done.4, f32[2048,512]{1,0:T(8,128)} %copy-done.2, f32[2048,512]{1,0:T(8,128)} %copy-done, f32[2048,128]{1,0:T(8,128)} %pad_maximum_fusion.refs_5_), custom_call_target="tpu_custom_call" | custom-call | tf_op jit(solution)/shard_map/pallas_call | solution.py:71
  112.9 4.2 %collective-permute-done.20 = f32[512,128]{1,0:T(8,128)S(1)} collective-permute-done((f32[512,128]{1,0:T(8,128)S(1)}, f32[512,128]{1,0:T(8,128)S(1)}, u32[]{:S(2)}, u32[]{:S(2)}) %collective-permute-start.20) | collective-permute-done | bytes 262176 | tf_op jit(solution)/shard_map/ppermute | solution.py:146
  (141 shorter events, 39.3 us)
Async XLA Ops:
  0.6 14.6 %collective-permute-start.2 = (f32[512,128]{1,0:T(8,128)}, f32[512,128]{1,0:T(8,128)S(1)}, u32[]{:S(2)}, u32[]{:S(2)}) collective-permute-start(f32[512,128]{1,0:T(8,128)} %param.5), channel_id=1, source_target_pairs={{0,12},{4,0},{8,4},{12,8},{1,13},{5,1},{9,5},{13,9},{2,14},{6,2},{... | collective-permute-start | bytes 786440 | tf_op jit(solution)/shard_map/ppermute | solution.py:165
  5.8 22.5 %collective-permute-start.1 = (f32[512,128]{1,0:T(8,128)}, f32[512,128]{1,0:T(8,128)S(1)}, u32[]{:S(2)}, u32[]{:S(2)}) collective-permute-start(f32[512,128]{1,0:T(8,128)} %param.5), channel_id=1, source_target_pairs={{0,8},{4,12},{8,0},{12,4},{1,9},{5,13},{9,1},{13,5},{2,10},{6,14},... | collective-permute-start | bytes 786440 | tf_op jit(solution)/shard_map/ppermute | solution.py:165
  5.8 27.1 %collective-permute-start = (f32[512,128]{1,0:T(8,128)}, f32[512,128]{1,0:T(8,128)S(1)}, u32[]{:S(2)}, u32[]{:S(2)}) collective-permute-start(f32[512,128]{1,0:T(8,128)} %param.5), channel_id=1, source_target_pairs={{0,4},{4,8},{8,12},{12,0},{1,5},{5,9},{9,13},{13,1},{2,6},{6,10},{... | collective-permute-start | bytes 786440 | tf_op jit(solution)/shard_map/ppermute | solution.py:165
  13.5 28.8 %copy-start.6 = (f32[2048,512]{1,0:T(8,128)}, f32[2048,512]{1,0:T(8,128)S(1)}, u32[]{:S(2)}) copy-start(f32[2048,512]{1,0:T(8,128)S(1)} %get-tuple-element.68.refs_1_) | copy-start | bytes 12582916
  17.9 26.0 %copy-start = (f32[2048,512]{1,0:T(8,128)}, f32[2048,512]{1,0:T(8,128)S(1)}, u32[]{:S(2)}) copy-start(f32[2048,512]{1,0:T(8,128)S(1)} %get-tuple-element.72.refs_4_) | copy-start | bytes 12582916
  37.4 3.1 %collective-permute-start.3 = (f32[2048]{0:T(1024)S(1)}, f32[2048]{0:T(1024)S(1)}, u32[]{:S(2)}, u32[]{:S(2)}) collective-permute-start(f32[2048]{0:T(1024)S(1)} %get-tuple-element.62), channel_id=1, source_target_pairs={{0,1},{1,2},{2,3},{3,0},{4,5},{5,6},{6,7},{7,4},{8,9},{9,10},{10,1... | collective-permute-start | bytes 24584 | tf_op jit(solution)/shard_map/ppermute | solution.py:109
  37.5 3.7 %collective-permute-start.4 = (f32[2048]{0:T(1024)S(1)}, f32[2048]{0:T(1024)S(1)}, u32[]{:S(2)}, u32[]{:S(2)}) collective-permute-start(f32[2048]{0:T(1024)S(1)} %get-tuple-element.62), channel_id=1, source_target_pairs={{0,2},{1,3},{2,0},{3,1},{4,6},{5,7},{6,4},{7,5},{8,10},{9,11},{10,... | collective-permute-start | bytes 24584 | tf_op jit(solution)/shard_map/ppermute | solution.py:109
  39.1 2.8 %collective-permute-start.5 = (f32[2048]{0:T(1024)S(1)}, f32[2048]{0:T(1024)S(1)}, u32[]{:S(2)}, u32[]{:S(2)}) collective-permute-start(f32[2048]{0:T(1024)S(1)} %get-tuple-element.62), channel_id=1, source_target_pairs={{0,3},{1,0},{2,1},{3,2},{4,7},{5,4},{6,5},{7,6},{8,11},{9,8},{10,9... | collective-permute-start | bytes 24584 | tf_op jit(solution)/shard_map/ppermute | solution.py:109
  47.0 5.5 %collective-permute-start.6 = (f32[2048]{0:T(1024)S(1)}, f32[2048]{0:T(1024)S(1)}, u32[]{:S(2)}, u32[]{:S(2)}) collective-permute-start(f32[2048]{0:T(1024)S(1)} %bitcast.109), channel_id=1, source_target_pairs={{0,4},{4,8},{8,12},{12,0},{1,5},{5,9},{9,13},{13,1},{2,6},{6,10},{... | collective-permute-start | bytes 24584 | tf_op jit(solution)/shard_map/ppermute | solution.py:109
  47.5 4.9 %collective-permute-start.7 = (f32[2048]{0:T(1024)S(1)}, f32[2048]{0:T(1024)S(1)}, u32[]{:S(2)}, u32[]{:S(2)}) collective-permute-start(f32[2048]{0:T(1024)S(1)} %bitcast.110), channel_id=1, source_target_pairs={{0,8},{4,12},{8,0},{12,4},{1,9},{5,13},{9,1},{13,5},{2,10},{6,14},... | collective-permute-start | bytes 24584 | tf_op jit(solution)/shard_map/ppermute | solution.py:109
  47.5 5.5 %collective-permute-start.8 = (f32[2048]{0:T(1024)S(1)}, f32[2048]{0:T(1024)S(1)}, u32[]{:S(2)}, u32[]{:S(2)}) collective-permute-start(f32[2048]{0:T(1024)S(1)} %bitcast.111), channel_id=1, source_target_pairs={{0,12},{4,0},{8,4},{12,8},{1,13},{5,1},{9,5},{13,9},{2,14},{6,2},{... | collective-permute-start | bytes 24584 | tf_op jit(solution)/shard_map/ppermute | solution.py:109
  64.6 3.7 %collective-permute-start.10 = (f32[2048]{0:T(1024)S(1)}, f32[2048]{0:T(1024)S(1)}, u32[]{:S(2)}, u32[]{:S(2)}) collective-permute-start(f32[2048]{0:T(1024)S(1)} %get-tuple-element.56), channel_id=1, source_target_pairs={{0,2},{1,3},{2,0},{3,1},{4,6},{5,7},{6,4},{7,5},{8,10},{9,11},{10,... | collective-permute-start | bytes 24584 | tf_op jit(solution)/shard_map/ppermute | solution.py:109
  65.6 2.7 %collective-permute-start.11 = (f32[2048]{0:T(1024)S(1)}, f32[2048]{0:T(1024)S(1)}, u32[]{:S(2)}, u32[]{:S(2)}) collective-permute-start(f32[2048]{0:T(1024)S(1)} %get-tuple-element.56), channel_id=1, source_target_pairs={{0,3},{1,0},{2,1},{3,2},{4,7},{5,4},{6,5},{7,6},{8,11},{9,8},{10,9... | collective-permute-start | bytes 24584 | tf_op jit(solution)/shard_map/ppermute | solution.py:109
  65.6 3.1 %collective-permute-start.9 = (f32[2048]{0:T(1024)S(1)}, f32[2048]{0:T(1024)S(1)}, u32[]{:S(2)}, u32[]{:S(2)}) collective-permute-start(f32[2048]{0:T(1024)S(1)} %get-tuple-element.56), channel_id=1, source_target_pairs={{0,1},{1,2},{2,3},{3,0},{4,5},{5,6},{6,7},{7,4},{8,9},{9,10},{10,1... | collective-permute-start | bytes 24584 | tf_op jit(solution)/shard_map/ppermute | solution.py:109
  73.9 5.5 %collective-permute-start.12 = (f32[2048]{0:T(1024)S(1)}, f32[2048]{0:T(1024)S(1)}, u32[]{:S(2)}, u32[]{:S(2)}) collective-permute-start(f32[2048]{0:T(1024)S(1)} %bitcast.113), channel_id=1, source_target_pairs={{0,4},{4,8},{8,12},{12,0},{1,5},{5,9},{9,13},{13,1},{2,6},{6,10},{... | collective-permute-start | bytes 24584 | tf_op jit(solution)/shard_map/ppermute | solution.py:109
  75.8 4.5 %collective-permute-start.13 = (f32[2048]{0:T(1024)S(1)}, f32[2048]{0:T(1024)S(1)}, u32[]{:S(2)}, u32[]{:S(2)}) collective-permute-start(f32[2048]{0:T(1024)S(1)} %bitcast.114), channel_id=1, source_target_pairs={{0,8},{4,12},{8,0},{12,4},{1,9},{5,13},{9,1},{13,5},{2,10},{6,14},... | collective-permute-start | bytes 24584 | tf_op jit(solution)/shard_map/ppermute | solution.py:109
  77.7 3.7 %collective-permute-start.14 = (f32[2048]{0:T(1024)S(1)}, f32[2048]{0:T(1024)S(1)}, u32[]{:S(2)}, u32[]{:S(2)}) collective-permute-start(f32[2048]{0:T(1024)S(1)} %bitcast.115), channel_id=1, source_target_pairs={{0,12},{4,0},{8,4},{12,8},{1,13},{5,1},{9,5},{13,9},{2,14},{6,2},{... | collective-permute-start | bytes 24584 | tf_op jit(solution)/shard_map/ppermute | solution.py:109
  100.8 3.4 %collective-permute-start.16 = (f32[2,512,128]{2,1,0:T(8,128)S(1)}, f32[2,512,128]{2,1,0:T(8,128)S(1)}, u32[]{:S(2)}, u32[]{:S(2)}) collective-permute-start(f32[2,512,128]{2,1,0:T(8,128)S(1)} %dynamic-slice_bitcast_fusion), channel_id=1, source_target_pairs={{0,1},{1,0},{2,3},{3,2},{4,5},{5,4},{6,7},{7,6},{8,9},{9,8},{10,11... | collective-permute-start | bytes 1572872 | tf_op jit(solution)/shard_map/ppermute | solution.py:134
  102.8 1.4 %collective-permute-start.15 = (f32[2,512]{1,0:T(2,128)S(1)}, f32[2,512]{1,0:T(2,128)S(1)}, u32[]{:S(2)}, u32[]{:S(2)}) collective-permute-start(f32[2,512]{1,0:T(2,128)S(1)} %bitcast.143), channel_id=1, source_target_pairs={{0,1},{1,0},{2,3},{3,2},{4,5},{5,4},{6,7},{7,6},{8,9},{9,8},{10,11... | collective-permute-start | bytes 12296 | tf_op jit(solution)/shard_map/ppermute | solution.py:135
  105.6 5.1 %collective-permute-start.17 = (f32[2048]{0:T(1024)}, f32[2048]{0:T(1024)S(1)}, u32[]{:S(2)}, u32[]{:S(2)}) collective-permute-start(f32[2048]{0:T(1024)} %bitcast.117), channel_id=1, source_target_pairs={{0,1},{1,2},{2,3},{3,0},{4,5},{5,6},{6,7},{7,4},{8,9},{9,10},{10,1... | collective-permute-start | bytes 24584 | tf_op jit(solution)/shard_map/ppermute | solution.py:109
  106.0 4.7 %collective-permute-start.18 = (f32[2048]{0:T(1024)}, f32[2048]{0:T(1024)S(1)}, u32[]{:S(2)}, u32[]{:S(2)}) collective-permute-start(f32[2048]{0:T(1024)} %bitcast.118), channel_id=1, source_target_pairs={{0,2},{1,3},{2,0},{3,1},{4,6},{5,7},{6,4},{7,5},{8,10},{9,11},{10,... | collective-permute-start | bytes 24584 | tf_op jit(solution)/shard_map/ppermute | solution.py:109
  107.4 3.3 %collective-permute-start.19 = (f32[2048]{0:T(1024)}, f32[2048]{0:T(1024)S(1)}, u32[]{:S(2)}, u32[]{:S(2)}) collective-permute-start(f32[2048]{0:T(1024)} %bitcast.119), channel_id=1, source_target_pairs={{0,3},{1,0},{2,1},{3,2},{4,7},{5,4},{6,5},{7,6},{8,11},{9,8},{10,9... | collective-permute-start | bytes 24584 | tf_op jit(solution)/shard_map/ppermute | solution.py:109
  108.5 4.3 %collective-permute-start.21 = (f32[512]{0:T(512)S(1)}, f32[512]{0:T(512)S(1)}, u32[]{:S(2)}, u32[]{:S(2)}) collective-permute-start(f32[512]{0:T(512)S(1)} %bitcast.144), channel_id=1, source_target_pairs={{0,2},{1,3},{2,0},{3,1},{4,6},{5,7},{6,4},{7,5},{8,10},{9,11},{10,... | collective-permute-start | bytes 6152 | tf_op jit(solution)/shard_map/ppermute | solution.py:147
  109.3 7.8 %collective-permute-start.20 = (f32[512,128]{1,0:T(8,128)S(1)}, f32[512,128]{1,0:T(8,128)S(1)}, u32[]{:S(2)}, u32[]{:S(2)}) collective-permute-start(f32[512,128]{1,0:T(8,128)S(1)} %dynamic-slice_bitcast_fusion.1), channel_id=1, source_target_pairs={{0,2},{1,3},{2,0},{3,1},{4,6},{5,7},{6,4},{7,5},{8,10},{9,11},{10,... | collective-permute-start | bytes 786440 | tf_op jit(solution)/shard_map/ppermute | solution.py:146
  (8 other events, 47.0 us)
